TPU v7x, 128 devices: a whole 4x4x4 slice. The times are simulated.
128 devices in a mesh: mass: 4 (over x), tile: 32 (over z, y, core).
Axes of the slice: x: 4, y: 4, z: 4, core: 2. Of those that a mesh axis runs over, the one named last changes fastest.
Arguments:
- spectra: bfloat16 [12288, 4096], P(('mass', 'tile')), may hold values from -6 to 6
- window: int32 [12288, 1], P(('mass', 'tile')), may hold values from 0 to 3; in each aligned block of 96 rows (0 to 95, 96 to 191, ...) at most 48 rows name the same one
- cluster: int32 [12288], P(('mass', 'tile')), may hold values from 0 to 127
Outputs:
- gram_tiles: float32 [24576, 6144], P(('mass', 'tile'))
- consensus: float32 [512, 4096], P(('mass', 'tile'))
Inputs may be any that keep to these rules, and one draw needn't show every extreme that they name: Among the 96 spectra of one run shard, at most 48 name one window, and in every draw some window is named by exactly 48 of some shard.
All inputs are finite; a program needn't handle non-finite values.
Results may differ from a plain program's by a relative error of at most 0.0029.
Values may be sent and summed in bfloat16 or wider, within the bound.
No kernel may reach another device: no remote copies, remote signals or barrier semaphores. Data moves between devices by JAX's collectives and lax.ppermute only.
A program may use at most 192 MiB of HBM per device.

v0:
```python
import jax
import jax.numpy as jnp
from jax import lax
from jax.sharding import PartitionSpec as P

CL_DEV = 4


def shards(spectra, window, cluster):
    s_dev, num_bins = spectra.shape
    mass_count = lax.axis_size("mass")
    tile_count = lax.axis_size("tile")
    per_window = CL_DEV * tile_count
    capacity = 2 * s_dev // mass_count
    slot_count = mass_count * capacity
    values = spectra.astype(jnp.float32)
    scaled = (values * lax.rsqrt(jnp.mean(values * values, axis=1, keepdims=True) + 1e-06)).astype(
        jnp.bfloat16
    )
    target = window[:, 0]
    global_ids = target * per_window + cluster
    member = (target[:, None] == jnp.arange(mass_count, dtype=jnp.int32)[None, :]).astype(jnp.int32)
    before = jnp.cumsum(member, axis=0) - member
    slot_rank = jnp.sum(before * member, axis=1)
    position = target * capacity + slot_rank
    chosen = jnp.arange(slot_count, dtype=jnp.int32)[:, None] == position[None, :]
    outgoing = jnp.dot(
        chosen.astype(jnp.bfloat16), scaled, preferred_element_type=jnp.float32
    ).astype(jnp.bfloat16)
    outgoing = outgoing.reshape(mass_count, capacity, num_bins)
    labels = jnp.max(jnp.where(chosen, global_ids[None, :], -1), axis=1).reshape(
        mass_count, capacity
    )
    arrived, arrived_labels = (
        lax.all_to_all(outgoing, "mass", split_axis=0, concat_axis=0, tiled=True),
        lax.all_to_all(labels, "mass", split_axis=0, concat_axis=0, tiled=True),
    )
    arrived = arrived.reshape(slot_count, num_bins)
    arrived_labels = arrived_labels.reshape(slot_count)
    product = lax.dot_general(
        arrived,
        lax.all_gather(arrived, "tile", axis=0, tiled=True),
        (((1,), (1,)), ((), ())),
        preferred_element_type=jnp.float32,
    )
    gram_tiles = product * (1.0 / num_bins)
    local_labels = arrived_labels - lax.axis_index("mass") * per_window
    cluster_ids = jnp.arange(lax.axis_size("tile") * CL_DEV, dtype=jnp.int32)
    one_hot = (cluster_ids[:, None] == local_labels[None, :]).astype(jnp.bfloat16)
    consensus = lax.psum_scatter(
        jnp.dot(one_hot, arrived, preferred_element_type=jnp.float32),
        "tile",
        scatter_dimension=0,
        tiled=True,
    )
    return (gram_tiles, consensus)


def solution(mesh):
    in_specs = (P(("mass", "tile"), None), P(("mass", "tile"), None), P(("mass", "tile")))
    out_specs = (P(("mass", "tile"), None), P(("mass", "tile"), None))
    return jax.shard_map(shards, mesh=mesh, in_specs=in_specs, out_specs=out_specs, check_vma=False)
```

profile of v0, /device:TPU:1, one launch (start us, length us, event | category | flops | bytes accessed | tf_op | source)
XLA Modules:
  0.0 346.4 jit_solution(1250881975775462067)
XLA Ops:
  7.2 0.7 fusion.7
  7.9 0.1 reduce_window_sum.11
  8.0 0.8 select_reduce_fusion.1
  8.9 0.7 multiply_add_fusion
  9.6 0.1 select_reduce_fusion
  9.7 0.7 all_to_all.10
  10.4 4.8 %all-to-all-start.1 = ((s32[4,1,48]{2,1,0:T(1,128)}), s32[4,1,48]{2,1,0:T(1,128)S(1)}, u32[]{:S(2)}, u32[]{:S(2)}) async-start(s32[4,1,48]{2,1,0:T(1,128)} %all_to_all.10), calls=%async_computation.1 | async-start | bytes 4096 | tf_op jit(solution)/shard_map/all_to_all | solution.py:36
  15.2 1.4 fusion
  16.6 2.9 convolution_convert_fusion
  19.5 0.0 all-to-all-done.1
  19.5 4.2 %all-to-all-start = ((bf16[4,48,4096]{2,1,0:T(8,128)(2,1)}), bf16[4,48,4096]{2,1,0:T(8,128)(2,1)S(1)}, u32[]{:S(2)}, u32[]{:S(2)}) async-start(bf16[4,48,4096]{2,1,0:T(8,128)(2,1)} %bitcast.1), calls=%async_computation | async-start | bytes 3145728 | tf_op jit(solution)/shard_map/all_to_all | solution.py:35
  23.8 0.0 all-reduce.3.cloned.1.call-start
  23.8 0.1 sub.19
  23.9 19.2 %all-to-all-done = bf16[4,48,4096]{2,1,0:T(8,128)(2,1)S(1)} async-done(((bf16[4,48,4096]{2,1,0:T(8,128)(2,1)}), bf16[4,48,4096]{2,1,0:T(8,128)(2,1)S(1)}, u32[]{:S(2)}, u32[]{:S(2)}) %all-to-all-start) | async-done | bytes 1572896 | tf_op jit(solution)/shard_map/all_to_all | solution.py:35
  43.0 0.0 copy-start
  43.1 1.8 fusion.4
  44.9 0.0 copy-done
  44.9 0.0 copy-start.2
  44.9 0.0 copy-start.1
  44.9 0.0 all-reduce.3.cloned.1.call-update
  44.9 0.0 all-gather.2.cloned.1.call-start
  45.0 0.7 all-gather.2.cloned.1.call-update
  45.7 0.0 copy-done.2
  45.7 0.6 dynamic-slice
  46.9 108.2 %all-reduce.3.cloned.1.call-done = f32[128,4096]{1,0:T(8,128)} async-done(((f32[128,4096]{1,0:T(8,128)}), f32[128,4096]{1,0:T(8,128)}) %all-reduce.3.cloned.1.call-update) | async-done | bytes 2097168
  155.1 1.5 constant_dynamic-slice_fusion
  156.7 158.2 %all-gather.2.cloned.1.call-done = bf16[6144,4096]{1,0:T(8,128)(2,1)} async-done(((bf16[192,4096]{1,0:T(8,128)(2,1)}), bf16[6144,4096]{1,0:T(8,128)(2,1)}) %all-gather.2.cloned.1.call-update) | async-done | bytes 50331664 | tf_op jit(solution)/shard_map/all_gather | solution.py:42
  314.9 0.0 copy-done.1
  314.9 24.6 %convolution_multiply_fusion = f32[192,6144]{1,0:T(8,128)} fusion(bf16[192,4096]{1,0:T(8,128)(2,1)S(1)} %bitcast.11, bf16[6144,4096]{1,0:T(8,128)(2,1)} %all-gather.2.cloned.1.call-done), kind=kOutput, calls=%fused_computation | convolution fusion | flops 9664856064 | bytes 56623104 | tf_op jit(solution)/shard_map/dot_general | solution.py:40
  (2 shorter events, 0.0 us)
Async XLA Ops:
  10.4 9.2 %all-to-all-start.1 = ((s32[4,1,48]{2,1,0:T(1,128)}), s32[4,1,48]{2,1,0:T(1,128)S(1)}, u32[]{:S(2)}, u32[]{:S(2)}) async-start(s32[4,1,48]{2,1,0:T(1,128)} %all_to_all.10), calls=%async_computation.1 | async-start | bytes 4096 | tf_op jit(solution)/shard_map/all_to_all | solution.py:36
  19.5 23.5 %all-to-all-start = ((bf16[4,48,4096]{2,1,0:T(8,128)(2,1)}), bf16[4,48,4096]{2,1,0:T(8,128)(2,1)S(1)}, u32[]{:S(2)}, u32[]{:S(2)}) async-start(bf16[4,48,4096]{2,1,0:T(8,128)(2,1)} %bitcast.1), calls=%async_computation | async-start | bytes 3145728 | tf_op jit(solution)/shard_map/all_to_all | solution.py:35
  23.8 131.4 %all-reduce.3.cloned.1.call-start = ((), (), s32[]{:S(2)}) async-start(), calls=%async_computation.3 | async-start | bytes 4194304
  43.0 1.8 copy-start
  44.9 0.8 copy-start.2
  44.9 270.0 %copy-start.1 = (bf16[4,48,4096]{2,1,0:T(8,128)(2,1)S(1)}, bf16[4,48,4096]{2,1,0:T(8,128)(2,1)}, u32[]{:S(2)}) copy-start(bf16[4,48,4096]{2,1,0:T(8,128)(2,1)} %copy-done) | copy-start | bytes 4718596
  44.9 270.0 %all-gather.2.cloned.1.call-start = ((), (), s32[]{:S(2)}) async-start(), calls=%async_computation.2 | async-start | bytes 51904512 | tf_op jit(solution)/shard_map/all_gather | solution.py:42
Sparse Core Ops, SparseCore 0:
  45.0 110.0 all-reduce.2
  157.4 157.4 all-gather.1
where the time goes:
time: 347 us; the launch traced here: 346 us
  waiting for transfers between devices  286 us (82%)
  matrix products  29.4 us (8%)
  between operations  14.7 us (4%)
  starting transfers between devices  9.11 us (3%)
  other arithmetic  3.92 us (1%)
    all_gather x1, waiting for transfers between devices, shards(): lax.all_gather(arrived, 'tile', axis=0, tiled=True)  158 us
    unnamed x3, waiting for transfers between devices  109 us
    dot_general x1, matrix products, shards(): lax.dot_general(arrived, lax.all_gather(arrived, 'tile', axis=0, tiled=Tr...  24.6 us
    all_to_all x1, waiting for transfers between devices, shards(): lax.all_to_all(outgoing, 'mass', split_axis=0, concat_axis=0, tiled=True)  19.2 us
  transfers between devices with their start and end apart: 4, of which 3 were waited for; matrix products, arithmetic and copies ran while one was open for 2% of the time, Pallas kernels for 0%

commit v1 on v0

--- a/solution.py
+++ b/solution.py
@@ -37,22 +37,22 @@
     )
     arrived = arrived.reshape(slot_count, num_bins)
     arrived_labels = arrived_labels.reshape(slot_count)
+    gathered = lax.all_gather(arrived, "tile", axis=0, tiled=True)
+    gathered_labels = lax.all_gather(arrived_labels, "tile", axis=0, tiled=True)
     product = lax.dot_general(
         arrived,
-        lax.all_gather(arrived, "tile", axis=0, tiled=True),
+        gathered,
         (((1,), (1,)), ((), ())),
         preferred_element_type=jnp.float32,
     )
     gram_tiles = product * (1.0 / num_bins)
-    local_labels = arrived_labels - lax.axis_index("mass") * per_window
-    cluster_ids = jnp.arange(lax.axis_size("tile") * CL_DEV, dtype=jnp.int32)
-    one_hot = (cluster_ids[:, None] == local_labels[None, :]).astype(jnp.bfloat16)
-    consensus = lax.psum_scatter(
-        jnp.dot(one_hot, arrived, preferred_element_type=jnp.float32),
-        "tile",
-        scatter_dimension=0,
-        tiled=True,
+    own_ids = (
+        lax.axis_index("mass") * per_window
+        + lax.axis_index("tile") * CL_DEV
+        + jnp.arange(CL_DEV, dtype=jnp.int32)
     )
+    one_hot = (own_ids[:, None] == gathered_labels[None, :]).astype(jnp.bfloat16)
+    consensus = jnp.dot(one_hot, gathered, preferred_element_type=jnp.float32)
     return (gram_tiles, consensus)
 
 

time: 347 us -> 249 us (0.72)
  waiting for transfers between devices: 286 us -> 23.6 us
  blocking collectives: 0 us -> 155 us
  matrix products: 29.4 us -> 45.3 us
  starting transfers between devices: 9.11 us -> 3.26 us
    all_gather x1, waiting for transfers between devices: 158 us -> 20.9 us  [shards(): gathered = lax.all_gather(arrived, 'tile', axis=0, tiled=True)]
    unnamed x0 -> x1, blocking collectives: none -> 130 us
    unnamed x3 -> x1, waiting for transfers between devices: 109 us -> 0.02 us
    all_to_all x0 -> x1, blocking collectives: none -> 24.6 us  [shards(): lax.all_to_all(outgoing, 'mass', split_axis=0, concat_axis=0, tiled=True)]
    all_to_all x1 -> x0, waiting for transfers between devices: 19.2 us -> none  [shards(): lax.all_to_all(outgoing, 'mass', split_axis=0, concat_axis=0, tiled=True)]
    dot_general x2, matrix products: 26.5 us -> 43.5 us  [the longest x1 24 us: shards(): lax.dot_general(arrived, gathered, (((1,), (1,)), ((), ())), preferred_el...]
    all_to_all x1 -> x0, starting transfers between devices: 4.24 us -> none  [shards(): lax.all_to_all(outgoing, 'mass', split_axis=0, concat_axis=0, tiled=True)]
  transfers between devices with their start and end apart: 4 -> 2, of which waited for: 3 -> 2; matrix products, arithmetic and copies ran while one was open for 2% -> 1% of each run, Pallas kernels for 0% -> 0%
where the time goes in v1:
time: 249 us
  blocking collectives  155 us (62%)
  matrix products  45.3 us (18%)
  waiting for transfers between devices  23.6 us (9%)
  between operations  14.8 us (6%)
  other arithmetic  4.57 us (2%)
  starting transfers between devices  3.26 us (1%)
    unnamed x1, blocking collectives  130 us
    all_to_all x1, blocking collectives, shards(): lax.all_to_all(outgoing, 'mass', split_axis=0, concat_axis=0, tiled=True)  24.6 us
    dot_general x1, matrix products, shards(): lax.dot_general(arrived, gathered, (((1,), (1,)), ((), ())), preferred_el...  24 us
    all_gather x1, waiting for transfers between devices, shards(): gathered = lax.all_gather(arrived, 'tile', axis=0, tiled=True)  20.9 us
    dot_general x1, matrix products, shards(): consensus = jnp.dot(one_hot, gathered, preferred_element_type=jnp.float32)  19.5 us
  transfers between devices with their start and end apart: 2, of which 2 were waited for; matrix products, arithmetic and copies ran while one was open for 1% of the time, Pallas kernels for 0%

profile of v1, /device:TPU:1, one launch (start us, length us, event | category | flops | bytes accessed | tf_op | source)
XLA Modules:
  0.0 248.5 jit_solution(9566248526745233393)
XLA Ops:
  7.2 0.0 all-gather.2.cloned.1.call-start
  7.2 1.4 fusion
  8.6 0.7 fusion.8
  9.4 0.1 reduce_window_sum.11
  9.5 0.8 select_reduce_fusion.1
  10.3 0.7 multiply_add_fusion
  11.0 0.0 copy-start
  11.0 1.8 convolution_convert_fusion
  12.8 24.6 %all_to_all.14 = bf16[4,48,4096]{2,1,0:T(8,128)(2,1)} all-to-all(bf16[4,48,4096]{2,1,0:T(8,128)(2,1)S(1)} %bitcast.11), channel_id=1, replica_groups=mesh['mass'=4,'tile'=32] {'mass'}, dimensions={0} | all-to-all | bytes 3145728 | tf_op jit(solution)/shard_map/all_to_all | solution.py:35
  37.4 0.0 all-gather.2.cloned.1.call-update
  37.4 0.1 select_reduce_fusion
  37.6 0.7 all_to_all.10
  38.2 3.2 %all-to-all-start.1 = ((s32[4,1,48]{2,1,0:T(1,128)}), s32[4,1,48]{2,1,0:T(1,128)S(1)}, u32[]{:S(2)}, u32[]{:S(2)}) async-start(s32[4,1,48]{2,1,0:T(1,128)} %all_to_all.10), calls=%async_computation.1 | async-start | bytes 4096 | tf_op jit(solution)/shard_map/all_to_all | solution.py:36
  41.5 0.0 copy-done
  41.5 0.6 dynamic-slice
  42.7 2.8 %all-to-all-done.1 = s32[4,1,48]{2,1,0:T(1,128)S(1)} async-done(((s32[4,1,48]{2,1,0:T(1,128)}), s32[4,1,48]{2,1,0:T(1,128)S(1)}, u32[]{:S(2)}, u32[]{:S(2)}) %all-to-all-start.1) | async-done | bytes 800 | tf_op jit(solution)/shard_map/all_to_all | solution.py:36
  45.5 0.5 broadcast.30
  46.0 0.7 reduce.3
  46.7 0.1 reshape.43
  46.7 0.2 dynamic-update-slice
  47.0 130.3 %all-reduce = s32[6144]{0:T(1024)S(1)} all-reduce(s32[6144]{0:T(1024)S(1)} %dynamic-update-slice), channel_id=1, replica_groups=mesh['mass'=4,'tile'=32] {'tile'}, use_global_device_ids=true, to_apply=%add | all-reduce | flops 6144 | bytes 49152
  177.3 20.9 %all-gather.2.cloned.1.call-done = bf16[6144,4096]{1,0:T(8,128)(2,1)} async-done(((bf16[192,4096]{1,0:T(8,128)(2,1)}), bf16[6144,4096]{1,0:T(8,128)(2,1)}) %all-gather.2.cloned.1.call-update) | async-done | bytes 50331664 | tf_op jit(solution)/shard_map/all_gather | solution.py:40
  198.2 24.0 %convolution_multiply_fusion = f32[192,6144]{1,0:T(8,128)} fusion(bf16[192,4096]{1,0:T(8,128)(2,1)} %bitcast.10, bf16[6144,4096]{1,0:T(8,128)(2,1)} %all-gather.2.cloned.1.call-done), kind=kOutput, calls=%fused_computation | convolution fusion | flops 9664856064 | bytes 56623104 | tf_op jit(solution)/shard_map/dot_general | solution.py:42
  222.2 19.5 %fusion.4 = f32[4,4096]{1,0:T(4,128)} fusion(bf16[6144,4096]{1,0:T(8,128)(2,1)} %all-gather.2.cloned.1.call-done, s32[6144]{0:T(1024)S(1)} %all-reduce, s32[4]{0:T(128)S(1)} %iota_add_fusion), kind=kOutput, calls=%fused_computation.9 | convolution fusion | flops 201351168 | bytes 50421776 | tf_op jit(solution)/shard_map/dot_general | solution.py:55
  (3 shorter events, 0.0 us)
Async XLA Ops:
  7.2 191.0 %all-gather.2.cloned.1.call-start = ((), (), s32[]{:S(2)}) async-start(), calls=%async_computation.2 | async-start | bytes 51904512 | tf_op jit(solution)/shard_map/all_gather | solution.py:40
  11.0 30.5 %copy-start = (u32[128]{0:T(128)S(1)}, u32[128]{0:T(128)}, u32[]{:S(2)}) copy-start(u32[128]{0:T(128)} %constant.39) | copy-start | bytes 1540
  38.2 7.3 %all-to-all-start.1 = ((s32[4,1,48]{2,1,0:T(1,128)}), s32[4,1,48]{2,1,0:T(1,128)S(1)}, u32[]{:S(2)}, u32[]{:S(2)}) async-start(s32[4,1,48]{2,1,0:T(1,128)} %all_to_all.10), calls=%async_computation.1 | async-start | bytes 4096 | tf_op jit(solution)/shard_map/all_to_all | solution.py:36
Sparse Core Ops, SparseCore 0:
  37.6 160.5 all-gather.1

commit v2 on v1

v2 whole, which is shorter than its diff:
```python
import jax
import jax.numpy as jnp
from jax import lax
from jax.sharding import PartitionSpec as P


CL_DEV = 4
CHUNKS = 4
LABEL_COLS = 128


def shards(spectra, window, cluster):
    s_dev, num_bins = spectra.shape
    mass_count = lax.axis_size("mass")
    capacity = 2 * s_dev // mass_count
    slot_count = mass_count * capacity
    values = spectra.astype(jnp.float32)
    scaled = (values * lax.rsqrt(jnp.mean(values * values, axis=1, keepdims=True) + 1e-06)).astype(
        jnp.bfloat16
    )
    target = window[:, 0]
    member = (target[:, None] == jnp.arange(mass_count, dtype=jnp.int32)[None, :]).astype(jnp.int32)
    before = jnp.cumsum(member, axis=0) - member
    slot_rank = jnp.sum(before * member, axis=1)
    position = target * capacity + slot_rank
    chosen = jnp.arange(slot_count, dtype=jnp.int32)[:, None] == position[None, :]
    tagged = jnp.concatenate(
        [
            jnp.broadcast_to(cluster[:, None].astype(jnp.bfloat16), (s_dev, LABEL_COLS)),
            scaled,
        ],
        axis=1,
    )
    outgoing = jnp.dot(
        chosen.astype(jnp.bfloat16), tagged, preferred_element_type=jnp.float32
    ).astype(jnp.bfloat16)
    empty = jnp.logical_not(jnp.any(chosen, axis=1))
    outgoing = outgoing.at[:, :LABEL_COLS].set(
        jnp.where(empty[:, None], jnp.bfloat16(-1), outgoing[:, :LABEL_COLS])
    )
    outgoing = outgoing.reshape(mass_count, capacity, LABEL_COLS + num_bins)
    own_ids = lax.axis_index("tile") * CL_DEV + jnp.arange(CL_DEV, dtype=jnp.int32)

    chunk = num_bins // CHUNKS
    gram = None
    one_hot = None
    consensus_parts = []
    for j in range(CHUNKS):
        lo = 0 if j == 0 else LABEL_COLS + j * chunk
        hi = LABEL_COLS + (j + 1) * chunk
        piece = outgoing[:, :, lo:hi]
        arrived = lax.all_to_all(piece, "mass", split_axis=0, concat_axis=0, tiled=True)
        arrived = arrived.reshape(slot_count, hi - lo)
        gathered = lax.all_gather(arrived, "tile", axis=0, tiled=True)
        if j == 0:
            labels = gathered[:, 0].astype(jnp.int32)
            one_hot = (own_ids[:, None] == labels[None, :]).astype(jnp.bfloat16)
            arrived = arrived[:, LABEL_COLS:]
            gathered = gathered[:, LABEL_COLS:]
        part = lax.dot_general(
            arrived, gathered, (((1,), (1,)), ((), ())), preferred_element_type=jnp.float32
        ) * (1.0 / num_bins)
        gram = lax.optimization_barrier(part if gram is None else gram + part)
        consensus_parts.append(jnp.dot(one_hot, gathered, preferred_element_type=jnp.float32))
    gram_tiles = gram
    consensus = jnp.concatenate(consensus_parts, axis=1)
    return (gram_tiles, consensus)


def solution(mesh):
    in_specs = (P(("mass", "tile"), None), P(("mass", "tile"), None), P(("mass", "tile")))
    out_specs = (P(("mass", "tile"), None), P(("mass", "tile"), None))
    return jax.shard_map(shards, mesh=mesh, in_specs=in_specs, out_specs=out_specs, check_vma=False)
```

time: 249 us -> 331 us (1.33)
  waiting for transfers between devices: 23.6 us -> 199 us
  blocking collectives: 155 us -> 40.1 us
  matrix products: 45.3 us -> 65.4 us
  other arithmetic: 4.57 us -> 10.3 us
    all_gather x1 -> x4, waiting for transfers between devices: 20.9 us -> 199 us  [shards(): gathered = lax.all_gather(arrived, 'tile', axis=0, tiled=True)]
    unnamed x1 -> x0, blocking collectives: 130 us -> none
    dot_general x1 -> x4, matrix products: 24 us -> 48.3 us  [shards(): lax.dot_general(arrived, gathered, (((1,), (1,)), ((), ())), preferred_el...]
    all_to_all x1 -> x4, blocking collectives: 24.6 us -> 40.1 us  [shards(): lax.all_to_all(piece, 'mass', split_axis=0, concat_axis=0, tiled=True)]
    convert_element_type x0 -> x3, other arithmetic: none -> 4.29 us  [the longest x1 2.29 us: shards(): labels = gathered[:, 0].astype(jnp.int32)]
    dot_general x2 -> x5, matrix products: 21.3 us -> 17.1 us  [the longest x4 16.5 us: shards(): jnp.dot(one_hot, gathered, preferred_element_type=jnp.float32)]
  transfers between devices with their start and end apart: 2 -> 4, of which waited for: 2 -> 4; matrix products, arithmetic and copies ran while one was open for 1% -> 11% of each run, Pallas kernels for 0% -> 0%
where the time goes in v2:
time: 331 us
  waiting for transfers between devices  199 us (60%)
  matrix products  65.4 us (20%)
  blocking collectives  40.1 us (12%)
  between operations  13.9 us (4%)
  other arithmetic  10.3 us (3%)
    all_gather x4, waiting for transfers between devices, shards(): gathered = lax.all_gather(arrived, 'tile', axis=0, tiled=True)  199 us
    dot_general x4, matrix products, shards(): lax.dot_general(arrived, gathered, (((1,), (1,)), ((), ())), preferred_el...  48.3 us
    all_to_all x4, blocking collectives, shards(): lax.all_to_all(piece, 'mass', split_axis=0, concat_axis=0, tiled=True)  40.1 us
    dot_general x4, matrix products, shards(): jnp.dot(one_hot, gathered, preferred_element_type=jnp.float32)  16.5 us
  transfers between devices with their start and end apart: 4, of which 4 were waited for; matrix products, arithmetic and copies ran while one was open for 11% of the time, Pallas kernels for 0%

profile of v2, /device:TPU:1, one launch (start us, length us, event | category | flops | bytes accessed | tf_op | source)
XLA Modules:
  0.0 330.8 jit_solution(12370668141826713607)
XLA Ops:
  7.2 0.6 compare_reduce_fusion
  7.8 0.7 convert_element_type.29
  8.5 1.4 fusion.10
  9.9 0.7 fusion.30
  10.7 0.1 reduce_window_sum.11
  10.8 0.8 select_reduce_fusion
  11.6 0.7 multiply_add_fusion
  12.3 0.1 fusion.23
  12.4 1.3 fusion.11
  13.9 0.6 convolution_convert_fusion
  14.4 0.8 fusion.24
  15.3 12.2 %all_to_all.20 = bf16[4,48,1152]{2,1,0:T(8,128)(2,1)} all-to-all(bf16[4,48,1152]{2,1,0:T(8,128)(2,1)S(1)} %slice.50), channel_id=1, replica_groups=mesh['mass'=4,'tile'=32] {'mass'}, dimensions={0} | all-to-all | bytes 884736 | tf_op jit(solution)/shard_map/all_to_all | solution.py:52
  27.5 0.1 fusion.36
  27.7 9.3 %all_to_all.21 = bf16[4,48,1024]{2,1,0:T(8,128)(2,1)} all-to-all(bf16[4,48,1024]{2,1,0:T(8,128)(2,1)S(1)} %get-tuple-element.16), channel_id=1, replica_groups=mesh['mass'=4,'tile'=32] {'mass'}, dimensions={0} | all-to-all | bytes 786432 | tf_op jit(solution)/shard_map/all_to_all | solution.py:52
  37.1 9.3 %all_to_all.22 = bf16[4,48,1024]{2,1,0:T(8,128)(2,1)} all-to-all(bf16[4,48,1024]{2,1,0:T(8,128)(2,1)S(1)} %get-tuple-element.15), channel_id=1, replica_groups=mesh['mass'=4,'tile'=32] {'mass'}, dimensions={0} | all-to-all | bytes 786432 | tf_op jit(solution)/shard_map/all_to_all | solution.py:52
  46.4 9.3 %all_to_all.23 = bf16[4,48,1024]{2,1,0:T(8,128)(2,1)} all-to-all(bf16[4,48,1024]{2,1,0:T(8,128)(2,1)S(1)} %get-tuple-element.14), channel_id=1, replica_groups=mesh['mass'=4,'tile'=32] {'mass'}, dimensions={0} | all-to-all | bytes 786432 | tf_op jit(solution)/shard_map/all_to_all | solution.py:52
  55.8 40.8 %all-gather.5.cloned.1.call-done = bf16[6144,1152]{1,0:T(8,128)(2,1)} async-done(((bf16[192,1152]{1,0:T(8,128)(2,1)}), bf16[6144,1152]{1,0:T(8,128)(2,1)}) %all-gather.5.cloned.1.call-update) | async-done | bytes 14155792 | tf_op jit(solution)/shard_map/all_gather | solution.py:54
  96.6 11.0 %fusion.4 = f32[192,6144]{1,0:T(8,128)} fusion(bf16[6144,1152]{1,0:T(8,128)(2,1)} %all-gather.5.cloned.1.call-done, bf16[192,1152]{1,0:T(8,128)(2,1)S(1)} %bitcast.29), kind=kOutput, calls=%fused_computation.7 | convolution fusion | flops 2417098752 | bytes 17694720 | tf_op jit(solution)/shard_map/dot_general | solution.py:60
  107.7 53.6 %all-gather.7.cloned.1.call-done = bf16[6144,1024]{1,0:T(8,128)(2,1)} async-done(((bf16[192,1024]{1,0:T(8,128)(2,1)}), bf16[6144,1024]{1,0:T(8,128)(2,1)}) %all-gather.7.cloned.1.call-update) | async-done | bytes 12582928 | tf_op jit(solution)/shard_map/all_gather | solution.py:54
  161.3 12.4 %fusion.7 = f32[192,6144]{1,0:T(8,128)} fusion(f32[192,6144]{1,0:T(8,128)} %fusion.4, bf16[192,1024]{1,0:T(8,128)(2,1)S(1)} %bitcast.23, bf16[6144,1024]{1,0:T(8,128)(2,1)} %all-gather.7.cloned.1.call-done), kind=kOutput, calls=%fused_computation.8 | convolution fusion | flops 2418278400 | bytes 22413312 | tf_op jit(solution)/shard_map/dot_general | solution.py:60
  173.7 52.3 %all-gather.9.cloned.1.call-done = bf16[6144,1024]{1,0:T(8,128)(2,1)} async-done(((bf16[192,1024]{1,0:T(8,128)(2,1)}), bf16[6144,1024]{1,0:T(8,128)(2,1)}) %all-gather.9.cloned.1.call-update) | async-done | bytes 12582928 | tf_op jit(solution)/shard_map/all_gather | solution.py:54
  226.0 12.4 %fusion.8 = f32[192,6144]{1,0:T(8,128)} fusion(f32[192,6144]{1,0:T(8,128)} %fusion.7, bf16[192,1024]{1,0:T(8,128)(2,1)S(1)} %bitcast.25, bf16[6144,1024]{1,0:T(8,128)(2,1)} %all-gather.9.cloned.1.call-done), kind=kOutput, calls=%fused_computation.9 | convolution fusion | flops 2418278400 | bytes 22413312 | tf_op jit(solution)/shard_map/dot_general | solution.py:60
  238.3 52.2 %all-gather.11.cloned.1.call-done = bf16[6144,1024]{1,0:T(8,128)(2,1)} async-done(((bf16[192,1024]{1,0:T(8,128)(2,1)}), bf16[6144,1024]{1,0:T(8,128)(2,1)}) %all-gather.11.cloned.1.call-update) | async-done | bytes 12582928 | tf_op jit(solution)/shard_map/all_gather | solution.py:54
  290.5 12.5 %fusion.9 = f32[192,6144]{1,0:T(8,128)} fusion(f32[192,6144]{1,0:T(8,128)} %fusion.8, bf16[192,1024]{1,0:T(8,128)(2,1)S(1)} %bitcast.27, bf16[6144,1024]{1,0:T(8,128)(2,1)} %all-gather.11.cloned.1.call-done), kind=kOutput, calls=%fused_computation.10 | convolution fusion | flops 2418278400 | bytes 22413312 | tf_op jit(solution)/shard_map/dot_general | solution.py:60
  303.0 2.3 convert_reduce_fusion
  305.4 6.5 %fusion.16 = f32[4,1024]{1,0:T(4,128)S(1)} fusion(bf16[6144,1024]{1,0:T(8,128)(2,1)} %all-gather.11.cloned.1.call-done, s32[6144]{0:T(1024)S(1)} %convert_reduce_fusion, s32[4]{0:T(128)S(1)} %iota_add_fusion), kind=kOutput, calls=%fused_computation.21 | convolution fusion | flops 50356224 | bytes 12623888 | tf_op jit(solution)/shard_map/dot_general | solution.py:64
  311.9 6.5 %fusion.18 = f32[4,1024]{1,0:T(4,128)S(1)} fusion(bf16[6144,1024]{1,0:T(8,128)(2,1)} %all-gather.9.cloned.1.call-done, s32[6144]{0:T(1024)S(1)} %convert_reduce_fusion, s32[4]{0:T(128)S(1)} %iota_add_fusion), kind=kOutput, calls=%fused_computation.23 | convolution fusion | flops 50356224 | bytes 12623888 | tf_op jit(solution)/shard_map/dot_general | solution.py:64
  318.4 1.8 fusion.20
  320.2 1.3 slice-done.5
  321.5 0.4 slice-done.6
  321.9 1.8 fusion
  323.6 0.7 pad_maximum_fusion
  (35 shorter events, 0.4 us)
Async XLA Ops:
  7.2 89.5 %all-gather.5.cloned.1.call-start = ((), (), s32[]{:S(2)}) async-start(), calls=%async_computation.4 | async-start | bytes 14598144 | tf_op jit(solution)/shard_map/all_gather | solution.py:54
  27.4 69.2 %copy-start.3 = (bf16[4,48,1152]{2,1,0:T(8,128)(2,1)S(1)}, bf16[4,48,1152]{2,1,0:T(8,128)(2,1)}, u32[]{:S(2)}) copy-start(bf16[4,48,1152]{2,1,0:T(8,128)(2,1)} %all_to_all.20) | copy-start | bytes 1327108
  27.5 133.8 %all-gather.7.cloned.1.call-start = ((), (), s32[]{:S(2)}) async-start(), calls=%async_computation.5 | async-start | bytes 12976128 | tf_op jit(solution)/shard_map/all_gather | solution.py:54
  37.0 189.0 %all-gather.9.cloned.1.call-start = ((), (), s32[]{:S(2)}) async-start(), calls=%async_computation.6 | async-start | bytes 12976128 | tf_op jit(solution)/shard_map/all_gather | solution.py:54
  46.4 244.1 %all-gather.11.cloned.1.call-start = ((), (), s32[]{:S(2)}) async-start(), calls=%async_computation.7 | async-start | bytes 12976128 | tf_op jit(solution)/shard_map/all_gather | solution.py:54
  55.8 105.5 %copy-start = (bf16[4,48,1024]{2,1,0:T(8,128)(2,1)S(1)}, bf16[4,48,1024]{2,1,0:T(8,128)(2,1)}, u32[]{:S(2)}) copy-start(bf16[4,48,1024]{2,1,0:T(8,128)(2,1)} %all_to_all.21) | copy-start | bytes 1179652
  107.6 118.3 %copy-start.1 = (bf16[4,48,1024]{2,1,0:T(8,128)(2,1)S(1)}, bf16[4,48,1024]{2,1,0:T(8,128)(2,1)}, u32[]{:S(2)}) copy-start(bf16[4,48,1024]{2,1,0:T(8,128)(2,1)} %all_to_all.22) | copy-start | bytes 1179652
  173.7 116.8 %copy-start.2 = (bf16[4,48,1024]{2,1,0:T(8,128)(2,1)S(1)}, bf16[4,48,1024]{2,1,0:T(8,128)(2,1)}, u32[]{:S(2)}) copy-start(bf16[4,48,1024]{2,1,0:T(8,128)(2,1)} %all_to_all.23) | copy-start | bytes 1179652
  305.3 13.0 %slice-start = ((s8[12582912]{0:T(1024)(128)(4,1)}), s8[4194304]{0:T(1024)(128)(4,1)S(1)}, s32[]{:S(2)}) async-start(s8[12582912]{0:T(1024)(128)(4,1)} %bitcast.16), calls=%async_computation.8 | async-start | bytes 8388608
  305.4 13.0 %slice-start.1 = ((s8[12582912]{0:T(1024)(128)(4,1)}), s8[4194304]{0:T(1024)(128)(4,1)S(1)}, s32[]{:S(2)}) async-start(s8[12582912]{0:T(1024)(128)(4,1)} %bitcast.16), calls=%async_computation.9 | async-start | bytes 8388608
  311.9 6.5 %slice-start.2 = ((s8[12582912]{0:T(1024)(128)(4,1)}), s8[4194304]{0:T(1024)(128)(4,1)S(1)}, s32[]{:S(2)}) async-start(s8[12582912]{0:T(1024)(128)(4,1)} %bitcast.16), calls=%async_computation.10 | async-start | bytes 8388608
  311.9 8.3 %slice-start.3 = ((s8[14155776]{0:T(1024)(128)(4,1)}), s8[4194304]{0:T(1024)(128)(4,1)S(1)}, s32[]{:S(2)}) async-start(s8[14155776]{0:T(1024)(128)(4,1)} %bitcast.18), calls=%async_computation.11 | async-start | bytes 8388608
  311.9 8.3 %slice-start.4 = ((s8[14155776]{0:T(1024)(128)(4,1)}), s8[4194304]{0:T(1024)(128)(4,1)S(1)}, s32[]{:S(2)}) async-start(s8[14155776]{0:T(1024)(128)(4,1)} %bitcast.18), calls=%async_computation.12 | async-start | bytes 8388608
  318.4 3.1 slice-start.5
  318.4 3.5 %slice-start.6 = ((s8[14155776]{0:T(1024)(128)(4,1)}), s8[1572864]{0:T(1024)(128)(4,1)S(1)}, s32[]{:S(2)}) async-start(s8[14155776]{0:T(1024)(128)(4,1)} %bitcast.18), calls=%async_computation.14 | async-start | bytes 3145728
Sparse Core Ops, SparseCore 0:
  27.6 68.9 all-gather.4
  98.9 62.3 all-gather.6
  163.5 62.3 all-gather.8
  228.1 62.3 all-gather.10

commit v3 on v1

--- a/solution.py
+++ b/solution.py
@@ -2,6 +2,7 @@
 import jax.numpy as jnp
 from jax import lax
 from jax.sharding import PartitionSpec as P
+
 
 CL_DEV = 4
 
@@ -37,8 +38,16 @@
     )
     arrived = arrived.reshape(slot_count, num_bins)
     arrived_labels = arrived_labels.reshape(slot_count)
+    tile_count = lax.axis_size("tile")
+    local_labels = arrived_labels - lax.axis_index("mass") * per_window
+    cluster_ids = jnp.arange(per_window, dtype=jnp.int32)
+    one_hot = (cluster_ids[:, None] == local_labels[None, :]).astype(jnp.bfloat16)
     gathered = lax.all_gather(arrived, "tile", axis=0, tiled=True)
-    gathered_labels = lax.all_gather(arrived_labels, "tile", axis=0, tiled=True)
+    partial = jnp.dot(one_hot, arrived, preferred_element_type=jnp.float32)
+    pieces = lax.all_to_all(
+        partial.reshape(tile_count, CL_DEV, num_bins), "tile", split_axis=0, concat_axis=0, tiled=True
+    )
+    consensus = jnp.sum(pieces, axis=0)
     product = lax.dot_general(
         arrived,
         gathered,
@@ -46,13 +55,6 @@
         preferred_element_type=jnp.float32,
     )
     gram_tiles = product * (1.0 / num_bins)
-    own_ids = (
-        lax.axis_index("mass") * per_window
-        + lax.axis_index("tile") * CL_DEV
-        + jnp.arange(CL_DEV, dtype=jnp.int32)
-    )
-    one_hot = (own_ids[:, None] == gathered_labels[None, :]).astype(jnp.bfloat16)
-    consensus = jnp.dot(one_hot, gathered, preferred_element_type=jnp.float32)
     return (gram_tiles, consensus)
 
 

time: 249 us -> 252 us (1.012)
  waiting for transfers between devices: 23.6 us -> 118 us
  blocking collectives: 155 us -> 80 us
  matrix products: 45.3 us -> 26.9 us
    unnamed x1 -> x0, blocking collectives: 130 us -> none
    all_gather x1, waiting for transfers between devices: 20.9 us -> 114 us  [shards(): gathered = lax.all_gather(arrived, 'tile', axis=0, tiled=True)]
    all_to_all x0 -> x1, blocking collectives: none -> 55.4 us  [shards(): lax.all_to_all(partial.reshape(tile_count, CL_DEV, num_bins), 'tile', spl...]
    dot_general x1, matrix products: 19.5 us -> 0.49 us  [shards(): partial = jnp.dot(one_hot, arrived, preferred_element_type=jnp.float32)]
    reduce_sum x0 -> x1, other arithmetic: none -> 2.54 us  [shards(): consensus = jnp.sum(pieces, axis=0)]
  transfers between devices with their start and end apart: 2 -> 2, of which waited for: 2 -> 2; matrix products, arithmetic and copies ran while one was open for 1% -> 2% of each run, Pallas kernels for 0% -> 0%
where the time goes in v3:
time: 252 us; the launch traced here: 251 us
  waiting for transfers between devices  118 us (47%)
  blocking collectives  80 us (32%)
  matrix products  26.9 us (11%)
  between operations  14.1 us (6%)
  other arithmetic  6.47 us (3%)
  starting transfers between devices  3.26 us (1%)
    all_gather x1, waiting for transfers between devices, shards(): gathered = lax.all_gather(arrived, 'tile', axis=0, tiled=True)  114 us
    all_to_all x1, blocking collectives, shards(): lax.all_to_all(partial.reshape(tile_count, CL_DEV, num_bins), 'tile', spl...  55.4 us
    dot_general x1, matrix products, shards(): lax.dot_general(arrived, gathered, (((1,), (1,)), ((), ())), preferred_el...  24.6 us
    all_to_all x1, blocking collectives, shards(): lax.all_to_all(outgoing, 'mass', split_axis=0, concat_axis=0, tiled=True)  24.6 us
  transfers between devices with their start and end apart: 2, of which 2 were waited for; matrix products, arithmetic and copies ran while one was open for 2% of the time, Pallas kernels for 0%

profile of v3, /device:TPU:1, one launch (start us, length us, event | category | flops | bytes accessed | tf_op | source)
XLA Modules:
  0.0 251.1 jit_solution(1831602644974548425)
XLA Ops:
  7.2 0.0 all-gather.2.cloned.1.call-start
  7.2 0.7 fusion.9
  7.9 0.1 reduce_window_sum.11
  8.1 0.8 select_reduce_fusion.1
  8.9 1.4 fusion
  10.3 0.7 multiply_add_fusion.1
  11.0 1.8 convolution_convert_fusion
  12.8 24.6 %all_to_all.19 = bf16[4,48,4096]{2,1,0:T(8,128)(2,1)} all-to-all(bf16[4,48,4096]{2,1,0:T(8,128)(2,1)S(1)} %bitcast.13), channel_id=1, replica_groups=mesh['mass'=4,'tile'=32] {'mass'}, dimensions={0} | all-to-all | bytes 3145728 | tf_op jit(solution)/shard_map/all_to_all | solution.py:36
  37.4 0.0 copy-start
  37.4 0.0 all-gather.2.cloned.1.call-update
  37.4 0.1 select_reduce_fusion
  37.5 0.7 all_to_all.13
  38.2 3.2 %all-to-all-start.1 = ((s32[4,1,48]{2,1,0:T(1,128)}), s32[4,1,48]{2,1,0:T(1,128)S(1)}, u32[]{:S(2)}, u32[]{:S(2)}) async-start(s32[4,1,48]{2,1,0:T(1,128)} %all_to_all.13), calls=%async_computation.1 | async-start | bytes 4096 | tf_op jit(solution)/shard_map/all_to_all | solution.py:37
  41.5 4.0 %all-to-all-done.1 = s32[4,1,48]{2,1,0:T(1,128)S(1)} async-done(((s32[4,1,48]{2,1,0:T(1,128)}), s32[4,1,48]{2,1,0:T(1,128)S(1)}, u32[]{:S(2)}, u32[]{:S(2)}) %all-to-all-start.1) | async-done | bytes 800 | tf_op jit(solution)/shard_map/all_to_all | solution.py:37
  45.5 0.1 sub.19
  45.6 0.0 copy-done
  45.6 0.5 fusion.4
  46.1 1.4 copy.6
  47.4 55.4 %all_to_all.20 = f32[32,4,4096]{2,1,0:T(4,128)} all-to-all(f32[32,4,4096]{2,1,0:T(4,128)S(1)} %copy.6), channel_id=1, replica_groups=mesh['mass'=4,'tile'=32] {'tile'}, dimensions={0} | all-to-all | bytes 4194304 | tf_op jit(solution)/shard_map/all_to_all | solution.py:47
  102.8 2.5 %reduce_sum.29 = f32[4,4096]{1,0:T(4,128)} reduce(f32[32,4,4096]{2,1,0:T(4,128)} %all_to_all.20, f32[]{:T(128)} %constant.7.clone.1), dimensions={0}, to_apply=%region_4.5 | reduce | flops 507904 | bytes 2162692 | tf_op jit(solution)/shard_map/reduce_sum | solution.py:50
  105.4 114.2 %all-gather.2.cloned.1.call-done = bf16[6144,4096]{1,0:T(8,128)(2,1)} async-done(((bf16[192,4096]{1,0:T(8,128)(2,1)}), bf16[6144,4096]{1,0:T(8,128)(2,1)}) %all-gather.2.cloned.1.call-update) | async-done | bytes 50331664 | tf_op jit(solution)/shard_map/all_gather | solution.py:45
  219.6 24.6 %convolution_multiply_fusion = f32[192,6144]{1,0:T(8,128)} fusion(bf16[192,4096]{1,0:T(8,128)(2,1)S(1)} %bitcast.12, bf16[6144,4096]{1,0:T(8,128)(2,1)} %all-gather.2.cloned.1.call-done), kind=kOutput, calls=%fused_computation | convolution fusion | flops 9664856064 | bytes 56623104 | tf_op jit(solution)/shard_map/dot_general | solution.py:51
  (3 shorter events, 0.0 us)
Async XLA Ops:
  7.2 212.4 %all-gather.2.cloned.1.call-start = ((), (), s32[]{:S(2)}) async-start(), calls=%async_computation.3 | async-start | bytes 51904512 | tf_op jit(solution)/shard_map/all_gather | solution.py:45
  37.4 8.2 %copy-start = (bf16[4,48,4096]{2,1,0:T(8,128)(2,1)S(1)}, bf16[4,48,4096]{2,1,0:T(8,128)(2,1)}, u32[]{:S(2)}) copy-start(bf16[4,48,4096]{2,1,0:T(8,128)(2,1)} %all_to_all.19) | copy-start | bytes 4718596
  38.2 7.3 %all-to-all-start.1 = ((s32[4,1,48]{2,1,0:T(1,128)}), s32[4,1,48]{2,1,0:T(1,128)S(1)}, u32[]{:S(2)}, u32[]{:S(2)}) async-start(s32[4,1,48]{2,1,0:T(1,128)} %all_to_all.13), calls=%async_computation.1 | async-start | bytes 4096 | tf_op jit(solution)/shard_map/all_to_all | solution.py:37
Sparse Core Ops, SparseCore 0:
  37.5 181.9 all-gather.1

commit v4 on v1

--- a/solution.py
+++ b/solution.py
@@ -1,9 +1,55 @@
+import functools
+
 import jax
 import jax.numpy as jnp
 from jax import lax
+from jax.experimental import pallas as pl
+from jax.experimental.pallas import tpu as pltpu
 from jax.sharding import PartitionSpec as P
 
 CL_DEV = 4
+ONE_HOT_ROWS = 8
+
+def _gram_consensus_kernel(scale, a_ref, oh_ref, p_ref, g_ref, c_ref):
+    j = pl.program_id(0)
+    blk = p_ref[...]
+    g_ref[...] = lax.dot_general(
+        a_ref[...], blk, (((1,), (1,)), ((), ())), preferred_element_type=jnp.float32
+    ) * scale
+
+    @pl.when(j == 0)
+    def _():
+        c_ref[...] = jnp.zeros_like(c_ref)
+
+    c_ref[...] += jnp.dot(oh_ref[...], blk, preferred_element_type=jnp.float32)
+
+
+def gram_consensus(arrived, one_hot, gathered, block_rows=1024):
+    rows, bins = arrived.shape
+    total = gathered.shape[0]
+    heads = one_hot.shape[0]
+    steps = total // block_rows
+    flops = 2 * rows * total * bins + 2 * heads * total * bins
+    bytes_accessed = 2 * (rows * bins + heads * total + total * bins) + 4 * (rows * total + heads * bins)
+    return pl.pallas_call(
+        functools.partial(_gram_consensus_kernel, 1.0 / bins),
+        grid=(steps,),
+        in_specs=[
+            pl.BlockSpec((rows, bins), lambda j: (0, 0)),
+            pl.BlockSpec((heads, block_rows), lambda j: (0, j)),
+            pl.BlockSpec((block_rows, bins), lambda j: (j, 0)),
+        ],
+        out_specs=[
+            pl.BlockSpec((rows, block_rows), lambda j: (0, j)),
+            pl.BlockSpec((heads, bins), lambda j: (0, 0)),
+        ],
+        out_shape=[
+            jax.ShapeDtypeStruct((rows, total), jnp.float32),
+            jax.ShapeDtypeStruct((heads, bins), jnp.float32),
+        ],
+        compiler_params=pltpu.CompilerParams(dimension_semantics=("arbitrary",)),
+        cost_estimate=pl.CostEstimate(flops=flops, bytes_accessed=bytes_accessed, transcendentals=0),
+    )(arrived, one_hot, gathered)
 
 
 def shards(spectra, window, cluster):
@@ -39,20 +85,15 @@
     arrived_labels = arrived_labels.reshape(slot_count)
     gathered = lax.all_gather(arrived, "tile", axis=0, tiled=True)
     gathered_labels = lax.all_gather(arrived_labels, "tile", axis=0, tiled=True)
-    product = lax.dot_general(
-        arrived,
-        gathered,
-        (((1,), (1,)), ((), ())),
-        preferred_element_type=jnp.float32,
-    )
-    gram_tiles = product * (1.0 / num_bins)
     own_ids = (
         lax.axis_index("mass") * per_window
         + lax.axis_index("tile") * CL_DEV
-        + jnp.arange(CL_DEV, dtype=jnp.int32)
+        + jnp.arange(ONE_HOT_ROWS, dtype=jnp.int32)
     )
+    own_ids = jnp.where(jnp.arange(ONE_HOT_ROWS) < CL_DEV, own_ids, -2)
     one_hot = (own_ids[:, None] == gathered_labels[None, :]).astype(jnp.bfloat16)
-    consensus = jnp.dot(one_hot, gathered, preferred_element_type=jnp.float32)
+    gram_tiles, consensus = gram_consensus(arrived, one_hot, gathered)
+    consensus = consensus[:CL_DEV]
     return (gram_tiles, consensus)
 
 

time: 249 us -> 236 us (0.948)
  matrix products: 45.3 us -> 1.78 us
  Pallas kernels: 0 us -> 29.1 us
    dot_general x2 -> x0, matrix products: 43.5 us -> none  [the longest x1 24 us: shards(): lax.dot_general(arrived, gathered, (((1,), (1,)), ((), ())), preferred_el...]
    pallas_call x0 -> x1, Pallas kernels: none -> 29.1 us  [gram_consensus(): pl.pallas_call(functools.partial(_gram_consensus_kernel, 1.0 / bins), gri...]
where the time goes in v4:
time: 236 us
  blocking collectives  155 us (66%)
  Pallas kernels  29.1 us (12%)
  waiting for transfers between devices  22.9 us (10%)
  between operations  14.8 us (6%)
  other arithmetic  5.28 us (2%)
  local copies, waits for them, and re-layouts  3.63 us (2%)
  starting transfers between devices  3.26 us (1%)
    unnamed x1, blocking collectives  130 us
    pallas_call x1, Pallas kernels, gram_consensus(): pl.pallas_call(functools.partial(_gram_consensus_kernel, 1.0 / bins), gri...  29.1 us
    all_to_all x1, blocking collectives, shards(): lax.all_to_all(outgoing, 'mass', split_axis=0, concat_axis=0, tiled=True)  24.6 us
    all_gather x1, waiting for transfers between devices, shards(): gathered = lax.all_gather(arrived, 'tile', axis=0, tiled=True)  20.1 us
  transfers between devices with their start and end apart: 2, of which 2 were waited for; matrix products, arithmetic and copies ran while one was open for 1% of the time, Pallas kernels for 0%

profile of v4, /device:TPU:1, one launch (start us, length us, event | category | flops | bytes accessed | tf_op | source)
XLA Modules:
  0.0 235.6 jit_solution(13421480366933918389)
XLA Ops:
  7.2 0.0 all-gather.2.cloned.1.call-start
  7.2 1.4 fusion
  8.6 0.7 fusion.5
  9.4 0.1 reduce_window_sum.11
  9.5 0.8 select_reduce_fusion.1
  10.3 0.7 multiply_add_fusion
  11.0 1.8 convolution_convert_fusion
  12.8 24.6 %all_to_all.14 = bf16[4,48,4096]{2,1,0:T(8,128)(2,1)} all-to-all(bf16[4,48,4096]{2,1,0:T(8,128)(2,1)S(1)} %bitcast.8), channel_id=1, replica_groups=mesh['mass'=4,'tile'=32] {'mass'}, dimensions={0} | all-to-all | bytes 3145728 | tf_op jit(solution)/shard_map/all_to_all | solution.py:81
  37.4 0.0 copy-start
  37.4 0.0 all-gather.2.cloned.1.call-update
  37.4 0.1 select_reduce_fusion
  37.5 0.7 all_to_all.10
  38.2 3.2 %all-to-all-start.1 = ((s32[4,1,48]{2,1,0:T(1,128)}), s32[4,1,48]{2,1,0:T(1,128)S(1)}, u32[]{:S(2)}, u32[]{:S(2)}) async-start(s32[4,1,48]{2,1,0:T(1,128)} %all_to_all.10), calls=%async_computation.1 | async-start | bytes 4096 | tf_op jit(solution)/shard_map/all_to_all | solution.py:82
  41.5 0.0 copy-done
  41.5 0.6 dynamic-slice
  42.7 2.8 %all-to-all-done.1 = s32[4,1,48]{2,1,0:T(1,128)S(1)} async-done(((s32[4,1,48]{2,1,0:T(1,128)}), s32[4,1,48]{2,1,0:T(1,128)S(1)}, u32[]{:S(2)}, u32[]{:S(2)}) %all-to-all-start.1) | async-done | bytes 800 | tf_op jit(solution)/shard_map/all_to_all | solution.py:82
  45.5 0.5 broadcast.43
  46.0 0.7 reduce.3
  46.6 0.1 reshape.48
  46.7 0.2 dynamic-update-slice
  47.0 130.3 %all-reduce = s32[6144]{0:T(1024)S(1)} all-reduce(s32[6144]{0:T(1024)S(1)} %dynamic-update-slice), channel_id=1, replica_groups=mesh['mass'=4,'tile'=32] {'tile'}, use_global_device_ids=true, to_apply=%add | all-reduce | flops 6144 | bytes 49152
  177.3 0.7 compare_convert_fusion.oh_ref
  178.0 20.1 %all-gather.2.cloned.1.call-done.p_ref = bf16[6144,4096]{1,0:T(8,128)(2,1)} async-done(((bf16[192,4096]{1,0:T(8,128)(2,1)}), bf16[6144,4096]{1,0:T(8,128)(2,1)}) %all-gather.2.cloned.1.call-update) | async-done | bytes 50331664 | tf_op jit(solution)/shard_map/all_gather | solution.py:86
  198.2 29.1 %shard_map.50 = (f32[192,6144]{1,0:T(8,128)}, f32[8,4096]{1,0:T(8,128)}) custom-call(bf16[192,4096]{1,0:T(8,128)(2,1)} %bitcast.7, bf16[8,6144]{1,0:T(8,128)(2,1)} %compare_convert_fusion.oh_ref, bf16[6144,4096]{1,0:T(8,128)(2,1)} %all-gather.2.cloned.1.call-done.p_ref), custom_call_target="tpu_custom_call" | custom-call | flops 10066329600 | bytes 56852480 | tf_op jit(solution)/shard_map/pallas_call | solution.py:34
  227.2 1.5 slice.3
  (3 shorter events, 0.0 us)
Async XLA Ops:
  7.2 191.0 %all-gather.2.cloned.1.call-start = ((), (), s32[]{:S(2)}) async-start(), calls=%async_computation.2 | async-start | bytes 51904512 | tf_op jit(solution)/shard_map/all_gather | solution.py:86
  37.4 4.1 %copy-start = (u32[128]{0:T(128)S(1)}, u32[128]{0:T(128)}, u32[]{:S(2)}) copy-start(u32[128]{0:T(128)} %constant.41) | copy-start | bytes 1540
  38.2 7.3 %all-to-all-start.1 = ((s32[4,1,48]{2,1,0:T(1,128)}), s32[4,1,48]{2,1,0:T(1,128)S(1)}, u32[]{:S(2)}, u32[]{:S(2)}) async-start(s32[4,1,48]{2,1,0:T(1,128)} %all_to_all.10), calls=%async_computation.1 | async-start | bytes 4096 | tf_op jit(solution)/shard_map/all_to_all | solution.py:82
Sparse Core Ops, SparseCore 0:
  37.5 160.5 all-gather.1

commit v5 on v4

--- a/solution.py
+++ b/solution.py
@@ -8,7 +8,7 @@
 from jax.sharding import PartitionSpec as P
 
 CL_DEV = 4
-ONE_HOT_ROWS = 8
+ONE_HOT_ROWS = 4
 
 def _gram_consensus_kernel(scale, a_ref, oh_ref, p_ref, g_ref, c_ref):
     j = pl.program_id(0)
@@ -52,6 +52,16 @@
     )(arrived, one_hot, gathered)
 
 
+def exchange_over_mass(pieces, mass_count):
+    me = lax.axis_index("mass")
+    held = [pieces[me]]
+    for shift in range(1, mass_count):
+        perm = [(i, (i + shift) % mass_count) for i in range(mass_count)]
+        held.append(lax.ppermute(pieces[(me + shift) % mass_count], "mass", perm))
+    stacked = jnp.stack(held)
+    return stacked[(me - jnp.arange(mass_count)) % mass_count]
+
+
 def shards(spectra, window, cluster):
     s_dev, num_bins = spectra.shape
     mass_count = lax.axis_size("mass")
@@ -77,10 +87,8 @@
     labels = jnp.max(jnp.where(chosen, global_ids[None, :], -1), axis=1).reshape(
         mass_count, capacity
     )
-    arrived, arrived_labels = (
-        lax.all_to_all(outgoing, "mass", split_axis=0, concat_axis=0, tiled=True),
-        lax.all_to_all(labels, "mass", split_axis=0, concat_axis=0, tiled=True),
-    )
+    arrived = exchange_over_mass(outgoing, mass_count)
+    arrived_labels = exchange_over_mass(labels, mass_count)
     arrived = arrived.reshape(slot_count, num_bins)
     arrived_labels = arrived_labels.reshape(slot_count)
     gathered = lax.all_gather(arrived, "tile", axis=0, tiled=True)
@@ -90,10 +98,8 @@
         + lax.axis_index("tile") * CL_DEV
         + jnp.arange(ONE_HOT_ROWS, dtype=jnp.int32)
     )
-    own_ids = jnp.where(jnp.arange(ONE_HOT_ROWS) < CL_DEV, own_ids, -2)
     one_hot = (own_ids[:, None] == gathered_labels[None, :]).astype(jnp.bfloat16)
     gram_tiles, consensus = gram_consensus(arrived, one_hot, gathered)
-    consensus = consensus[:CL_DEV]
     return (gram_tiles, consensus)
 
 

time: 236 us -> 233 us (0.987)
  blocking collectives: 155 us -> 130 us
  waiting for transfers between devices: 22.9 us -> 44.1 us
  starting transfers between devices: 3.26 us -> 6.06 us
    all_to_all x1 -> x0, blocking collectives: 24.6 us -> none  [shards(): lax.all_to_all(outgoing, 'mass', split_axis=0, concat_axis=0, tiled=True)]
    ppermute x0 -> x6, waiting for transfers between devices: none -> 21.9 us  [exchange_over_mass(): held.append(lax.ppermute(pieces[(me + shift) % mass_count], 'mass', perm))]
    ppermute x0 -> x6, starting transfers between devices: none -> 6.02 us  [exchange_over_mass(): held.append(lax.ppermute(pieces[(me + shift) % mass_count], 'mass', perm))]
    all_to_all x1 -> x0, starting transfers between devices: 3.22 us -> none  [shards(): lax.all_to_all(labels, 'mass', split_axis=0, concat_axis=0, tiled=True)]
    all_to_all x1 -> x0, waiting for transfers between devices: 2.75 us -> none  [shards(): lax.all_to_all(labels, 'mass', split_axis=0, concat_axis=0, tiled=True)]
  transfers between devices with their start and end apart: 2 -> 7, of which waited for: 2 -> 6; matrix products, arithmetic and copies ran while one was open for 1% -> 1% of each run, Pallas kernels for 0% -> 0%
where the time goes in v5:
time: 233 us
  blocking collectives  130 us (56%)
  waiting for transfers between devices  44.1 us (19%)
  Pallas kernels  29.1 us (12%)
  between operations  14.8 us (6%)
  starting transfers between devices  6.06 us (3%)
  other arithmetic  4.89 us (2%)
  local copies, waits for them, and re-layouts  3.47 us (1%)
    unnamed x1, blocking collectives  130 us
    pallas_call x1, Pallas kernels, gram_consensus(): pl.pallas_call(functools.partial(_gram_consensus_kernel, 1.0 / bins), gri...  29.1 us
    all_gather x1, waiting for transfers between devices, shards(): gathered = lax.all_gather(arrived, 'tile', axis=0, tiled=True)  22.1 us
    ppermute x6, waiting for transfers between devices, exchange_over_mass(): held.append(lax.ppermute(pieces[(me + shift) % mass_count], 'mass', perm))  21.9 us
    ppermute x6, starting transfers between devices, exchange_over_mass(): held.append(lax.ppermute(pieces[(me + shift) % mass_count], 'mass', perm))  6.02 us
  transfers between devices with their start and end apart: 7, of which 6 were waited for; matrix products, arithmetic and copies ran while one was open for 1% of the time, Pallas kernels for 0%

profile of v5, /device:TPU:1, one launch (start us, length us, event | category | flops | bytes accessed | tf_op | source)
XLA Modules:
  0.0 233.2 jit_solution(3197682480672462925)
XLA Ops:
  7.2 0.0 all-gather.2.cloned.1.call-start
  7.3 1.4 fusion
  8.7 0.7 fusion.5
  9.5 0.1 reduce_window_sum.11
  9.6 0.8 select_reduce_fusion.1
  10.5 0.7 multiply_add_fusion
  11.1 0.6 convolution_convert_fusion
  11.8 0.1 constant_dynamic-slice_fusion.4
  11.9 3.4 %collective-permute-start.2 = (bf16[48,4096]{1,0:T(8,128)(2,1)S(1)}, bf16[48,4096]{1,0:T(8,128)(2,1)S(1)}, u32[]{:S(2)}, u32[]{:S(2)}) collective-permute-start(bf16[48,4096]{1,0:T(8,128)(2,1)S(1)} %get-tuple-element.3), channel_id=1, source_target_pairs={{0,96},{32,0},{64,32},{96,64},{1,97},{33,1},{65,33},{97,65},{2,98}... | collective-permute-start | bytes 1179656 | tf_op jit(solution)/shard_map/ppermute | solution.py:60
  15.3 0.5 collective-permute-start.1
  15.8 0.6 collective-permute-start
  16.4 7.8 %collective-permute-done.2 = bf16[48,4096]{1,0:T(8,128)(2,1)S(1)} collective-permute-done((bf16[48,4096]{1,0:T(8,128)(2,1)S(1)}, bf16[48,4096]{1,0:T(8,128)(2,1)S(1)}, u32[]{:S(2)}, u32[]{:S(2)}) %collective-permute-start.2) | collective-permute-done | bytes 393248 | tf_op jit(solution)/shard_map/ppermute | solution.py:60
  24.2 2.3 %collective-permute-done.1 = bf16[48,4096]{1,0:T(8,128)(2,1)S(1)} collective-permute-done((bf16[48,4096]{1,0:T(8,128)(2,1)S(1)}, bf16[48,4096]{1,0:T(8,128)(2,1)S(1)}, u32[]{:S(2)}, u32[]{:S(2)}) %collective-permute-start.1) | collective-permute-done | bytes 393248 | tf_op jit(solution)/shard_map/ppermute | solution.py:60
  26.5 9.7 %collective-permute-done = bf16[48,4096]{1,0:T(8,128)(2,1)S(1)} collective-permute-done((bf16[48,4096]{1,0:T(8,128)(2,1)S(1)}, bf16[48,4096]{1,0:T(8,128)(2,1)S(1)}, u32[]{:S(2)}, u32[]{:S(2)}) %collective-permute-start) | collective-permute-done | bytes 393248 | tf_op jit(solution)/shard_map/ppermute | solution.py:60
  36.2 0.2 pad_maximum_fusion
  36.4 1.8 gather_fusion
  38.2 0.0 all-gather.2.cloned.1.call-update
  38.3 0.1 select_reduce_fusion
  38.4 0.1 reshape.89
  38.5 0.1 collective-permute-start.5
  38.6 0.6 collective-permute-start.4
  39.2 0.9 collective-permute-start.3
  40.0 0.6 dynamic-slice
  41.3 1.3 collective-permute-done.4
  42.6 0.8 collective-permute-done.3
  43.4 0.6 gather_fusion.1
  43.9 0.1 reshape.107
  44.0 0.2 dynamic-update-slice
  44.3 130.2 %all-reduce = s32[6144]{0:T(1024)S(1)} all-reduce(s32[6144]{0:T(1024)S(1)} %dynamic-update-slice), channel_id=1, replica_groups=mesh['mass'=4,'tile'=32] {'tile'}, use_global_device_ids=true, to_apply=%add | all-reduce | flops 6144 | bytes 49152
  174.5 0.7 compare_convert_fusion.oh_ref
  175.2 22.1 %all-gather.2.cloned.1.call-done.p_ref = bf16[6144,4096]{1,0:T(8,128)(2,1)} async-done(((bf16[192,4096]{1,0:T(8,128)(2,1)}), bf16[6144,4096]{1,0:T(8,128)(2,1)}) %all-gather.2.cloned.1.call-update) | async-done | bytes 50331664 | tf_op jit(solution)/shard_map/all_gather | solution.py:94
  197.3 29.1 %shard_map.50 = (f32[192,6144]{1,0:T(8,128)}, f32[4,4096]{1,0:T(4,128)}) custom-call(bf16[192,4096]{1,0:T(8,128)(2,1)} %bitcast.27, bf16[4,6144]{1,0:T(4,128)(2,1)} %compare_convert_fusion.oh_ref, bf16[6144,4096]{1,0:T(8,128)(2,1)} %all-gather.2.cloned.1.call-done.p_ref), custom_call_target="tpu_custom_call" | custom-call | flops 9865003008 | bytes 56737792 | tf_op jit(solution)/shard_map/pallas_call | solution.py:34
  (12 shorter events, 0.1 us)
Async XLA Ops:
  7.2 4.0 %copy-start = (bf16[96,4096]{1,0:T(8,128)(2,1)S(1)}, bf16[96,4096]{1,0:T(8,128)(2,1)}, u32[]{:S(2)}) copy-start(bf16[96,4096]{1,0:T(8,128)(2,1)} %param.3) | copy-start | bytes 2359300
  7.2 190.1 %all-gather.2.cloned.1.call-start = ((), (), s32[]{:S(2)}) async-start(), calls=%async_computation | async-start | bytes 51904512 | tf_op jit(solution)/shard_map/all_gather | solution.py:94
  11.9 12.3 %collective-permute-start.2 = (bf16[48,4096]{1,0:T(8,128)(2,1)S(1)}, bf16[48,4096]{1,0:T(8,128)(2,1)S(1)}, u32[]{:S(2)}, u32[]{:S(2)}) collective-permute-start(bf16[48,4096]{1,0:T(8,128)(2,1)S(1)} %get-tuple-element.3), channel_id=1, source_target_pairs={{0,96},{32,0},{64,32},{96,64},{1,97},{33,1},{65,33},{97,65},{2,98}... | collective-permute-start | bytes 1179656 | tf_op jit(solution)/shard_map/ppermute | solution.py:60
  15.3 11.3 %collective-permute-start.1 = (bf16[48,4096]{1,0:T(8,128)(2,1)S(1)}, bf16[48,4096]{1,0:T(8,128)(2,1)S(1)}, u32[]{:S(2)}, u32[]{:S(2)}) collective-permute-start(bf16[48,4096]{1,0:T(8,128)(2,1)S(1)} %get-tuple-element.4), channel_id=1, source_target_pairs={{0,64},{32,96},{64,0},{96,32},{1,65},{33,97},{65,1},{97,33},{2,66}... | collective-permute-start | bytes 1179656 | tf_op jit(solution)/shard_map/ppermute | solution.py:60
  15.8 20.4 %collective-permute-start = (bf16[48,4096]{1,0:T(8,128)(2,1)S(1)}, bf16[48,4096]{1,0:T(8,128)(2,1)S(1)}, u32[]{:S(2)}, u32[]{:S(2)}) collective-permute-start(bf16[48,4096]{1,0:T(8,128)(2,1)S(1)} %get-tuple-element.5), channel_id=1, source_target_pairs={{0,32},{32,64},{64,96},{96,0},{1,33},{33,65},{65,97},{97,1},{2,34}... | collective-permute-start | bytes 1179656 | tf_op jit(solution)/shard_map/ppermute | solution.py:60
  38.2 1.8 copy-start.1
  38.5 2.8 %collective-permute-start.5 = (s32[48]{0:T(128)S(1)}, s32[48]{0:T(128)S(1)}, u32[]{:S(2)}, u32[]{:S(2)}) collective-permute-start(s32[48]{0:T(128)S(1)} %get-tuple-element.7), channel_id=1, source_target_pairs={{0,96},{32,0},{64,32},{96,64},{1,97},{33,1},{65,33},{97,65},{2,98}... | collective-permute-start | bytes 584 | tf_op jit(solution)/shard_map/ppermute | solution.py:60
  38.6 4.0 %collective-permute-start.4 = (s32[48]{0:T(128)S(1)}, s32[48]{0:T(128)S(1)}, u32[]{:S(2)}, u32[]{:S(2)}) collective-permute-start(s32[48]{0:T(128)S(1)} %get-tuple-element.8), channel_id=1, source_target_pairs={{0,64},{32,96},{64,0},{96,32},{1,65},{33,97},{65,1},{97,33},{2,66}... | collective-permute-start | bytes 584 | tf_op jit(solution)/shard_map/ppermute | solution.py:60
  39.2 4.2 %collective-permute-start.3 = (s32[48]{0:T(128)S(1)}, s32[48]{0:T(128)S(1)}, u32[]{:S(2)}, u32[]{:S(2)}) collective-permute-start(s32[48]{0:T(128)S(1)} %get-tuple-element.9), channel_id=1, source_target_pairs={{0,32},{32,64},{64,96},{96,0},{1,33},{33,65},{65,97},{97,1},{2,34}... | collective-permute-start | bytes 584 | tf_op jit(solution)/shard_map/ppermute | solution.py:60
Sparse Core Ops, SparseCore 0:
  38.4 158.8 all-gather.1

commit v6 on v5

--- a/solution.py
+++ b/solution.py
@@ -54,11 +54,16 @@
 
 def exchange_over_mass(pieces, mass_count):
     me = lax.axis_index("mass")
-    held = [pieces[me]]
-    for shift in range(1, mass_count):
-        perm = [(i, (i + shift) % mass_count) for i in range(mass_count)]
-        held.append(lax.ppermute(pieces[(me + shift) % mass_count], "mass", perm))
-    stacked = jnp.stack(held)
+    ahead = [(i, (i + 1) % mass_count) for i in range(mass_count)]
+    behind = [(i, (i - 1) % mass_count) for i in range(mass_count)]
+    from_behind = lax.ppermute(pieces[(me + 1) % mass_count], "mass", ahead)
+    from_ahead = lax.ppermute(pieces[(me - 1) % mass_count], "mass", behind)
+    far = pieces[(me + 2) % mass_count]
+    half = far.shape[0] // 2
+    first = lax.ppermute(lax.ppermute(far[:half], "mass", ahead), "mass", ahead)
+    second = lax.ppermute(lax.ppermute(far[half:], "mass", behind), "mass", behind)
+    opposite = jnp.concatenate([first, second], axis=0)
+    stacked = jnp.stack([pieces[me], from_behind, opposite, from_ahead])
     return stacked[(me - jnp.arange(mass_count)) % mass_count]
 
 

time: 233 us -> 233 us (level)
  waiting for transfers between devices: 44.1 us -> 34.5 us
  starting transfers between devices: 6.06 us -> 14.6 us
    ppermute x6 -> x12, starting transfers between devices: 6.02 us -> 14.5 us  [the longest x2 5.06 us: exchange_over_mass(): lax.ppermute(lax.ppermute(far[half:], 'mass', behind), 'mass', behind)]
    ppermute x6 -> x12, waiting for transfers between devices: 21.9 us -> 13.4 us  [the longest x4 12.7 us: exchange_over_mass(): first = lax.ppermute(lax.ppermute(far[:half], 'mass', ahead), 'mass', ahead)]
  transfers between devices with their start and end apart: 7 -> 13, of which waited for: 6 -> 5; matrix products, arithmetic and copies ran while one was open for 1% -> 1% of each run, Pallas kernels for 0% -> 0%
where the time goes in v6:
time: 233 us
  blocking collectives  130 us (56%)
  waiting for transfers between devices  34.5 us (15%)
  Pallas kernels  29.1 us (12%)
  between operations  14.8 us (6%)
  starting transfers between devices  14.6 us (6%)
  other arithmetic  4.99 us (2%)
  local copies, waits for them, and re-layouts  3.56 us (2%)
    unnamed x1, blocking collectives  130 us
    pallas_call x1, Pallas kernels, gram_consensus(): pl.pallas_call(functools.partial(_gram_consensus_kernel, 1.0 / bins), gri...  29.1 us
    all_gather x1, waiting for transfers between devices, shards(): gathered = lax.all_gather(arrived, 'tile', axis=0, tiled=True)  21 us
    ppermute x4, waiting for transfers between devices, exchange_over_mass(): first = lax.ppermute(lax.ppermute(far[:half], 'mass', ahead), 'mass', ahead)  12.7 us
    ppermute x2, starting transfers between devices, exchange_over_mass(): lax.ppermute(lax.ppermute(far[half:], 'mass', behind), 'mass', behind)  5.06 us
  transfers between devices with their start and end apart: 13, of which 5 were waited for; matrix products, arithmetic and copies ran while one was open for 1% of the time, Pallas kernels for 0%

profile of v6, /device:TPU:1, one launch (start us, length us, event | category | flops | bytes accessed | tf_op | source)
XLA Modules:
  0.0 232.5 jit_solution(1404697789368569646)
XLA Ops:
  7.2 1.4 fusion
  8.7 0.7 fusion.5
  9.4 0.1 reduce_window_sum.11
  9.6 0.8 select_reduce_fusion.1
  10.4 0.7 multiply_add_fusion
  11.1 0.6 convolution_convert_fusion
  11.8 2.1 collective-permute-start.1
  13.9 1.3 collective-permute-start.3
  15.2 0.1 constant_dynamic-slice_fusion.4
  15.4 1.5 collective-permute-start.5
  16.9 2.5 %collective-permute-done.1 = bf16[24,4096]{1,0:T(8,128)(2,1)S(1)} collective-permute-done((bf16[24,4096]{1,0:T(8,128)(2,1)S(1)}, bf16[24,4096]{1,0:T(8,128)(2,1)S(1)}, u32[]{:S(2)}, u32[]{:S(2)}) %collective-permute-start.1) | collective-permute-done | bytes 196640 | tf_op jit(solution)/shard_map/ppermute | solution.py:63
  19.4 0.3 collective-permute-start.2
  19.7 2.4 %collective-permute-start.4 = (bf16[24,4096]{1,0:T(8,128)(2,1)S(1)}, bf16[24,4096]{1,0:T(8,128)(2,1)S(1)}, u32[]{:S(2)}, u32[]{:S(2)}) collective-permute-start(bf16[24,4096]{1,0:T(8,128)(2,1)S(1)} %collective-permute-done.3), channel_id=1, source_target_pairs={{0,96},{32,0},{64,32},{96,64},{1,97},{33,1},{65,33},{97,65},{2,98}... | collective-permute-start | bytes 589832 | tf_op jit(solution)/shard_map/ppermute | solution.py:64
  22.1 9.3 %collective-permute-done.2 = bf16[24,4096]{1,0:T(8,128)(2,1)S(1)} collective-permute-done((bf16[24,4096]{1,0:T(8,128)(2,1)S(1)}, bf16[24,4096]{1,0:T(8,128)(2,1)S(1)}, u32[]{:S(2)}, u32[]{:S(2)}) %collective-permute-start.2) | collective-permute-done | bytes 196640 | tf_op jit(solution)/shard_map/ppermute | solution.py:63
  31.4 0.6 collective-permute-done.4
  32.1 0.2 pad_maximum_fusion
  32.3 1.8 gather_fusion
  34.1 0.1 select_reduce_fusion
  34.4 1.2 collective-permute-start.7
  35.6 1.5 collective-permute-start.9
  37.1 1.3 collective-permute-start.11
  38.4 0.1 collective-permute-start.6
  38.5 0.6 dynamic-slice
  39.9 2.7 %collective-permute-start.10 = (s32[24]{0:T(128)S(1)}, s32[24]{0:T(128)S(1)}, u32[]{:S(2)}, u32[]{:S(2)}) collective-permute-start(s32[24]{0:T(128)S(1)} %collective-permute-done.9), channel_id=1, source_target_pairs={{0,96},{32,0},{64,32},{96,64},{1,97},{33,1},{65,33},{97,65},{2,98}... | collective-permute-start | bytes 296 | tf_op jit(solution)/shard_map/ppermute | solution.py:64
  42.5 0.9 collective-permute-done.8
  43.6 0.6 gather_fusion.1
  44.2 0.1 reshape.111
  44.2 0.2 dynamic-update-slice
  44.5 130.4 %all-reduce = s32[6144]{0:T(1024)S(1)} all-reduce(s32[6144]{0:T(1024)S(1)} %dynamic-update-slice), channel_id=1, replica_groups=mesh['mass'=4,'tile'=32] {'tile'}, use_global_device_ids=true, to_apply=%add | all-reduce | flops 6144 | bytes 49152
  174.9 0.7 compare_convert_fusion.oh_ref
  175.6 21.0 %all-gather.2.cloned.1.call-done.p_ref = bf16[6144,4096]{1,0:T(8,128)(2,1)} async-done(((bf16[192,4096]{1,0:T(8,128)(2,1)}), bf16[6144,4096]{1,0:T(8,128)(2,1)}) %all-gather.2.cloned.1.call-update) | async-done | bytes 50331664 | tf_op jit(solution)/shard_map/all_gather | solution.py:99
  196.6 29.1 %shard_map.50 = (f32[192,6144]{1,0:T(8,128)}, f32[4,4096]{1,0:T(4,128)}) custom-call(bf16[192,4096]{1,0:T(8,128)(2,1)} %bitcast.33, bf16[4,6144]{1,0:T(4,128)(2,1)} %compare_convert_fusion.oh_ref, bf16[6144,4096]{1,0:T(8,128)(2,1)} %all-gather.2.cloned.1.call-done.p_ref), custom_call_target="tpu_custom_call" | custom-call | flops 9865003008 | bytes 56737792 | tf_op jit(solution)/shard_map/pallas_call | solution.py:34
  (28 shorter events, 0.6 us)
Async XLA Ops:
  7.2 4.0 %copy-start = (bf16[96,4096]{1,0:T(8,128)(2,1)S(1)}, bf16[96,4096]{1,0:T(8,128)(2,1)}, u32[]{:S(2)}) copy-start(bf16[96,4096]{1,0:T(8,128)(2,1)} %param.3) | copy-start | bytes 2359300
  7.2 189.5 %all-gather.2.cloned.1.call-start = ((), (), s32[]{:S(2)}) async-start(), calls=%async_computation | async-start | bytes 51904512 | tf_op jit(solution)/shard_map/all_gather | solution.py:99
  11.8 7.6 %collective-permute-start.1 = (bf16[24,4096]{1,0:T(8,128)(2,1)S(1)}, bf16[24,4096]{1,0:T(8,128)(2,1)S(1)}, u32[]{:S(2)}, u32[]{:S(2)}) collective-permute-start(bf16[24,4096]{1,0:T(8,128)(2,1)S(1)} %get-tuple-element.5), channel_id=1, source_target_pairs={{0,32},{32,64},{64,96},{96,0},{1,33},{33,65},{65,97},{97,1},{2,34}... | collective-permute-start | bytes 589832 | tf_op jit(solution)/shard_map/ppermute | solution.py:63
  13.9 5.8 %collective-permute-start.3 = (bf16[24,4096]{1,0:T(8,128)(2,1)S(1)}, bf16[24,4096]{1,0:T(8,128)(2,1)S(1)}, u32[]{:S(2)}, u32[]{:S(2)}) collective-permute-start(bf16[24,4096]{1,0:T(8,128)(2,1)S(1)} %get-tuple-element.6), channel_id=1, source_target_pairs={{0,96},{32,0},{64,32},{96,64},{1,97},{33,1},{65,33},{97,65},{2,98}... | collective-permute-start | bytes 589832 | tf_op jit(solution)/shard_map/ppermute | solution.py:64
  15.4 16.7 %collective-permute-start.5 = (bf16[48,4096]{1,0:T(8,128)(2,1)S(1)}, bf16[48,4096]{1,0:T(8,128)(2,1)S(1)}, u32[]{:S(2)}, u32[]{:S(2)}) collective-permute-start(bf16[48,4096]{1,0:T(8,128)(2,1)S(1)} %get-tuple-element.3), channel_id=1, source_target_pairs={{0,96},{32,0},{64,32},{96,64},{1,97},{33,1},{65,33},{97,65},{2,98}... | collective-permute-start | bytes 1179656 | tf_op jit(solution)/shard_map/ppermute | solution.py:60
  16.8 15.3 %collective-permute-start = (bf16[48,4096]{1,0:T(8,128)(2,1)S(1)}, bf16[48,4096]{1,0:T(8,128)(2,1)S(1)}, u32[]{:S(2)}, u32[]{:S(2)}) collective-permute-start(bf16[48,4096]{1,0:T(8,128)(2,1)S(1)} %get-tuple-element.4), channel_id=1, source_target_pairs={{0,32},{32,64},{64,96},{96,0},{1,33},{33,65},{65,97},{97,1},{2,34}... | collective-permute-start | bytes 1179656 | tf_op jit(solution)/shard_map/ppermute | solution.py:59
  19.4 12.0 %collective-permute-start.2 = (bf16[24,4096]{1,0:T(8,128)(2,1)S(1)}, bf16[24,4096]{1,0:T(8,128)(2,1)S(1)}, u32[]{:S(2)}, u32[]{:S(2)}) collective-permute-start(bf16[24,4096]{1,0:T(8,128)(2,1)S(1)} %collective-permute-done.1), channel_id=1, source_target_pairs={{0,32},{32,64},{64,96},{96,0},{1,33},{33,65},{65,97},{97,1},{2,34}... | collective-permute-start | bytes 589832 | tf_op jit(solution)/shard_map/ppermute | solution.py:63
  19.7 12.4 %collective-permute-start.4 = (bf16[24,4096]{1,0:T(8,128)(2,1)S(1)}, bf16[24,4096]{1,0:T(8,128)(2,1)S(1)}, u32[]{:S(2)}, u32[]{:S(2)}) collective-permute-start(bf16[24,4096]{1,0:T(8,128)(2,1)S(1)} %collective-permute-done.3), channel_id=1, source_target_pairs={{0,96},{32,0},{64,32},{96,64},{1,97},{33,1},{65,33},{97,65},{2,98}... | collective-permute-start | bytes 589832 | tf_op jit(solution)/shard_map/ppermute | solution.py:64
  34.1 4.5 %copy-start.1 = (u32[128]{0:T(128)S(1)}, u32[128]{0:T(128)}, u32[]{:S(2)}) copy-start(u32[128]{0:T(128)} %constant.80) | copy-start | bytes 1540
  34.4 5.4 %collective-permute-start.7 = (s32[24]{0:T(128)S(1)}, s32[24]{0:T(128)S(1)}, u32[]{:S(2)}, u32[]{:S(2)}) collective-permute-start(s32[24]{0:T(128)S(1)} %get-tuple-element.11), channel_id=1, source_target_pairs={{0,32},{32,64},{64,96},{96,0},{1,33},{33,65},{65,97},{97,1},{2,34}... | collective-permute-start | bytes 296 | tf_op jit(solution)/shard_map/ppermute | solution.py:63
  35.6 4.3 %collective-permute-start.9 = (s32[24]{0:T(128)S(1)}, s32[24]{0:T(128)S(1)}, u32[]{:S(2)}, u32[]{:S(2)}) collective-permute-start(s32[24]{0:T(128)S(1)} %get-tuple-element.12), channel_id=1, source_target_pairs={{0,96},{32,0},{64,32},{96,64},{1,97},{33,1},{65,33},{97,65},{2,98}... | collective-permute-start | bytes 296 | tf_op jit(solution)/shard_map/ppermute | solution.py:64
  37.1 6.5 %collective-permute-start.11 = (s32[48]{0:T(128)S(1)}, s32[48]{0:T(128)S(1)}, u32[]{:S(2)}, u32[]{:S(2)}) collective-permute-start(s32[48]{0:T(128)S(1)} %get-tuple-element.8), channel_id=1, source_target_pairs={{0,96},{32,0},{64,32},{96,64},{1,97},{33,1},{65,33},{97,65},{2,98}... | collective-permute-start | bytes 584 | tf_op jit(solution)/shard_map/ppermute | solution.py:60
  38.4 5.2 %collective-permute-start.6 = (s32[48]{0:T(128)S(1)}, s32[48]{0:T(128)S(1)}, u32[]{:S(2)}, u32[]{:S(2)}) collective-permute-start(s32[48]{0:T(128)S(1)} %get-tuple-element.10), channel_id=1, source_target_pairs={{0,32},{32,64},{64,96},{96,0},{1,33},{33,65},{65,97},{97,1},{2,34}... | collective-permute-start | bytes 584 | tf_op jit(solution)/shard_map/ppermute | solution.py:59
  39.8 3.7 %collective-permute-start.8 = (s32[24]{0:T(128)S(1)}, s32[24]{0:T(128)S(1)}, u32[]{:S(2)}, u32[]{:S(2)}) collective-permute-start(s32[24]{0:T(128)S(1)} %collective-permute-done.7), channel_id=1, source_target_pairs={{0,32},{32,64},{64,96},{96,0},{1,33},{33,65},{65,97},{97,1},{2,34}... | collective-permute-start | bytes 296 | tf_op jit(solution)/shard_map/ppermute | solution.py:63
  39.9 3.6 %collective-permute-start.10 = (s32[24]{0:T(128)S(1)}, s32[24]{0:T(128)S(1)}, u32[]{:S(2)}, u32[]{:S(2)}) collective-permute-start(s32[24]{0:T(128)S(1)} %collective-permute-done.9), channel_id=1, source_target_pairs={{0,96},{32,0},{64,32},{96,64},{1,97},{33,1},{65,33},{97,65},{2,98}... | collective-permute-start | bytes 296 | tf_op jit(solution)/shard_map/ppermute | solution.py:64
Sparse Core Ops, SparseCore 0:
  34.2 162.3 all-gather.1

commit v7 on v6

--- a/solution.py
+++ b/solution.py
@@ -8,14 +8,15 @@
 from jax.sharding import PartitionSpec as P
 
 CL_DEV = 4
-ONE_HOT_ROWS = 4
 
-def _gram_consensus_kernel(scale, a_ref, oh_ref, p_ref, g_ref, c_ref):
+def _gram_consensus_kernel(scale, rows, half_ref, a_ref, oh_ref, p_ref, mine_ref, theirs_ref, c_ref):
     j = pl.program_id(0)
     blk = p_ref[...]
-    g_ref[...] = lax.dot_general(
+    res = lax.dot_general(
         a_ref[...], blk, (((1,), (1,)), ((), ())), preferred_element_type=jnp.float32
     ) * scale
+    mine_ref[...] = res[:rows]
+    theirs_ref[...] = res[rows:]
 
     @pl.when(j == 0)
     def _():
@@ -24,32 +25,41 @@
     c_ref[...] += jnp.dot(oh_ref[...], blk, preferred_element_type=jnp.float32)
 
 
-def gram_consensus(arrived, one_hot, gathered, block_rows=1024):
-    rows, bins = arrived.shape
+def gram_consensus(half, pair_rows, one_hot, gathered, block_rows=1024):
+    rows = pair_rows.shape[0] // 2
+    bins = pair_rows.shape[1]
     total = gathered.shape[0]
     heads = one_hot.shape[0]
-    steps = total // block_rows
-    flops = 2 * rows * total * bins + 2 * heads * total * bins
-    bytes_accessed = 2 * (rows * bins + heads * total + total * bins) + 4 * (rows * total + heads * bins)
-    return pl.pallas_call(
-        functools.partial(_gram_consensus_kernel, 1.0 / bins),
+    steps = total // 2 // block_rows
+    flops = 2 * 2 * rows * (total // 2) * bins + 2 * heads * (total // 2) * bins
+    bytes_accessed = 2 * (2 * rows * bins + heads * total // 2 + total // 2 * bins) + 4 * (
+        2 * rows * total // 2 + heads * bins
+    )
+    grid_spec = pltpu.PrefetchScalarGridSpec(
+        num_scalar_prefetch=1,
         grid=(steps,),
         in_specs=[
-            pl.BlockSpec((rows, bins), lambda j: (0, 0)),
-            pl.BlockSpec((heads, block_rows), lambda j: (0, j)),
-            pl.BlockSpec((block_rows, bins), lambda j: (j, 0)),
+            pl.BlockSpec((2 * rows, bins), lambda j, h: (0, 0)),
+            pl.BlockSpec((heads, block_rows), lambda j, h: (0, h[0] * steps + j)),
+            pl.BlockSpec((block_rows, bins), lambda j, h: (h[0] * steps + j, 0)),
         ],
         out_specs=[
-            pl.BlockSpec((rows, block_rows), lambda j: (0, j)),
-            pl.BlockSpec((heads, bins), lambda j: (0, 0)),
+            pl.BlockSpec((rows, block_rows), lambda j, h: (0, h[0] * steps + j)),
+            pl.BlockSpec((rows, block_rows), lambda j, h: (0, j)),
+            pl.BlockSpec((heads, bins), lambda j, h: (0, 0)),
         ],
+    )
+    return pl.pallas_call(
+        functools.partial(_gram_consensus_kernel, 1.0 / bins, rows),
+        grid_spec=grid_spec,
         out_shape=[
             jax.ShapeDtypeStruct((rows, total), jnp.float32),
+            jax.ShapeDtypeStruct((rows, total // 2), jnp.float32),
             jax.ShapeDtypeStruct((heads, bins), jnp.float32),
         ],
         compiler_params=pltpu.CompilerParams(dimension_semantics=("arbitrary",)),
         cost_estimate=pl.CostEstimate(flops=flops, bytes_accessed=bytes_accessed, transcendentals=0),
-    )(arrived, one_hot, gathered)
+    )(half, pair_rows, one_hot, gathered)
 
 
 def exchange_over_mass(pieces, mass_count):
@@ -98,13 +108,22 @@
     arrived_labels = arrived_labels.reshape(slot_count)
     gathered = lax.all_gather(arrived, "tile", axis=0, tiled=True)
     gathered_labels = lax.all_gather(arrived_labels, "tile", axis=0, tiled=True)
+    tile = lax.axis_index("tile")
+    swap = [(i, i ^ 1) for i in range(tile_count)]
+    half = tile % 2
+    partner_rows = lax.ppermute(arrived, "tile", swap)
+    pair_rows = jnp.concatenate([arrived, partner_rows], axis=0)
+    owners = jnp.where(jnp.arange(2 * CL_DEV) < CL_DEV, tile, tile ^ 1)
     own_ids = (
         lax.axis_index("mass") * per_window
-        + lax.axis_index("tile") * CL_DEV
-        + jnp.arange(ONE_HOT_ROWS, dtype=jnp.int32)
+        + owners * CL_DEV
+        + jnp.arange(2 * CL_DEV, dtype=jnp.int32) % CL_DEV
     )
     one_hot = (own_ids[:, None] == gathered_labels[None, :]).astype(jnp.bfloat16)
-    gram_tiles, consensus = gram_consensus(arrived, one_hot, gathered)
+    mine, theirs, sums = gram_consensus(half.reshape(1), pair_rows, one_hot, gathered)
+    returned = lax.ppermute(theirs, "tile", swap)
+    gram_tiles = lax.dynamic_update_slice(mine, returned, (0, (1 - half) * theirs.shape[1]))
+    consensus = sums[:CL_DEV] + lax.ppermute(sums[CL_DEV:], "tile", swap)
     return (gram_tiles, consensus)
 
 

time: 233 us -> 231 us (level)
  Pallas kernels: 29.1 us -> 18.9 us
  starting transfers between devices: 14.6 us -> 19.6 us
  other arithmetic: 4.99 us -> 8.46 us
  waiting for transfers between devices: 34.5 us -> 31.4 us
  local copies, waits for them, and re-layouts: 3.56 us -> 6.02 us
    pallas_call x1, Pallas kernels: 29.1 us -> 18.9 us  [gram_consensus(): pl.pallas_call(functools.partial(_gram_consensus_kernel, 1.0 / bins, rows...]
    all_gather x1, waiting for transfers between devices: 21 us -> 16.4 us  [shards(): gathered = lax.all_gather(arrived, 'tile', axis=0, tiled=True)]
    ppermute x0 -> x3, starting transfers between devices: none -> 3.91 us  [the longest x1 3.24 us: shards(): partner_rows = lax.ppermute(arrived, 'tile', swap)]
    ppermute x0 -> x3, waiting for transfers between devices: none -> 3.33 us  [the longest x1 3.33 us: shards(): consensus = sums[:CL_DEV] + lax.ppermute(sums[CL_DEV:], 'tile', swap)]
    ppermute x2, starting transfers between devices: 2.8 us -> 5.17 us  [exchange_over_mass(): from_ahead = lax.ppermute(pieces[(me - 1) % mass_count], 'mass', behind)]
  transfers between devices with their start and end apart: 13 -> 16, of which waited for: 5 -> 5; matrix products, arithmetic and copies ran while one was open for 1% -> 3% of each run, Pallas kernels for 0% -> 0%
where the time goes in v7:
time: 231 us; the launch traced here: 230 us
  blocking collectives  131 us (57%)
  waiting for transfers between devices  31.4 us (14%)
  starting transfers between devices  19.6 us (8%)
  Pallas kernels  18.9 us (8%)
  between operations  14.9 us (6%)
  other arithmetic  8.46 us (4%)
  local copies, waits for them, and re-layouts  6.02 us (3%)
    unnamed x1, blocking collectives  131 us
    pallas_call x1, Pallas kernels, gram_consensus(): pl.pallas_call(functools.partial(_gram_consensus_kernel, 1.0 / bins, rows...  18.9 us
    all_gather x1, waiting for transfers between devices, shards(): gathered = lax.all_gather(arrived, 'tile', axis=0, tiled=True)  16.4 us
    ppermute x4, waiting for transfers between devices, exchange_over_mass(): first = lax.ppermute(lax.ppermute(far[:half], 'mass', ahead), 'mass', ahead)  11.6 us
    ppermute x2, starting transfers between devices, exchange_over_mass(): from_ahead = lax.ppermute(pieces[(me - 1) % mass_count], 'mass', behind)  5.17 us
  transfers between devices with their start and end apart: 16, of which 5 were waited for; matrix products, arithmetic and copies ran while one was open for 3% of the time, Pallas kernels for 0%

profile of v7, /device:TPU:1, one launch (start us, length us, event | category | flops | bytes accessed | tf_op | source)
XLA Modules:
  0.0 230.5 jit_solution(10673383053975226394)
XLA Ops:
  7.2 0.8 fusion.5
  8.2 0.8 select_reduce_fusion.1
  9.0 1.4 fusion
  10.4 0.7 multiply_add_fusion
  11.1 0.6 convolution_convert_fusion
  11.8 2.1 collective-permute-start.1
  13.9 1.3 collective-permute-start.3
  15.5 2.6 %collective-permute-start.5 = (bf16[48,4096]{1,0:T(8,128)(2,1)S(1)}, bf16[48,4096]{1,0:T(8,128)(2,1)S(1)}, u32[]{:S(2)}, u32[]{:S(2)}) collective-permute-start(bf16[48,4096]{1,0:T(8,128)(2,1)S(1)} %get-tuple-element.9), channel_id=1, source_target_pairs={{0,96},{32,0},{64,32},{96,64},{1,97},{33,1},{65,33},{97,65},{2,98}... | collective-permute-start | bytes 1179656 | tf_op jit(solution)/shard_map/ppermute | solution.py:70
  18.1 1.3 collective-permute-done.1
  19.4 0.3 collective-permute-start.2
  19.7 2.4 %collective-permute-start.4 = (bf16[24,4096]{1,0:T(8,128)(2,1)S(1)}, bf16[24,4096]{1,0:T(8,128)(2,1)S(1)}, u32[]{:S(2)}, u32[]{:S(2)}) collective-permute-start(bf16[24,4096]{1,0:T(8,128)(2,1)S(1)} %collective-permute-done.3), channel_id=1, source_target_pairs={{0,96},{32,0},{64,32},{96,64},{1,97},{33,1},{65,33},{97,65},{2,98}... | collective-permute-start | bytes 589832 | tf_op jit(solution)/shard_map/ppermute | solution.py:74
  22.1 9.9 %collective-permute-done.2 = bf16[24,4096]{1,0:T(8,128)(2,1)S(1)} collective-permute-done((bf16[24,4096]{1,0:T(8,128)(2,1)S(1)}, bf16[24,4096]{1,0:T(8,128)(2,1)S(1)}, u32[]{:S(2)}, u32[]{:S(2)}) %collective-permute-start.2) | collective-permute-done | bytes 196640 | tf_op jit(solution)/shard_map/ppermute | solution.py:73
  32.3 1.8 gather_fusion
  34.4 2.6 %collective-permute-start.10 = (s32[24]{0:T(128)S(1)}, s32[24]{0:T(128)S(1)}, u32[]{:S(2)}, u32[]{:S(2)}) collective-permute-start(s32[24]{0:T(128)S(1)} %get-tuple-element.18), channel_id=1, source_target_pairs={{0,96},{32,0},{64,32},{96,64},{1,97},{33,1},{65,33},{97,65},{2,98}... | collective-permute-start | bytes 296 | tf_op jit(solution)/shard_map/ppermute | solution.py:74
  37.1 2.6 %collective-permute-start.12 = (s32[48]{0:T(128)S(1)}, s32[48]{0:T(128)S(1)}, u32[]{:S(2)}, u32[]{:S(2)}) collective-permute-start(s32[48]{0:T(128)S(1)} %get-tuple-element.14), channel_id=1, source_target_pairs={{0,96},{32,0},{64,32},{96,64},{1,97},{33,1},{65,33},{97,65},{2,98}... | collective-permute-start | bytes 584 | tf_op jit(solution)/shard_map/ppermute | solution.py:70
  39.7 0.6 dynamic-slice
  41.0 1.5 collective-permute-start.11
  42.5 3.2 %collective-permute-start.6 = (bf16[192,4096]{1,0:T(8,128)(2,1)S(1)}, bf16[192,4096]{1,0:T(8,128)(2,1)S(1)}, u32[]{:S(2)}, u32[]{:S(2)}) collective-permute-start(bf16[192,4096]{1,0:T(8,128)(2,1)S(1)} %bitcast.34), channel_id=1, source_target_pairs={{0,1},{1,0},{2,3},{3,2},{4,5},{5,4},{6,7},{7,6},{8,9},{9,8},{10,11... | collective-permute-start | bytes 4718600 | tf_op jit(solution)/shard_map/ppermute | solution.py:114
  45.8 0.4 collective-permute-done.9
  46.2 0.6 gather_fusion.1
  46.9 0.2 dynamic-update-slice
  47.1 130.5 %all-reduce = s32[6144]{0:T(1024)S(1)} all-reduce(s32[6144]{0:T(1024)S(1)} %dynamic-update-slice), channel_id=1, replica_groups=mesh['mass'=4,'tile'=32] {'tile'}, use_global_device_ids=true, to_apply=%add | all-reduce | flops 6144 | bytes 49152
  177.7 0.7 compare_convert_fusion.oh_ref
  178.4 1.9 pad_maximum_fusion.a_ref
  180.3 16.4 %all-gather.2.cloned.1.call-done.p_ref = bf16[6144,4096]{1,0:T(8,128)(2,1)} async-done(((bf16[192,4096]{1,0:T(8,128)(2,1)}), bf16[6144,4096]{1,0:T(8,128)(2,1)}) %all-gather.2.cloned.1.call-update) | async-done | bytes 50331664 | tf_op jit(solution)/shard_map/all_gather | solution.py:109
  196.7 18.9 %shard_map.50 = (f32[192,6144]{1,0:T(8,128)}, f32[192,3072]{1,0:T(8,128)}, f32[8,4096]{1,0:T(8,128)}) custom-call(s32[1]{0:T(128)} %bitcast.half_ref, bf16[384,4096]{1,0:T(8,128)(2,1)} %pad_maximum_fusion.a_ref, bf16[8,6144]{1,0:T(8,128)(2,1)} %compare_convert_fusion.oh_ref, bf16[6144,4096]{1,0:T(8,128)(2,1)} %all-gather.2.cloned.1.call-done.p_ref), custom_call_target="tpu_custom_call" | custom-call | flops 9865003008 | bytes 33210368 | tf_op jit(solution)/shard_map/pallas_call | solution.py:52
  215.6 0.3 collective-permute-start.13
  215.9 0.9 slice.39
  216.9 0.3 collective-permute-start.14
  217.2 3.3 %collective-permute-done.14 = f32[4,4096]{1,0:T(4,128)S(1)} collective-permute-done((f32[4,4096]{1,0:T(4,128)S(1)}, f32[4,4096]{1,0:T(4,128)S(1)}, u32[]{:S(2)}, u32[]{:S(2)}) %collective-permute-start.14) | collective-permute-done | bytes 65568 | tf_op jit(solution)/shard_map/ppermute | solution.py:126
  220.5 1.5 slice_add_fusion
  222.1 1.6 constant_dynamic-update-slice_fusion
  (40 shorter events, 1.4 us)
Async XLA Ops:
  7.2 4.0 %copy-start.1 = (bf16[96,4096]{1,0:T(8,128)(2,1)S(1)}, bf16[96,4096]{1,0:T(8,128)(2,1)}, u32[]{:S(2)}) copy-start(bf16[96,4096]{1,0:T(8,128)(2,1)} %param.3) | copy-start | bytes 2359300
  7.2 189.5 %all-gather.2.cloned.1.call-start = ((), (), s32[]{:S(2)}) async-start(), calls=%async_computation | async-start | bytes 51904512 | tf_op jit(solution)/shard_map/all_gather | solution.py:109
  11.8 7.6 %collective-permute-start.1 = (bf16[24,4096]{1,0:T(8,128)(2,1)S(1)}, bf16[24,4096]{1,0:T(8,128)(2,1)S(1)}, u32[]{:S(2)}, u32[]{:S(2)}) collective-permute-start(bf16[24,4096]{1,0:T(8,128)(2,1)S(1)} %get-tuple-element.11), channel_id=1, source_target_pairs={{0,32},{32,64},{64,96},{96,0},{1,33},{33,65},{65,97},{97,1},{2,34}... | collective-permute-start | bytes 589832 | tf_op jit(solution)/shard_map/ppermute | solution.py:73
  13.9 5.8 %collective-permute-start.3 = (bf16[24,4096]{1,0:T(8,128)(2,1)S(1)}, bf16[24,4096]{1,0:T(8,128)(2,1)S(1)}, u32[]{:S(2)}, u32[]{:S(2)}) collective-permute-start(bf16[24,4096]{1,0:T(8,128)(2,1)S(1)} %get-tuple-element.12), channel_id=1, source_target_pairs={{0,96},{32,0},{64,32},{96,64},{1,97},{33,1},{65,33},{97,65},{2,98}... | collective-permute-start | bytes 589832 | tf_op jit(solution)/shard_map/ppermute | solution.py:74
  15.3 16.8 %collective-permute-start = (bf16[48,4096]{1,0:T(8,128)(2,1)S(1)}, bf16[48,4096]{1,0:T(8,128)(2,1)S(1)}, u32[]{:S(2)}, u32[]{:S(2)}) collective-permute-start(bf16[48,4096]{1,0:T(8,128)(2,1)S(1)} %get-tuple-element.10), channel_id=1, source_target_pairs={{0,32},{32,64},{64,96},{96,0},{1,33},{33,65},{65,97},{97,1},{2,34}... | collective-permute-start | bytes 1179656 | tf_op jit(solution)/shard_map/ppermute | solution.py:69
  15.5 16.6 %collective-permute-start.5 = (bf16[48,4096]{1,0:T(8,128)(2,1)S(1)}, bf16[48,4096]{1,0:T(8,128)(2,1)S(1)}, u32[]{:S(2)}, u32[]{:S(2)}) collective-permute-start(bf16[48,4096]{1,0:T(8,128)(2,1)S(1)} %get-tuple-element.9), channel_id=1, source_target_pairs={{0,96},{32,0},{64,32},{96,64},{1,97},{33,1},{65,33},{97,65},{2,98}... | collective-permute-start | bytes 1179656 | tf_op jit(solution)/shard_map/ppermute | solution.py:70
  19.4 12.6 %collective-permute-start.2 = (bf16[24,4096]{1,0:T(8,128)(2,1)S(1)}, bf16[24,4096]{1,0:T(8,128)(2,1)S(1)}, u32[]{:S(2)}, u32[]{:S(2)}) collective-permute-start(bf16[24,4096]{1,0:T(8,128)(2,1)S(1)} %collective-permute-done.1), channel_id=1, source_target_pairs={{0,32},{32,64},{64,96},{96,0},{1,33},{33,65},{65,97},{97,1},{2,34}... | collective-permute-start | bytes 589832 | tf_op jit(solution)/shard_map/ppermute | solution.py:73
  19.7 12.4 %collective-permute-start.4 = (bf16[24,4096]{1,0:T(8,128)(2,1)S(1)}, bf16[24,4096]{1,0:T(8,128)(2,1)S(1)}, u32[]{:S(2)}, u32[]{:S(2)}) collective-permute-start(bf16[24,4096]{1,0:T(8,128)(2,1)S(1)} %collective-permute-done.3), channel_id=1, source_target_pairs={{0,96},{32,0},{64,32},{96,64},{1,97},{33,1},{65,33},{97,65},{2,98}... | collective-permute-start | bytes 589832 | tf_op jit(solution)/shard_map/ppermute | solution.py:74
  34.1 5.6 %copy-start.2 = (u32[128]{0:T(128)S(1)}, u32[128]{0:T(128)}, u32[]{:S(2)}) copy-start(u32[128]{0:T(128)} %constant.101) | copy-start | bytes 1540
  34.1 8.4 %copy-start = (bf16[4,48,4096]{2,1,0:T(8,128)(2,1)S(1)}, bf16[4,48,4096]{2,1,0:T(8,128)(2,1)}, u32[]{:S(2)}) copy-start(bf16[4,48,4096]{2,1,0:T(8,128)(2,1)} %gather_fusion) | copy-start | bytes 4718596
  34.4 6.6 %collective-permute-start.10 = (s32[24]{0:T(128)S(1)}, s32[24]{0:T(128)S(1)}, u32[]{:S(2)}, u32[]{:S(2)}) collective-permute-start(s32[24]{0:T(128)S(1)} %get-tuple-element.18), channel_id=1, source_target_pairs={{0,96},{32,0},{64,32},{96,64},{1,97},{33,1},{65,33},{97,65},{2,98}... | collective-permute-start | bytes 296 | tf_op jit(solution)/shard_map/ppermute | solution.py:74
  37.0 5.5 %collective-permute-start.8 = (s32[24]{0:T(128)S(1)}, s32[24]{0:T(128)S(1)}, u32[]{:S(2)}, u32[]{:S(2)}) collective-permute-start(s32[24]{0:T(128)S(1)} %get-tuple-element.17), channel_id=1, source_target_pairs={{0,32},{32,64},{64,96},{96,0},{1,33},{33,65},{65,97},{97,1},{2,34}... | collective-permute-start | bytes 296 | tf_op jit(solution)/shard_map/ppermute | solution.py:73
  37.0 9.2 %collective-permute-start.7 = (s32[48]{0:T(128)S(1)}, s32[48]{0:T(128)S(1)}, u32[]{:S(2)}, u32[]{:S(2)}) collective-permute-start(s32[48]{0:T(128)S(1)} %get-tuple-element.16), channel_id=1, source_target_pairs={{0,32},{32,64},{64,96},{96,0},{1,33},{33,65},{65,97},{97,1},{2,34}... | collective-permute-start | bytes 584 | tf_op jit(solution)/shard_map/ppermute | solution.py:69
  37.1 9.1 %collective-permute-start.12 = (s32[48]{0:T(128)S(1)}, s32[48]{0:T(128)S(1)}, u32[]{:S(2)}, u32[]{:S(2)}) collective-permute-start(s32[48]{0:T(128)S(1)} %get-tuple-element.14), channel_id=1, source_target_pairs={{0,96},{32,0},{64,32},{96,64},{1,97},{33,1},{65,33},{97,65},{2,98}... | collective-permute-start | bytes 584 | tf_op jit(solution)/shard_map/ppermute | solution.py:70
  41.0 4.8 %collective-permute-start.11 = (s32[24]{0:T(128)S(1)}, s32[24]{0:T(128)S(1)}, u32[]{:S(2)}, u32[]{:S(2)}) collective-permute-start(s32[24]{0:T(128)S(1)} %collective-permute-done.10), channel_id=1, source_target_pairs={{0,96},{32,0},{64,32},{96,64},{1,97},{33,1},{65,33},{97,65},{2,98}... | collective-permute-start | bytes 296 | tf_op jit(solution)/shard_map/ppermute | solution.py:74
  42.5 3.6 %collective-permute-start.9 = (s32[24]{0:T(128)S(1)}, s32[24]{0:T(128)S(1)}, u32[]{:S(2)}, u32[]{:S(2)}) collective-permute-start(s32[24]{0:T(128)S(1)} %collective-permute-done.8), channel_id=1, source_target_pairs={{0,32},{32,64},{64,96},{96,0},{1,33},{33,65},{65,97},{97,1},{2,34}... | collective-permute-start | bytes 296 | tf_op jit(solution)/shard_map/ppermute | solution.py:73
  42.5 135.8 %collective-permute-start.6 = (bf16[192,4096]{1,0:T(8,128)(2,1)S(1)}, bf16[192,4096]{1,0:T(8,128)(2,1)S(1)}, u32[]{:S(2)}, u32[]{:S(2)}) collective-permute-start(bf16[192,4096]{1,0:T(8,128)(2,1)S(1)} %bitcast.34), channel_id=1, source_target_pairs={{0,1},{1,0},{2,3},{3,2},{4,5},{5,4},{6,7},{7,6},{8,9},{9,8},{10,11... | collective-permute-start | bytes 4718600 | tf_op jit(solution)/shard_map/ppermute | solution.py:114
  215.6 6.5 %collective-permute-start.13 = (f32[192,3072]{1,0:T(8,128)}, f32[192,3072]{1,0:T(8,128)S(1)}, u32[]{:S(2)}, u32[]{:S(2)}) collective-permute-start(f32[192,3072]{1,0:T(8,128)} %get-tuple-element.6), channel_id=1, source_target_pairs={{0,1},{1,0},{2,3},{3,2},{4,5},{5,4},{6,7},{7,6},{8,9},{9,8},{10,11... | collective-permute-start | bytes 7077896 | tf_op jit(solution)/shard_map/ppermute | solution.py:124
  216.9 3.7 %collective-permute-start.14 = (f32[4,4096]{1,0:T(4,128)S(1)}, f32[4,4096]{1,0:T(4,128)S(1)}, u32[]{:S(2)}, u32[]{:S(2)}) collective-permute-start(f32[4,4096]{1,0:T(4,128)S(1)} %slice.39), channel_id=1, source_target_pairs={{0,1},{1,0},{2,3},{3,2},{4,5},{5,4},{6,7},{7,6},{8,9},{9,8},{10,11... | collective-permute-start | bytes 196616 | tf_op jit(solution)/shard_map/ppermute | solution.py:126
Sparse Core Ops, SparseCore 0:
  34.2 162.3 all-gather.1

commit v8 on v7

--- a/solution.py
+++ b/solution.py
@@ -9,7 +9,8 @@
 
 CL_DEV = 4
 
-def _gram_consensus_kernel(scale, rows, half_ref, a_ref, oh_ref, p_ref, mine_ref, theirs_ref, c_ref):
+def _gram_consensus_kernel(scale, rows, half_ref, a_ref, oh_ref, p_ref, prior_ref, mine_ref, theirs_ref, c_ref):
+    del prior_ref
     j = pl.program_id(0)
     blk = p_ref[...]
     res = lax.dot_general(
@@ -25,26 +26,28 @@
     c_ref[...] += jnp.dot(oh_ref[...], blk, preferred_element_type=jnp.float32)
 
 
-def gram_consensus(half, pair_rows, one_hot, gathered, block_rows=1024):
+def gram_consensus(half, part, parts, pair_rows, one_hot, gathered, prior, block_rows=512):
     rows = pair_rows.shape[0] // 2
     bins = pair_rows.shape[1]
     total = gathered.shape[0]
     heads = one_hot.shape[0]
-    steps = total // 2 // block_rows
-    flops = 2 * 2 * rows * (total // 2) * bins + 2 * heads * (total // 2) * bins
-    bytes_accessed = 2 * (2 * rows * bins + heads * total // 2 + total // 2 * bins) + 4 * (
-        2 * rows * total // 2 + heads * bins
-    )
+    width = total // 2 // parts
+    steps = width // block_rows
+    per_half = total // 2 // block_rows
+    first = part * steps
+    flops = 2 * 2 * rows * width * bins + 2 * heads * width * bins
+    bytes_accessed = 2 * (2 * rows * bins + heads * width + width * bins) + 4 * (2 * rows * width + heads * bins)
     grid_spec = pltpu.PrefetchScalarGridSpec(
         num_scalar_prefetch=1,
         grid=(steps,),
         in_specs=[
             pl.BlockSpec((2 * rows, bins), lambda j, h: (0, 0)),
-            pl.BlockSpec((heads, block_rows), lambda j, h: (0, h[0] * steps + j)),
-            pl.BlockSpec((block_rows, bins), lambda j, h: (h[0] * steps + j, 0)),
+            pl.BlockSpec((heads, block_rows), lambda j, h: (0, h[0] * per_half + first + j)),
+            pl.BlockSpec((block_rows, bins), lambda j, h: (h[0] * per_half + first + j, 0)),
+            pl.BlockSpec(memory_space=pl.ANY),
         ],
         out_specs=[
-            pl.BlockSpec((rows, block_rows), lambda j, h: (0, h[0] * steps + j)),
+            pl.BlockSpec((rows, block_rows), lambda j, h: (0, h[0] * per_half + first + j)),
             pl.BlockSpec((rows, block_rows), lambda j, h: (0, j)),
             pl.BlockSpec((heads, bins), lambda j, h: (0, 0)),
         ],
@@ -54,12 +57,13 @@
         grid_spec=grid_spec,
         out_shape=[
             jax.ShapeDtypeStruct((rows, total), jnp.float32),
-            jax.ShapeDtypeStruct((rows, total // 2), jnp.float32),
+            jax.ShapeDtypeStruct((rows, width), jnp.float32),
             jax.ShapeDtypeStruct((heads, bins), jnp.float32),
         ],
+        input_output_aliases={4: 0},
         compiler_params=pltpu.CompilerParams(dimension_semantics=("arbitrary",)),
         cost_estimate=pl.CostEstimate(flops=flops, bytes_accessed=bytes_accessed, transcendentals=0),
-    )(half, pair_rows, one_hot, gathered)
+    )(half, pair_rows, one_hot, gathered, prior)
 
 
 def exchange_over_mass(pieces, mass_count):
@@ -120,9 +124,20 @@
         + jnp.arange(2 * CL_DEV, dtype=jnp.int32) % CL_DEV
     )
     one_hot = (own_ids[:, None] == gathered_labels[None, :]).astype(jnp.bfloat16)
-    mine, theirs, sums = gram_consensus(half.reshape(1), pair_rows, one_hot, gathered)
-    returned = lax.ppermute(theirs, "tile", swap)
-    gram_tiles = lax.dynamic_update_slice(mine, returned, (0, (1 - half) * theirs.shape[1]))
+    parts = 2
+    mine = jnp.zeros((slot_count, gathered.shape[0]), jnp.float32)
+    other = (1 - half) * (gathered.shape[0] // 2)
+    returned = []
+    sums = None
+    for part in range(parts):
+        mine, theirs, part_sums = gram_consensus(
+            half.reshape(1), part, parts, pair_rows, one_hot, gathered, mine
+        )
+        returned.append((part * theirs.shape[1], lax.ppermute(theirs, "tile", swap)))
+        sums = part_sums if sums is None else sums + part_sums
+    gram_tiles = mine
+    for offset, piece in returned:
+        gram_tiles = lax.dynamic_update_slice(gram_tiles, piece, (0, other + offset))
     consensus = sums[:CL_DEV] + lax.ppermute(sums[CL_DEV:], "tile", swap)
     return (gram_tiles, consensus)
 

time: 231 us -> 235 us (1.017)
  Pallas kernels: 18.9 us -> 22.6 us
  local copies, waits for them, and re-layouts: 6.02 us -> 8.46 us
    pallas_call x1 -> x2, Pallas kernels: 18.9 us -> 22.6 us  [gram_consensus(): pl.pallas_call(functools.partial(_gram_consensus_kernel, 1.0 / bins, rows...]
    broadcast_in_dim x0 -> x1, local copies, waits for them, and re-layouts: none -> 2.72 us  [shards(): mine = jnp.zeros((slot_count, gathered.shape[0]), jnp.float32)]
    ppermute x1, waiting for transfers between devices: 3.33 us -> 0.74 us  [shards(): consensus = sums[:CL_DEV] + lax.ppermute(sums[CL_DEV:], 'tile', swap)]
  transfers between devices with their start and end apart: 16 -> 17, of which waited for: 5 -> 6; matrix products, arithmetic and copies ran while one was open for 3% -> 3% of each run, Pallas kernels for 0% -> 5%
where the time goes in v8:
time: 235 us
  blocking collectives  131 us (56%)
  waiting for transfers between devices  29.2 us (12%)
  Pallas kernels  22.6 us (10%)
  starting transfers between devices  20.1 us (9%)
  between operations  14.9 us (6%)
  local copies, waits for them, and re-layouts  8.46 us (4%)
  other arithmetic  8.45 us (4%)
    unnamed x1, blocking collectives  131 us
    pallas_call x2, Pallas kernels, gram_consensus(): pl.pallas_call(functools.partial(_gram_consensus_kernel, 1.0 / bins, rows...  22.6 us
    all_gather x1, waiting for transfers between devices, shards(): gathered = lax.all_gather(arrived, 'tile', axis=0, tiled=True)  16.4 us
    ppermute x4, waiting for transfers between devices, exchange_over_mass(): first = lax.ppermute(lax.ppermute(far[:half], 'mass', ahead), 'mass', ahead)  11.6 us
    ppermute x2, starting transfers between devices, exchange_over_mass(): from_ahead = lax.ppermute(pieces[(me - 1) % mass_count], 'mass', behind)  5.2 us
  transfers between devices with their start and end apart: 17, of which 6 were waited for; matrix products, arithmetic and copies ran while one was open for 3% of the time, Pallas kernels for 5%

profile of v8, /device:TPU:1, one launch (start us, length us, event | category | flops | bytes accessed | tf_op | source)
XLA Modules:
  0.0 234.8 jit_solution(7035785637644431747)
XLA Ops:
  7.2 0.8 fusion.5
  8.2 0.8 select_reduce_fusion.1
  9.0 1.4 fusion
  10.4 0.7 multiply_add_fusion
  11.1 0.6 convolution_convert_fusion
  11.8 2.1 collective-permute-start.1
  13.9 1.4 collective-permute-start.3
  15.5 2.6 %collective-permute-start.5 = (bf16[48,4096]{1,0:T(8,128)(2,1)S(1)}, bf16[48,4096]{1,0:T(8,128)(2,1)S(1)}, u32[]{:S(2)}, u32[]{:S(2)}) collective-permute-start(bf16[48,4096]{1,0:T(8,128)(2,1)S(1)} %get-tuple-element.15), channel_id=1, source_target_pairs={{0,96},{32,0},{64,32},{96,64},{1,97},{33,1},{65,33},{97,65},{2,98}... | collective-permute-start | bytes 1179656 | tf_op jit(solution)/shard_map/ppermute | solution.py:74
  18.1 1.3 collective-permute-done.1
  19.7 2.4 %collective-permute-start.4 = (bf16[24,4096]{1,0:T(8,128)(2,1)S(1)}, bf16[24,4096]{1,0:T(8,128)(2,1)S(1)}, u32[]{:S(2)}, u32[]{:S(2)}) collective-permute-start(bf16[24,4096]{1,0:T(8,128)(2,1)S(1)} %collective-permute-done.3), channel_id=1, source_target_pairs={{0,96},{32,0},{64,32},{96,64},{1,97},{33,1},{65,33},{97,65},{2,98}... | collective-permute-start | bytes 589832 | tf_op jit(solution)/shard_map/ppermute | solution.py:78
  22.1 9.9 %collective-permute-done.2 = bf16[24,4096]{1,0:T(8,128)(2,1)S(1)} collective-permute-done((bf16[24,4096]{1,0:T(8,128)(2,1)S(1)}, bf16[24,4096]{1,0:T(8,128)(2,1)S(1)}, u32[]{:S(2)}, u32[]{:S(2)}) %collective-permute-start.2) | collective-permute-done | bytes 196640 | tf_op jit(solution)/shard_map/ppermute | solution.py:77
  32.3 1.8 gather_fusion
  34.4 2.6 %collective-permute-start.10 = (s32[24]{0:T(128)S(1)}, s32[24]{0:T(128)S(1)}, u32[]{:S(2)}, u32[]{:S(2)}) collective-permute-start(s32[24]{0:T(128)S(1)} %get-tuple-element.24), channel_id=1, source_target_pairs={{0,96},{32,0},{64,32},{96,64},{1,97},{33,1},{65,33},{97,65},{2,98}... | collective-permute-start | bytes 296 | tf_op jit(solution)/shard_map/ppermute | solution.py:78
  37.1 2.6 %collective-permute-start.12 = (s32[48]{0:T(128)S(1)}, s32[48]{0:T(128)S(1)}, u32[]{:S(2)}, u32[]{:S(2)}) collective-permute-start(s32[48]{0:T(128)S(1)} %get-tuple-element.20), channel_id=1, source_target_pairs={{0,96},{32,0},{64,32},{96,64},{1,97},{33,1},{65,33},{97,65},{2,98}... | collective-permute-start | bytes 584 | tf_op jit(solution)/shard_map/ppermute | solution.py:74
  39.7 0.6 dynamic-slice
  41.0 1.5 collective-permute-start.11
  42.5 3.2 %collective-permute-start.6 = (bf16[192,4096]{1,0:T(8,128)(2,1)S(1)}, bf16[192,4096]{1,0:T(8,128)(2,1)S(1)}, u32[]{:S(2)}, u32[]{:S(2)}) collective-permute-start(bf16[192,4096]{1,0:T(8,128)(2,1)S(1)} %bitcast.34), channel_id=1, source_target_pairs={{0,1},{1,0},{2,3},{3,2},{4,5},{5,4},{6,7},{7,6},{8,9},{9,8},{10,11... | collective-permute-start | bytes 4718600 | tf_op jit(solution)/shard_map/ppermute | solution.py:118
  45.8 0.4 collective-permute-done.9
  46.2 0.6 gather_fusion.1
  47.1 130.5 %all-reduce = s32[6144]{0:T(1024)S(1)} all-reduce(s32[6144]{0:T(1024)S(1)} %dynamic-update-slice), channel_id=1, replica_groups=mesh['mass'=4,'tile'=32] {'tile'}, use_global_device_ids=true, to_apply=%add | all-reduce | flops 6144 | bytes 49152
  177.6 0.7 compare_convert_fusion.oh_ref
  178.4 1.9 pad_maximum_fusion.a_ref
  180.2 16.4 %all-gather.2.cloned.1.call-done.p_ref = bf16[6144,4096]{1,0:T(8,128)(2,1)} async-done(((bf16[192,4096]{1,0:T(8,128)(2,1)}), bf16[6144,4096]{1,0:T(8,128)(2,1)}) %all-gather.2.cloned.1.call-update) | async-done | bytes 50331664 | tf_op jit(solution)/shard_map/all_gather | solution.py:113
  196.7 2.7 %broadcast_in_dim.36.prior_ref = f32[192,6144]{1,0:T(8,128)} broadcast(f32[]{:T(128)} %constant.87.clone.1), dimensions={} | broadcast | bytes 4718596 | tf_op jit(solution)/shard_map/broadcast_in_dim | solution.py:128
  199.4 11.3 %shard_map.50 = (f32[192,6144]{1,0:T(8,128)}, f32[192,1536]{1,0:T(8,128)}, f32[8,4096]{1,0:T(8,128)}) custom-call(s32[1]{0:T(128)} %bitcast.half_ref, bf16[384,4096]{1,0:T(8,128)(2,1)} %pad_maximum_fusion.a_ref, bf16[8,6144]{1,0:T(8,128)(2,1)} %compare_convert_fusion.oh_ref, ...), custom_call_target="tpu_custom_call", output_to_operand_aliasing={{0}: (4, {})} | custom-call | flops 4932501504 | bytes 18243584 | tf_op jit(solution)/shard_map/pallas_call | solution.py:55
  210.7 0.5 collective-permute-start.13
  211.2 11.3 %shard_map.51 = (f32[192,6144]{1,0:T(8,128)}, f32[192,1536]{1,0:T(8,128)}, f32[8,4096]{1,0:T(8,128)}) custom-call(s32[1]{0:T(128)} %bitcast.half_ref, bf16[384,4096]{1,0:T(8,128)(2,1)} %pad_maximum_fusion.a_ref, bf16[8,6144]{1,0:T(8,128)(2,1)} %compare_convert_fusion.oh_ref, ...), custom_call_target="tpu_custom_call", output_to_operand_aliasing={{0}: (4, {})} | custom-call | flops 4932501504 | bytes 18243584 | tf_op jit(solution)/shard_map/pallas_call | solution.py:55
  222.5 0.9 add.155
  224.1 0.7 collective-permute-done.15
  224.8 0.6 slice_add_fusion
  225.5 1.1 constant_dynamic-update-slice_fusion.1
  226.9 1.1 constant_dynamic-update-slice_fusion
  (48 shorter events, 2.8 us)
Async XLA Ops:
  7.2 4.0 %copy-start.1 = (bf16[96,4096]{1,0:T(8,128)(2,1)S(1)}, bf16[96,4096]{1,0:T(8,128)(2,1)}, u32[]{:S(2)}) copy-start(bf16[96,4096]{1,0:T(8,128)(2,1)} %param.3) | copy-start | bytes 2359300
  7.2 189.5 %all-gather.2.cloned.1.call-start = ((), (), s32[]{:S(2)}) async-start(), calls=%async_computation | async-start | bytes 51904512 | tf_op jit(solution)/shard_map/all_gather | solution.py:113
  11.8 7.6 %collective-permute-start.1 = (bf16[24,4096]{1,0:T(8,128)(2,1)S(1)}, bf16[24,4096]{1,0:T(8,128)(2,1)S(1)}, u32[]{:S(2)}, u32[]{:S(2)}) collective-permute-start(bf16[24,4096]{1,0:T(8,128)(2,1)S(1)} %get-tuple-element.17), channel_id=1, source_target_pairs={{0,32},{32,64},{64,96},{96,0},{1,33},{33,65},{65,97},{97,1},{2,34}... | collective-permute-start | bytes 589832 | tf_op jit(solution)/shard_map/ppermute | solution.py:77
  13.9 5.8 %collective-permute-start.3 = (bf16[24,4096]{1,0:T(8,128)(2,1)S(1)}, bf16[24,4096]{1,0:T(8,128)(2,1)S(1)}, u32[]{:S(2)}, u32[]{:S(2)}) collective-permute-start(bf16[24,4096]{1,0:T(8,128)(2,1)S(1)} %get-tuple-element.18), channel_id=1, source_target_pairs={{0,96},{32,0},{64,32},{96,64},{1,97},{33,1},{65,33},{97,65},{2,98}... | collective-permute-start | bytes 589832 | tf_op jit(solution)/shard_map/ppermute | solution.py:78
  15.3 16.8 %collective-permute-start = (bf16[48,4096]{1,0:T(8,128)(2,1)S(1)}, bf16[48,4096]{1,0:T(8,128)(2,1)S(1)}, u32[]{:S(2)}, u32[]{:S(2)}) collective-permute-start(bf16[48,4096]{1,0:T(8,128)(2,1)S(1)} %get-tuple-element.16), channel_id=1, source_target_pairs={{0,32},{32,64},{64,96},{96,0},{1,33},{33,65},{65,97},{97,1},{2,34}... | collective-permute-start | bytes 1179656 | tf_op jit(solution)/shard_map/ppermute | solution.py:73
  15.5 16.6 %collective-permute-start.5 = (bf16[48,4096]{1,0:T(8,128)(2,1)S(1)}, bf16[48,4096]{1,0:T(8,128)(2,1)S(1)}, u32[]{:S(2)}, u32[]{:S(2)}) collective-permute-start(bf16[48,4096]{1,0:T(8,128)(2,1)S(1)} %get-tuple-element.15), channel_id=1, source_target_pairs={{0,96},{32,0},{64,32},{96,64},{1,97},{33,1},{65,33},{97,65},{2,98}... | collective-permute-start | bytes 1179656 | tf_op jit(solution)/shard_map/ppermute | solution.py:74
  19.4 12.6 %collective-permute-start.2 = (bf16[24,4096]{1,0:T(8,128)(2,1)S(1)}, bf16[24,4096]{1,0:T(8,128)(2,1)S(1)}, u32[]{:S(2)}, u32[]{:S(2)}) collective-permute-start(bf16[24,4096]{1,0:T(8,128)(2,1)S(1)} %collective-permute-done.1), channel_id=1, source_target_pairs={{0,32},{32,64},{64,96},{96,0},{1,33},{33,65},{65,97},{97,1},{2,34}... | collective-permute-start | bytes 589832 | tf_op jit(solution)/shard_map/ppermute | solution.py:77
  19.7 12.4 %collective-permute-start.4 = (bf16[24,4096]{1,0:T(8,128)(2,1)S(1)}, bf16[24,4096]{1,0:T(8,128)(2,1)S(1)}, u32[]{:S(2)}, u32[]{:S(2)}) collective-permute-start(bf16[24,4096]{1,0:T(8,128)(2,1)S(1)} %collective-permute-done.3), channel_id=1, source_target_pairs={{0,96},{32,0},{64,32},{96,64},{1,97},{33,1},{65,33},{97,65},{2,98}... | collective-permute-start | bytes 589832 | tf_op jit(solution)/shard_map/ppermute | solution.py:78
  34.1 5.6 %copy-start.3 = (u32[128]{0:T(128)S(1)}, u32[128]{0:T(128)}, u32[]{:S(2)}) copy-start(u32[128]{0:T(128)} %constant.106) | copy-start | bytes 1540
  34.1 8.4 %copy-start = (bf16[4,48,4096]{2,1,0:T(8,128)(2,1)S(1)}, bf16[4,48,4096]{2,1,0:T(8,128)(2,1)}, u32[]{:S(2)}) copy-start(bf16[4,48,4096]{2,1,0:T(8,128)(2,1)} %gather_fusion) | copy-start | bytes 4718596
  34.4 6.6 %collective-permute-start.10 = (s32[24]{0:T(128)S(1)}, s32[24]{0:T(128)S(1)}, u32[]{:S(2)}, u32[]{:S(2)}) collective-permute-start(s32[24]{0:T(128)S(1)} %get-tuple-element.24), channel_id=1, source_target_pairs={{0,96},{32,0},{64,32},{96,64},{1,97},{33,1},{65,33},{97,65},{2,98}... | collective-permute-start | bytes 296 | tf_op jit(solution)/shard_map/ppermute | solution.py:78
  37.0 5.5 %collective-permute-start.8 = (s32[24]{0:T(128)S(1)}, s32[24]{0:T(128)S(1)}, u32[]{:S(2)}, u32[]{:S(2)}) collective-permute-start(s32[24]{0:T(128)S(1)} %get-tuple-element.23), channel_id=1, source_target_pairs={{0,32},{32,64},{64,96},{96,0},{1,33},{33,65},{65,97},{97,1},{2,34}... | collective-permute-start | bytes 296 | tf_op jit(solution)/shard_map/ppermute | solution.py:77
  37.0 9.2 %collective-permute-start.7 = (s32[48]{0:T(128)S(1)}, s32[48]{0:T(128)S(1)}, u32[]{:S(2)}, u32[]{:S(2)}) collective-permute-start(s32[48]{0:T(128)S(1)} %get-tuple-element.22), channel_id=1, source_target_pairs={{0,32},{32,64},{64,96},{96,0},{1,33},{33,65},{65,97},{97,1},{2,34}... | collective-permute-start | bytes 584 | tf_op jit(solution)/shard_map/ppermute | solution.py:73
  37.1 9.1 %collective-permute-start.12 = (s32[48]{0:T(128)S(1)}, s32[48]{0:T(128)S(1)}, u32[]{:S(2)}, u32[]{:S(2)}) collective-permute-start(s32[48]{0:T(128)S(1)} %get-tuple-element.20), channel_id=1, source_target_pairs={{0,96},{32,0},{64,32},{96,64},{1,97},{33,1},{65,33},{97,65},{2,98}... | collective-permute-start | bytes 584 | tf_op jit(solution)/shard_map/ppermute | solution.py:74
  41.0 4.8 %collective-permute-start.11 = (s32[24]{0:T(128)S(1)}, s32[24]{0:T(128)S(1)}, u32[]{:S(2)}, u32[]{:S(2)}) collective-permute-start(s32[24]{0:T(128)S(1)} %collective-permute-done.10), channel_id=1, source_target_pairs={{0,96},{32,0},{64,32},{96,64},{1,97},{33,1},{65,33},{97,65},{2,98}... | collective-permute-start | bytes 296 | tf_op jit(solution)/shard_map/ppermute | solution.py:78
  42.5 3.6 %collective-permute-start.9 = (s32[24]{0:T(128)S(1)}, s32[24]{0:T(128)S(1)}, u32[]{:S(2)}, u32[]{:S(2)}) collective-permute-start(s32[24]{0:T(128)S(1)} %collective-permute-done.8), channel_id=1, source_target_pairs={{0,32},{32,64},{64,96},{96,0},{1,33},{33,65},{65,97},{97,1},{2,34}... | collective-permute-start | bytes 296 | tf_op jit(solution)/shard_map/ppermute | solution.py:77
  42.5 135.8 %collective-permute-start.6 = (bf16[192,4096]{1,0:T(8,128)(2,1)S(1)}, bf16[192,4096]{1,0:T(8,128)(2,1)S(1)}, u32[]{:S(2)}, u32[]{:S(2)}) collective-permute-start(bf16[192,4096]{1,0:T(8,128)(2,1)S(1)} %bitcast.34), channel_id=1, source_target_pairs={{0,1},{1,0},{2,3},{3,2},{4,5},{5,4},{6,7},{7,6},{8,9},{9,8},{10,11... | collective-permute-start | bytes 4718600 | tf_op jit(solution)/shard_map/ppermute | solution.py:118
  210.7 14.8 %collective-permute-start.13 = (f32[192,1536]{1,0:T(8,128)}, f32[192,1536]{1,0:T(8,128)S(1)}, u32[]{:S(2)}, u32[]{:S(2)}) collective-permute-start(f32[192,1536]{1,0:T(8,128)} %get-tuple-element.10), channel_id=1, source_target_pairs={{0,1},{1,0},{2,3},{3,2},{4,5},{5,4},{6,7},{7,6},{8,9},{9,8},{10,11... | collective-permute-start | bytes 3538952 | tf_op jit(solution)/shard_map/ppermute | solution.py:136
  211.2 11.3 %copy-start.2 = (f32[8,4096]{1,0:T(8,128)S(1)}, f32[8,4096]{1,0:T(8,128)}, u32[]{:S(2)}) copy-start(f32[8,4096]{1,0:T(8,128)} %get-tuple-element.12) | copy-start | bytes 393220
  223.5 1.3 collective-permute-start.15
  223.8 3.1 %collective-permute-start.14 = (f32[192,1536]{1,0:T(8,128)}, f32[192,1536]{1,0:T(8,128)S(1)}, u32[]{:S(2)}, u32[]{:S(2)}) collective-permute-start(f32[192,1536]{1,0:T(8,128)} %get-tuple-element.11), channel_id=1, source_target_pairs={{0,1},{1,0},{2,3},{3,2},{4,5},{5,4},{6,7},{7,6},{8,9},{9,8},{10,11... | collective-permute-start | bytes 3538952 | tf_op jit(solution)/shard_map/ppermute | solution.py:136
Sparse Core Ops, SparseCore 0:
  34.3 162.3 all-gather.1

commit v9 on v7

--- a/solution.py
+++ b/solution.py
@@ -121,8 +121,14 @@
     )
     one_hot = (own_ids[:, None] == gathered_labels[None, :]).astype(jnp.bfloat16)
     mine, theirs, sums = gram_consensus(half.reshape(1), pair_rows, one_hot, gathered)
-    returned = lax.ppermute(theirs, "tile", swap)
-    gram_tiles = lax.dynamic_update_slice(mine, returned, (0, (1 - half) * theirs.shape[1]))
+    pieces = 4
+    step = theirs.shape[0] // pieces
+    gram_tiles = mine
+    for p in range(pieces):
+        returned = lax.ppermute(theirs[p * step:(p + 1) * step], "tile", swap)
+        gram_tiles = lax.dynamic_update_slice(
+            gram_tiles, returned, (p * step, (1 - half) * theirs.shape[1])
+        )
     consensus = sums[:CL_DEV] + lax.ppermute(sums[CL_DEV:], "tile", swap)
     return (gram_tiles, consensus)
 

time: 231 us -> 231 us (level)
  local copies, waits for them, and re-layouts: 6.02 us -> 9.78 us
  waiting for transfers between devices: 31.4 us -> 28.3 us
    ppermute x1, waiting for transfers between devices: 3.33 us -> 0.01 us  [shards(): consensus = sums[:CL_DEV] + lax.ppermute(sums[CL_DEV:], 'tile', swap)]
  transfers between devices with their start and end apart: 16 -> 19, of which waited for: 5 -> 5; matrix products, arithmetic and copies ran while one was open for 3% -> 4% of each run, Pallas kernels for 0% -> 0%
where the time goes in v9:
time: 231 us
  blocking collectives  131 us (57%)
  waiting for transfers between devices  28.3 us (12%)
  starting transfers between devices  20.4 us (9%)
  Pallas kernels  18.9 us (8%)
  between operations  14.9 us (6%)
  local copies, waits for them, and re-layouts  9.78 us (4%)
  other arithmetic  7.48 us (3%)
    unnamed x1, blocking collectives  131 us
    pallas_call x1, Pallas kernels, gram_consensus(): pl.pallas_call(functools.partial(_gram_consensus_kernel, 1.0 / bins, rows...  18.9 us
    all_gather x1, waiting for transfers between devices, shards(): gathered = lax.all_gather(arrived, 'tile', axis=0, tiled=True)  16.3 us
    ppermute x4, waiting for transfers between devices, exchange_over_mass(): first = lax.ppermute(lax.ppermute(far[:half], 'mass', ahead), 'mass', ahead)  11.6 us
    ppermute x2, starting transfers between devices, exchange_over_mass(): from_ahead = lax.ppermute(pieces[(me - 1) % mass_count], 'mass', behind)  5.19 us
  transfers between devices with their start and end apart: 19, of which 5 were waited for; matrix products, arithmetic and copies ran while one was open for 4% of the time, Pallas kernels for 0%

profile of v9, /device:TPU:1, one launch (start us, length us, event | category | flops | bytes accessed | tf_op | source)
XLA Modules:
  0.0 231.0 jit_solution(10402115115185789388)
XLA Ops:
  7.2 0.8 fusion.5
  8.2 0.8 select_reduce_fusion.1
  9.0 1.4 fusion
  10.4 0.7 multiply_add_fusion
  11.1 0.6 convolution_convert_fusion
  11.8 2.1 collective-permute-start.1
  13.9 1.3 collective-permute-start.3
  15.5 2.6 %collective-permute-start.5 = (bf16[48,4096]{1,0:T(8,128)(2,1)S(1)}, bf16[48,4096]{1,0:T(8,128)(2,1)S(1)}, u32[]{:S(2)}, u32[]{:S(2)}) collective-permute-start(bf16[48,4096]{1,0:T(8,128)(2,1)S(1)} %get-tuple-element.13), channel_id=1, source_target_pairs={{0,96},{32,0},{64,32},{96,64},{1,97},{33,1},{65,33},{97,65},{2,98}... | collective-permute-start | bytes 1179656 | tf_op jit(solution)/shard_map/ppermute | solution.py:70
  18.1 1.3 collective-permute-done.1
  19.7 2.4 %collective-permute-start.4 = (bf16[24,4096]{1,0:T(8,128)(2,1)S(1)}, bf16[24,4096]{1,0:T(8,128)(2,1)S(1)}, u32[]{:S(2)}, u32[]{:S(2)}) collective-permute-start(bf16[24,4096]{1,0:T(8,128)(2,1)S(1)} %collective-permute-done.3), channel_id=1, source_target_pairs={{0,96},{32,0},{64,32},{96,64},{1,97},{33,1},{65,33},{97,65},{2,98}... | collective-permute-start | bytes 589832 | tf_op jit(solution)/shard_map/ppermute | solution.py:74
  22.1 9.9 %collective-permute-done.2 = bf16[24,4096]{1,0:T(8,128)(2,1)S(1)} collective-permute-done((bf16[24,4096]{1,0:T(8,128)(2,1)S(1)}, bf16[24,4096]{1,0:T(8,128)(2,1)S(1)}, u32[]{:S(2)}, u32[]{:S(2)}) %collective-permute-start.2) | collective-permute-done | bytes 196640 | tf_op jit(solution)/shard_map/ppermute | solution.py:73
  32.3 1.8 gather_fusion
  34.4 2.6 %collective-permute-start.10 = (s32[24]{0:T(128)S(1)}, s32[24]{0:T(128)S(1)}, u32[]{:S(2)}, u32[]{:S(2)}) collective-permute-start(s32[24]{0:T(128)S(1)} %get-tuple-element.22), channel_id=1, source_target_pairs={{0,96},{32,0},{64,32},{96,64},{1,97},{33,1},{65,33},{97,65},{2,98}... | collective-permute-start | bytes 296 | tf_op jit(solution)/shard_map/ppermute | solution.py:74
  37.1 2.6 %collective-permute-start.12 = (s32[48]{0:T(128)S(1)}, s32[48]{0:T(128)S(1)}, u32[]{:S(2)}, u32[]{:S(2)}) collective-permute-start(s32[48]{0:T(128)S(1)} %get-tuple-element.18), channel_id=1, source_target_pairs={{0,96},{32,0},{64,32},{96,64},{1,97},{33,1},{65,33},{97,65},{2,98}... | collective-permute-start | bytes 584 | tf_op jit(solution)/shard_map/ppermute | solution.py:70
  39.7 0.7 dynamic-slice
  41.1 1.5 collective-permute-start.11
  42.7 3.2 %collective-permute-start.6 = (bf16[192,4096]{1,0:T(8,128)(2,1)S(1)}, bf16[192,4096]{1,0:T(8,128)(2,1)S(1)}, u32[]{:S(2)}, u32[]{:S(2)}) collective-permute-start(bf16[192,4096]{1,0:T(8,128)(2,1)S(1)} %bitcast.34), channel_id=1, source_target_pairs={{0,1},{1,0},{2,3},{3,2},{4,5},{5,4},{6,7},{7,6},{8,9},{9,8},{10,11... | collective-permute-start | bytes 4718600 | tf_op jit(solution)/shard_map/ppermute | solution.py:114
  45.9 0.4 collective-permute-done.9
  46.4 0.6 gather_fusion.1
  47.3 130.6 %all-reduce = s32[6144]{0:T(1024)S(1)} all-reduce(s32[6144]{0:T(1024)S(1)} %dynamic-update-slice), channel_id=1, replica_groups=mesh['mass'=4,'tile'=32] {'tile'}, use_global_device_ids=true, to_apply=%add | all-reduce | flops 6144 | bytes 49152
  177.8 0.7 compare_convert_fusion.oh_ref
  178.6 1.8 pad_maximum_fusion.a_ref
  180.4 16.3 %all-gather.2.cloned.1.call-done.p_ref = bf16[6144,4096]{1,0:T(8,128)(2,1)} async-done(((bf16[192,4096]{1,0:T(8,128)(2,1)}), bf16[6144,4096]{1,0:T(8,128)(2,1)}) %all-gather.2.cloned.1.call-update) | async-done | bytes 50331664 | tf_op jit(solution)/shard_map/all_gather | solution.py:109
  196.7 18.9 %shard_map.50 = (f32[192,6144]{1,0:T(8,128)}, f32[192,3072]{1,0:T(8,128)}, f32[8,4096]{1,0:T(8,128)}) custom-call(s32[1]{0:T(128)} %bitcast.half_ref, bf16[384,4096]{1,0:T(8,128)(2,1)} %pad_maximum_fusion.a_ref, bf16[8,6144]{1,0:T(8,128)(2,1)} %compare_convert_fusion.oh_ref, bf16[6144,4096]{1,0:T(8,128)(2,1)} %all-gather.2.cloned.1.call-done.p_ref), custom_call_target="tpu_custom_call" | custom-call | flops 9865003008 | bytes 33210368 | tf_op jit(solution)/shard_map/pallas_call | solution.py:52
  215.6 0.9 slice.55
  216.5 0.3 collective-permute-start.17
  216.9 1.8 fusion.13
  219.8 0.6 slice_add_fusion
  220.8 0.9 constant_dynamic-update-slice_fusion
  221.6 0.9 constant_dynamic-update-slice_fusion.3
  222.5 0.9 constant_dynamic-update-slice_fusion.2
  223.3 0.9 constant_dynamic-update-slice_fusion.1
  (52 shorter events, 3.3 us)
Async XLA Ops:
  7.2 4.0 %copy-start.1 = (bf16[96,4096]{1,0:T(8,128)(2,1)S(1)}, bf16[96,4096]{1,0:T(8,128)(2,1)}, u32[]{:S(2)}) copy-start(bf16[96,4096]{1,0:T(8,128)(2,1)} %param.3) | copy-start | bytes 2359300
  7.2 189.5 %all-gather.2.cloned.1.call-start = ((), (), s32[]{:S(2)}) async-start(), calls=%async_computation | async-start | bytes 51904512 | tf_op jit(solution)/shard_map/all_gather | solution.py:109
  11.8 7.6 %collective-permute-start.1 = (bf16[24,4096]{1,0:T(8,128)(2,1)S(1)}, bf16[24,4096]{1,0:T(8,128)(2,1)S(1)}, u32[]{:S(2)}, u32[]{:S(2)}) collective-permute-start(bf16[24,4096]{1,0:T(8,128)(2,1)S(1)} %get-tuple-element.15), channel_id=1, source_target_pairs={{0,32},{32,64},{64,96},{96,0},{1,33},{33,65},{65,97},{97,1},{2,34}... | collective-permute-start | bytes 589832 | tf_op jit(solution)/shard_map/ppermute | solution.py:73
  13.9 5.8 %collective-permute-start.3 = (bf16[24,4096]{1,0:T(8,128)(2,1)S(1)}, bf16[24,4096]{1,0:T(8,128)(2,1)S(1)}, u32[]{:S(2)}, u32[]{:S(2)}) collective-permute-start(bf16[24,4096]{1,0:T(8,128)(2,1)S(1)} %get-tuple-element.16), channel_id=1, source_target_pairs={{0,96},{32,0},{64,32},{96,64},{1,97},{33,1},{65,33},{97,65},{2,98}... | collective-permute-start | bytes 589832 | tf_op jit(solution)/shard_map/ppermute | solution.py:74
  15.4 16.7 %collective-permute-start = (bf16[48,4096]{1,0:T(8,128)(2,1)S(1)}, bf16[48,4096]{1,0:T(8,128)(2,1)S(1)}, u32[]{:S(2)}, u32[]{:S(2)}) collective-permute-start(bf16[48,4096]{1,0:T(8,128)(2,1)S(1)} %get-tuple-element.14), channel_id=1, source_target_pairs={{0,32},{32,64},{64,96},{96,0},{1,33},{33,65},{65,97},{97,1},{2,34}... | collective-permute-start | bytes 1179656 | tf_op jit(solution)/shard_map/ppermute | solution.py:69
  15.5 16.5 %collective-permute-start.5 = (bf16[48,4096]{1,0:T(8,128)(2,1)S(1)}, bf16[48,4096]{1,0:T(8,128)(2,1)S(1)}, u32[]{:S(2)}, u32[]{:S(2)}) collective-permute-start(bf16[48,4096]{1,0:T(8,128)(2,1)S(1)} %get-tuple-element.13), channel_id=1, source_target_pairs={{0,96},{32,0},{64,32},{96,64},{1,97},{33,1},{65,33},{97,65},{2,98}... | collective-permute-start | bytes 1179656 | tf_op jit(solution)/shard_map/ppermute | solution.py:70
  19.4 12.6 %collective-permute-start.2 = (bf16[24,4096]{1,0:T(8,128)(2,1)S(1)}, bf16[24,4096]{1,0:T(8,128)(2,1)S(1)}, u32[]{:S(2)}, u32[]{:S(2)}) collective-permute-start(bf16[24,4096]{1,0:T(8,128)(2,1)S(1)} %collective-permute-done.1), channel_id=1, source_target_pairs={{0,32},{32,64},{64,96},{96,0},{1,33},{33,65},{65,97},{97,1},{2,34}... | collective-permute-start | bytes 589832 | tf_op jit(solution)/shard_map/ppermute | solution.py:73
  19.7 12.4 %collective-permute-start.4 = (bf16[24,4096]{1,0:T(8,128)(2,1)S(1)}, bf16[24,4096]{1,0:T(8,128)(2,1)S(1)}, u32[]{:S(2)}, u32[]{:S(2)}) collective-permute-start(bf16[24,4096]{1,0:T(8,128)(2,1)S(1)} %collective-permute-done.3), channel_id=1, source_target_pairs={{0,96},{32,0},{64,32},{96,64},{1,97},{33,1},{65,33},{97,65},{2,98}... | collective-permute-start | bytes 589832 | tf_op jit(solution)/shard_map/ppermute | solution.py:74
  34.1 5.6 %copy-start.3 = (u32[128]{0:T(128)S(1)}, u32[128]{0:T(128)}, u32[]{:S(2)}) copy-start(u32[128]{0:T(128)} %constant.106) | copy-start | bytes 1540
  34.1 8.6 %copy-start = (bf16[4,48,4096]{2,1,0:T(8,128)(2,1)S(1)}, bf16[4,48,4096]{2,1,0:T(8,128)(2,1)}, u32[]{:S(2)}) copy-start(bf16[4,48,4096]{2,1,0:T(8,128)(2,1)} %gather_fusion) | copy-start | bytes 4718596
  34.4 6.7 %collective-permute-start.10 = (s32[24]{0:T(128)S(1)}, s32[24]{0:T(128)S(1)}, u32[]{:S(2)}, u32[]{:S(2)}) collective-permute-start(s32[24]{0:T(128)S(1)} %get-tuple-element.22), channel_id=1, source_target_pairs={{0,96},{32,0},{64,32},{96,64},{1,97},{33,1},{65,33},{97,65},{2,98}... | collective-permute-start | bytes 296 | tf_op jit(solution)/shard_map/ppermute | solution.py:74
  37.0 5.6 %collective-permute-start.8 = (s32[24]{0:T(128)S(1)}, s32[24]{0:T(128)S(1)}, u32[]{:S(2)}, u32[]{:S(2)}) collective-permute-start(s32[24]{0:T(128)S(1)} %get-tuple-element.21), channel_id=1, source_target_pairs={{0,32},{32,64},{64,96},{96,0},{1,33},{33,65},{65,97},{97,1},{2,34}... | collective-permute-start | bytes 296 | tf_op jit(solution)/shard_map/ppermute | solution.py:73
  37.0 9.3 %collective-permute-start.7 = (s32[48]{0:T(128)S(1)}, s32[48]{0:T(128)S(1)}, u32[]{:S(2)}, u32[]{:S(2)}) collective-permute-start(s32[48]{0:T(128)S(1)} %get-tuple-element.20), channel_id=1, source_target_pairs={{0,32},{32,64},{64,96},{96,0},{1,33},{33,65},{65,97},{97,1},{2,34}... | collective-permute-start | bytes 584 | tf_op jit(solution)/shard_map/ppermute | solution.py:69
  37.1 9.3 %collective-permute-start.12 = (s32[48]{0:T(128)S(1)}, s32[48]{0:T(128)S(1)}, u32[]{:S(2)}, u32[]{:S(2)}) collective-permute-start(s32[48]{0:T(128)S(1)} %get-tuple-element.18), channel_id=1, source_target_pairs={{0,96},{32,0},{64,32},{96,64},{1,97},{33,1},{65,33},{97,65},{2,98}... | collective-permute-start | bytes 584 | tf_op jit(solution)/shard_map/ppermute | solution.py:70
  41.1 4.8 %collective-permute-start.11 = (s32[24]{0:T(128)S(1)}, s32[24]{0:T(128)S(1)}, u32[]{:S(2)}, u32[]{:S(2)}) collective-permute-start(s32[24]{0:T(128)S(1)} %collective-permute-done.10), channel_id=1, source_target_pairs={{0,96},{32,0},{64,32},{96,64},{1,97},{33,1},{65,33},{97,65},{2,98}... | collective-permute-start | bytes 296 | tf_op jit(solution)/shard_map/ppermute | solution.py:74
  42.6 3.6 %collective-permute-start.9 = (s32[24]{0:T(128)S(1)}, s32[24]{0:T(128)S(1)}, u32[]{:S(2)}, u32[]{:S(2)}) collective-permute-start(s32[24]{0:T(128)S(1)} %collective-permute-done.8), channel_id=1, source_target_pairs={{0,32},{32,64},{64,96},{96,0},{1,33},{33,65},{65,97},{97,1},{2,34}... | collective-permute-start | bytes 296 | tf_op jit(solution)/shard_map/ppermute | solution.py:73
  42.7 135.9 %collective-permute-start.6 = (bf16[192,4096]{1,0:T(8,128)(2,1)S(1)}, bf16[192,4096]{1,0:T(8,128)(2,1)S(1)}, u32[]{:S(2)}, u32[]{:S(2)}) collective-permute-start(bf16[192,4096]{1,0:T(8,128)(2,1)S(1)} %bitcast.34), channel_id=1, source_target_pairs={{0,1},{1,0},{2,3},{3,2},{4,5},{5,4},{6,7},{7,6},{8,9},{9,8},{10,11... | collective-permute-start | bytes 4718600 | tf_op jit(solution)/shard_map/ppermute | solution.py:114
  216.5 3.2 %collective-permute-start.17 = (f32[4,4096]{1,0:T(4,128)S(1)}, f32[4,4096]{1,0:T(4,128)S(1)}, u32[]{:S(2)}, u32[]{:S(2)}) collective-permute-start(f32[4,4096]{1,0:T(4,128)S(1)} %slice.55), channel_id=1, source_target_pairs={{0,1},{1,0},{2,3},{3,2},{4,5},{5,4},{6,7},{7,6},{8,9},{9,8},{10,11... | collective-permute-start | bytes 196616 | tf_op jit(solution)/shard_map/ppermute | solution.py:132
  216.9 2.9 %copy-start.2 = (f32[8,4096]{1,0:T(8,128)S(1)}, f32[8,4096]{1,0:T(8,128)}, u32[]{:S(2)}) copy-start(f32[8,4096]{1,0:T(8,128)} %get-tuple-element.7) | copy-start | bytes 393220
  218.7 2.1 collective-permute-start.13
  219.0 2.6 %collective-permute-start.14 = (f32[48,3072]{1,0:T(8,128)S(1)}, f32[48,3072]{1,0:T(8,128)S(1)}, u32[]{:S(2)}, u32[]{:S(2)}) collective-permute-start(f32[48,3072]{1,0:T(8,128)S(1)} %get-tuple-element.10), channel_id=1, source_target_pairs={{0,1},{1,0},{2,3},{3,2},{4,5},{5,4},{6,7},{7,6},{8,9},{9,8},{10,11... | collective-permute-start | bytes 1769480 | tf_op jit(solution)/shard_map/ppermute | solution.py:128
  219.3 3.2 %collective-permute-start.15 = (f32[48,3072]{1,0:T(8,128)S(1)}, f32[48,3072]{1,0:T(8,128)S(1)}, u32[]{:S(2)}, u32[]{:S(2)}) collective-permute-start(f32[48,3072]{1,0:T(8,128)S(1)} %get-tuple-element.9), channel_id=1, source_target_pairs={{0,1},{1,0},{2,3},{3,2},{4,5},{5,4},{6,7},{7,6},{8,9},{9,8},{10,11... | collective-permute-start | bytes 1769480 | tf_op jit(solution)/shard_map/ppermute | solution.py:128
  219.5 3.8 %collective-permute-start.16 = (f32[48,3072]{1,0:T(8,128)S(1)}, f32[48,3072]{1,0:T(8,128)S(1)}, u32[]{:S(2)}, u32[]{:S(2)}) collective-permute-start(f32[48,3072]{1,0:T(8,128)S(1)} %get-tuple-element.8), channel_id=1, source_target_pairs={{0,1},{1,0},{2,3},{3,2},{4,5},{5,4},{6,7},{7,6},{8,9},{9,8},{10,11... | collective-permute-start | bytes 1769480 | tf_op jit(solution)/shard_map/ppermute | solution.py:128
Sparse Core Ops, SparseCore 0:
  34.2 162.3 all-gather.1

commit v10 on v7

--- a/solution.py
+++ b/solution.py
@@ -9,28 +9,36 @@
 
 CL_DEV = 4
 
-def _gram_consensus_kernel(scale, rows, half_ref, a_ref, oh_ref, p_ref, mine_ref, theirs_ref, c_ref):
+def _gram_consensus_kernel(scale, rows, pieces, half_ref, a_ref, oh_ref, p_ref, mine_ref, *out_refs):
+    theirs_refs, c_mine_ref, c_theirs_ref = out_refs[:pieces], out_refs[pieces], out_refs[pieces + 1]
     j = pl.program_id(0)
     blk = p_ref[...]
     res = lax.dot_general(
         a_ref[...], blk, (((1,), (1,)), ((), ())), preferred_element_type=jnp.float32
     ) * scale
     mine_ref[...] = res[:rows]
-    theirs_ref[...] = res[rows:]
+    step = rows // pieces
+    for p, ref in enumerate(theirs_refs):
+        ref[...] = res[rows + p * step:rows + (p + 1) * step]
 
     @pl.when(j == 0)
     def _():
-        c_ref[...] = jnp.zeros_like(c_ref)
+        c_mine_ref[...] = jnp.zeros_like(c_mine_ref)
+        c_theirs_ref[...] = jnp.zeros_like(c_theirs_ref)
 
-    c_ref[...] += jnp.dot(oh_ref[...], blk, preferred_element_type=jnp.float32)
+    sums = jnp.dot(oh_ref[...], blk, preferred_element_type=jnp.float32)
+    heads = sums.shape[0] // 2
+    c_mine_ref[...] += sums[:heads]
+    c_theirs_ref[...] += sums[heads:]
 
 
-def gram_consensus(half, pair_rows, one_hot, gathered, block_rows=1024):
+def gram_consensus(half, pair_rows, one_hot, gathered, pieces=4, block_rows=1024):
     rows = pair_rows.shape[0] // 2
     bins = pair_rows.shape[1]
     total = gathered.shape[0]
     heads = one_hot.shape[0]
     steps = total // 2 // block_rows
+    step = rows // pieces
     flops = 2 * 2 * rows * (total // 2) * bins + 2 * heads * (total // 2) * bins
     bytes_accessed = 2 * (2 * rows * bins + heads * total // 2 + total // 2 * bins) + 4 * (
         2 * rows * total // 2 + heads * bins
@@ -43,20 +51,16 @@
             pl.BlockSpec((heads, block_rows), lambda j, h: (0, h[0] * steps + j)),
             pl.BlockSpec((block_rows, bins), lambda j, h: (h[0] * steps + j, 0)),
         ],
-        out_specs=[
-            pl.BlockSpec((rows, block_rows), lambda j, h: (0, h[0] * steps + j)),
-            pl.BlockSpec((rows, block_rows), lambda j, h: (0, j)),
-            pl.BlockSpec((heads, bins), lambda j, h: (0, 0)),
-        ],
+        out_specs=[pl.BlockSpec((rows, block_rows), lambda j, h: (0, h[0] * steps + j))]
+        + [pl.BlockSpec((step, block_rows), lambda j, h: (0, j)) for _ in range(pieces)]
+        + [pl.BlockSpec((heads // 2, bins), lambda j, h: (0, 0))] * 2,
     )
     return pl.pallas_call(
-        functools.partial(_gram_consensus_kernel, 1.0 / bins, rows),
+        functools.partial(_gram_consensus_kernel, 1.0 / bins, rows, pieces),
         grid_spec=grid_spec,
-        out_shape=[
-            jax.ShapeDtypeStruct((rows, total), jnp.float32),
-            jax.ShapeDtypeStruct((rows, total // 2), jnp.float32),
-            jax.ShapeDtypeStruct((heads, bins), jnp.float32),
-        ],
+        out_shape=[jax.ShapeDtypeStruct((rows, total), jnp.float32)]
+        + [jax.ShapeDtypeStruct((step, total // 2), jnp.float32) for _ in range(pieces)]
+        + [jax.ShapeDtypeStruct((heads // 2, bins), jnp.float32)] * 2,
         compiler_params=pltpu.CompilerParams(dimension_semantics=("arbitrary",)),
         cost_estimate=pl.CostEstimate(flops=flops, bytes_accessed=bytes_accessed, transcendentals=0),
     )(half, pair_rows, one_hot, gathered)
@@ -120,10 +124,13 @@
         + jnp.arange(2 * CL_DEV, dtype=jnp.int32) % CL_DEV
     )
     one_hot = (own_ids[:, None] == gathered_labels[None, :]).astype(jnp.bfloat16)
-    mine, theirs, sums = gram_consensus(half.reshape(1), pair_rows, one_hot, gathered)
-    returned = lax.ppermute(theirs, "tile", swap)
-    gram_tiles = lax.dynamic_update_slice(mine, returned, (0, (1 - half) * theirs.shape[1]))
-    consensus = sums[:CL_DEV] + lax.ppermute(sums[CL_DEV:], "tile", swap)
+    outs = gram_consensus(half.reshape(1), pair_rows, one_hot, gathered)
+    gram_tiles, theirs, sums_mine, sums_theirs = outs[0], outs[1:-2], outs[-2], outs[-1]
+    other = (1 - half) * (gathered.shape[0] // 2)
+    for p, piece in enumerate(theirs):
+        returned = lax.ppermute(piece, "tile", swap)
+        gram_tiles = lax.dynamic_update_slice(gram_tiles, returned, (p * piece.shape[0], other))
+    consensus = sums_mine + lax.ppermute(sums_theirs, "tile", swap)
     return (gram_tiles, consensus)
 
 

time: 231 us -> 231 us (level)
  transfers between devices with their start and end apart: 16 -> 19, of which waited for: 5 -> 5; matrix products, arithmetic and copies ran while one was open for 3% -> 4% of each run, Pallas kernels for 0% -> 0%
where the time goes in v10:
time: 231 us
  blocking collectives  131 us (57%)
  waiting for transfers between devices  30 us (13%)
  starting transfers between devices  20.3 us (9%)
  Pallas kernels  18.9 us (8%)
  between operations  14.9 us (6%)
  other arithmetic  8.37 us (4%)
  local copies, waits for them, and re-layouts  6.96 us (3%)
    unnamed x1, blocking collectives  131 us
    pallas_call x1, Pallas kernels, gram_consensus(): pl.pallas_call(functools.partial(_gram_consensus_kernel, 1.0 / bins, rows...  18.9 us
    all_gather x1, waiting for transfers between devices, shards(): gathered = lax.all_gather(arrived, 'tile', axis=0, tiled=True)  16.4 us
    ppermute x4, waiting for transfers between devices, exchange_over_mass(): first = lax.ppermute(lax.ppermute(far[:half], 'mass', ahead), 'mass', ahead)  11.6 us
    ppermute x2, starting transfers between devices, exchange_over_mass(): from_ahead = lax.ppermute(pieces[(me - 1) % mass_count], 'mass', behind)  5.17 us
  transfers between devices with their start and end apart: 19, of which 5 were waited for; matrix products, arithmetic and copies ran while one was open for 4% of the time, Pallas kernels for 0%

profile of v10, /device:TPU:1, one launch (start us, length us, event | category | flops | bytes accessed | tf_op | source)
XLA Modules:
  0.0 230.6 jit_solution(16105118687699659462)
XLA Ops:
  7.2 0.8 fusion.5
  8.2 0.8 select_reduce_fusion.1
  9.0 1.4 fusion
  10.4 0.7 multiply_add_fusion
  11.1 0.6 convolution_convert_fusion
  11.8 2.1 collective-permute-start.1
  13.9 1.3 collective-permute-start.3
  15.5 2.6 %collective-permute-start.5 = (bf16[48,4096]{1,0:T(8,128)(2,1)S(1)}, bf16[48,4096]{1,0:T(8,128)(2,1)S(1)}, u32[]{:S(2)}, u32[]{:S(2)}) collective-permute-start(bf16[48,4096]{1,0:T(8,128)(2,1)S(1)} %get-tuple-element.17), channel_id=1, source_target_pairs={{0,96},{32,0},{64,32},{96,64},{1,97},{33,1},{65,33},{97,65},{2,98}... | collective-permute-start | bytes 1179656 | tf_op jit(solution)/shard_map/ppermute | solution.py:74
  18.1 1.3 collective-permute-done.1
  19.4 0.3 collective-permute-start.2
  19.7 2.4 %collective-permute-start.4 = (bf16[24,4096]{1,0:T(8,128)(2,1)S(1)}, bf16[24,4096]{1,0:T(8,128)(2,1)S(1)}, u32[]{:S(2)}, u32[]{:S(2)}) collective-permute-start(bf16[24,4096]{1,0:T(8,128)(2,1)S(1)} %collective-permute-done.3), channel_id=1, source_target_pairs={{0,96},{32,0},{64,32},{96,64},{1,97},{33,1},{65,33},{97,65},{2,98}... | collective-permute-start | bytes 589832 | tf_op jit(solution)/shard_map/ppermute | solution.py:78
  22.1 9.9 %collective-permute-done.2 = bf16[24,4096]{1,0:T(8,128)(2,1)S(1)} collective-permute-done((bf16[24,4096]{1,0:T(8,128)(2,1)S(1)}, bf16[24,4096]{1,0:T(8,128)(2,1)S(1)}, u32[]{:S(2)}, u32[]{:S(2)}) %collective-permute-start.2) | collective-permute-done | bytes 196640 | tf_op jit(solution)/shard_map/ppermute | solution.py:77
  32.3 1.8 gather_fusion
  34.4 2.6 %collective-permute-start.10 = (s32[24]{0:T(128)S(1)}, s32[24]{0:T(128)S(1)}, u32[]{:S(2)}, u32[]{:S(2)}) collective-permute-start(s32[24]{0:T(128)S(1)} %get-tuple-element.26), channel_id=1, source_target_pairs={{0,96},{32,0},{64,32},{96,64},{1,97},{33,1},{65,33},{97,65},{2,98}... | collective-permute-start | bytes 296 | tf_op jit(solution)/shard_map/ppermute | solution.py:78
  37.1 2.6 %collective-permute-start.12 = (s32[48]{0:T(128)S(1)}, s32[48]{0:T(128)S(1)}, u32[]{:S(2)}, u32[]{:S(2)}) collective-permute-start(s32[48]{0:T(128)S(1)} %get-tuple-element.22), channel_id=1, source_target_pairs={{0,96},{32,0},{64,32},{96,64},{1,97},{33,1},{65,33},{97,65},{2,98}... | collective-permute-start | bytes 584 | tf_op jit(solution)/shard_map/ppermute | solution.py:74
  39.7 0.6 dynamic-slice
  41.0 1.5 collective-permute-start.11
  42.5 3.2 %collective-permute-start.6 = (bf16[192,4096]{1,0:T(8,128)(2,1)S(1)}, bf16[192,4096]{1,0:T(8,128)(2,1)S(1)}, u32[]{:S(2)}, u32[]{:S(2)}) collective-permute-start(bf16[192,4096]{1,0:T(8,128)(2,1)S(1)} %bitcast.34), channel_id=1, source_target_pairs={{0,1},{1,0},{2,3},{3,2},{4,5},{5,4},{6,7},{7,6},{8,9},{9,8},{10,11... | collective-permute-start | bytes 4718600 | tf_op jit(solution)/shard_map/ppermute | solution.py:118
  45.8 0.4 collective-permute-done.9
  46.2 0.6 gather_fusion.1
  47.1 130.5 %all-reduce = s32[6144]{0:T(1024)S(1)} all-reduce(s32[6144]{0:T(1024)S(1)} %dynamic-update-slice), channel_id=1, replica_groups=mesh['mass'=4,'tile'=32] {'tile'}, use_global_device_ids=true, to_apply=%add | all-reduce | flops 6144 | bytes 49152
  177.7 0.7 compare_convert_fusion.oh_ref
  178.4 1.9 pad_maximum_fusion.a_ref
  180.2 16.4 %all-gather.2.cloned.1.call-done.p_ref = bf16[6144,4096]{1,0:T(8,128)(2,1)} async-done(((bf16[192,4096]{1,0:T(8,128)(2,1)}), bf16[6144,4096]{1,0:T(8,128)(2,1)}) %all-gather.2.cloned.1.call-update) | async-done | bytes 50331664 | tf_op jit(solution)/shard_map/all_gather | solution.py:113
  196.7 18.9 %shard_map.50 = (f32[192,6144]{1,0:T(8,128)}, f32[48,3072]{1,0:T(8,128)}, f32[48,3072]{1,0:T(8,128)}, f32[48,3072]{1,0:T(8,128)}, f32[48,3072]{1,0:T(8,128)}, /*index=5*/f32[4,4096]{1,0:T(4,128)}, f32[4,4096]{1,0:T(4,128)}) custom-call(s32[1]{0:T(128)} %bitcast.half_ref, bf16[384,4096]{1,0:T(8,128)(2,1)} %pad_maximum_fusion.a_ref, ...), custom_call_target="tpu_custom_call" | custom-call | flops 9865003008 | bytes 33210368 | tf_op jit(solution)/shard_map/pallas_call | solution.py:58
  215.6 0.3 collective-permute-start.13
  217.0 1.9 collective-permute-done.17
  218.9 1.5 add.145
  220.3 0.9 constant_dynamic-update-slice_fusion
  221.2 0.9 constant_dynamic-update-slice_fusion.3
  222.1 0.9 constant_dynamic-update-slice_fusion.2
  222.9 0.9 constant_dynamic-update-slice_fusion.1
  (48 shorter events, 2.6 us)
Async XLA Ops:
  7.2 4.0 %copy-start.1 = (bf16[96,4096]{1,0:T(8,128)(2,1)S(1)}, bf16[96,4096]{1,0:T(8,128)(2,1)}, u32[]{:S(2)}) copy-start(bf16[96,4096]{1,0:T(8,128)(2,1)} %param.3) | copy-start | bytes 2359300
  7.2 189.5 %all-gather.2.cloned.1.call-start = ((), (), s32[]{:S(2)}) async-start(), calls=%async_computation | async-start | bytes 51904512 | tf_op jit(solution)/shard_map/all_gather | solution.py:113
  11.8 7.6 %collective-permute-start.1 = (bf16[24,4096]{1,0:T(8,128)(2,1)S(1)}, bf16[24,4096]{1,0:T(8,128)(2,1)S(1)}, u32[]{:S(2)}, u32[]{:S(2)}) collective-permute-start(bf16[24,4096]{1,0:T(8,128)(2,1)S(1)} %get-tuple-element.19), channel_id=1, source_target_pairs={{0,32},{32,64},{64,96},{96,0},{1,33},{33,65},{65,97},{97,1},{2,34}... | collective-permute-start | bytes 589832 | tf_op jit(solution)/shard_map/ppermute | solution.py:77
  13.9 5.8 %collective-permute-start.3 = (bf16[24,4096]{1,0:T(8,128)(2,1)S(1)}, bf16[24,4096]{1,0:T(8,128)(2,1)S(1)}, u32[]{:S(2)}, u32[]{:S(2)}) collective-permute-start(bf16[24,4096]{1,0:T(8,128)(2,1)S(1)} %get-tuple-element.20), channel_id=1, source_target_pairs={{0,96},{32,0},{64,32},{96,64},{1,97},{33,1},{65,33},{97,65},{2,98}... | collective-permute-start | bytes 589832 | tf_op jit(solution)/shard_map/ppermute | solution.py:78
  15.3 16.8 %collective-permute-start = (bf16[48,4096]{1,0:T(8,128)(2,1)S(1)}, bf16[48,4096]{1,0:T(8,128)(2,1)S(1)}, u32[]{:S(2)}, u32[]{:S(2)}) collective-permute-start(bf16[48,4096]{1,0:T(8,128)(2,1)S(1)} %get-tuple-element.18), channel_id=1, source_target_pairs={{0,32},{32,64},{64,96},{96,0},{1,33},{33,65},{65,97},{97,1},{2,34}... | collective-permute-start | bytes 1179656 | tf_op jit(solution)/shard_map/ppermute | solution.py:73
  15.5 16.6 %collective-permute-start.5 = (bf16[48,4096]{1,0:T(8,128)(2,1)S(1)}, bf16[48,4096]{1,0:T(8,128)(2,1)S(1)}, u32[]{:S(2)}, u32[]{:S(2)}) collective-permute-start(bf16[48,4096]{1,0:T(8,128)(2,1)S(1)} %get-tuple-element.17), channel_id=1, source_target_pairs={{0,96},{32,0},{64,32},{96,64},{1,97},{33,1},{65,33},{97,65},{2,98}... | collective-permute-start | bytes 1179656 | tf_op jit(solution)/shard_map/ppermute | solution.py:74
  19.4 12.6 %collective-permute-start.2 = (bf16[24,4096]{1,0:T(8,128)(2,1)S(1)}, bf16[24,4096]{1,0:T(8,128)(2,1)S(1)}, u32[]{:S(2)}, u32[]{:S(2)}) collective-permute-start(bf16[24,4096]{1,0:T(8,128)(2,1)S(1)} %collective-permute-done.1), channel_id=1, source_target_pairs={{0,32},{32,64},{64,96},{96,0},{1,33},{33,65},{65,97},{97,1},{2,34}... | collective-permute-start | bytes 589832 | tf_op jit(solution)/shard_map/ppermute | solution.py:77
  19.7 12.4 %collective-permute-start.4 = (bf16[24,4096]{1,0:T(8,128)(2,1)S(1)}, bf16[24,4096]{1,0:T(8,128)(2,1)S(1)}, u32[]{:S(2)}, u32[]{:S(2)}) collective-permute-start(bf16[24,4096]{1,0:T(8,128)(2,1)S(1)} %collective-permute-done.3), channel_id=1, source_target_pairs={{0,96},{32,0},{64,32},{96,64},{1,97},{33,1},{65,33},{97,65},{2,98}... | collective-permute-start | bytes 589832 | tf_op jit(solution)/shard_map/ppermute | solution.py:78
  34.1 5.6 %copy-start.2 = (u32[128]{0:T(128)S(1)}, u32[128]{0:T(128)}, u32[]{:S(2)}) copy-start(u32[128]{0:T(128)} %constant.106) | copy-start | bytes 1540
  34.1 8.4 %copy-start = (bf16[4,48,4096]{2,1,0:T(8,128)(2,1)S(1)}, bf16[4,48,4096]{2,1,0:T(8,128)(2,1)}, u32[]{:S(2)}) copy-start(bf16[4,48,4096]{2,1,0:T(8,128)(2,1)} %gather_fusion) | copy-start | bytes 4718596
  34.4 6.6 %collective-permute-start.10 = (s32[24]{0:T(128)S(1)}, s32[24]{0:T(128)S(1)}, u32[]{:S(2)}, u32[]{:S(2)}) collective-permute-start(s32[24]{0:T(128)S(1)} %get-tuple-element.26), channel_id=1, source_target_pairs={{0,96},{32,0},{64,32},{96,64},{1,97},{33,1},{65,33},{97,65},{2,98}... | collective-permute-start | bytes 296 | tf_op jit(solution)/shard_map/ppermute | solution.py:78
  37.0 5.5 %collective-permute-start.8 = (s32[24]{0:T(128)S(1)}, s32[24]{0:T(128)S(1)}, u32[]{:S(2)}, u32[]{:S(2)}) collective-permute-start(s32[24]{0:T(128)S(1)} %get-tuple-element.25), channel_id=1, source_target_pairs={{0,32},{32,64},{64,96},{96,0},{1,33},{33,65},{65,97},{97,1},{2,34}... | collective-permute-start | bytes 296 | tf_op jit(solution)/shard_map/ppermute | solution.py:77
  37.0 9.2 %collective-permute-start.7 = (s32[48]{0:T(128)S(1)}, s32[48]{0:T(128)S(1)}, u32[]{:S(2)}, u32[]{:S(2)}) collective-permute-start(s32[48]{0:T(128)S(1)} %get-tuple-element.24), channel_id=1, source_target_pairs={{0,32},{32,64},{64,96},{96,0},{1,33},{33,65},{65,97},{97,1},{2,34}... | collective-permute-start | bytes 584 | tf_op jit(solution)/shard_map/ppermute | solution.py:73
  37.1 9.1 %collective-permute-start.12 = (s32[48]{0:T(128)S(1)}, s32[48]{0:T(128)S(1)}, u32[]{:S(2)}, u32[]{:S(2)}) collective-permute-start(s32[48]{0:T(128)S(1)} %get-tuple-element.22), channel_id=1, source_target_pairs={{0,96},{32,0},{64,32},{96,64},{1,97},{33,1},{65,33},{97,65},{2,98}... | collective-permute-start | bytes 584 | tf_op jit(solution)/shard_map/ppermute | solution.py:74
  41.0 4.8 %collective-permute-start.11 = (s32[24]{0:T(128)S(1)}, s32[24]{0:T(128)S(1)}, u32[]{:S(2)}, u32[]{:S(2)}) collective-permute-start(s32[24]{0:T(128)S(1)} %collective-permute-done.10), channel_id=1, source_target_pairs={{0,96},{32,0},{64,32},{96,64},{1,97},{33,1},{65,33},{97,65},{2,98}... | collective-permute-start | bytes 296 | tf_op jit(solution)/shard_map/ppermute | solution.py:78
  42.5 3.6 %collective-permute-start.9 = (s32[24]{0:T(128)S(1)}, s32[24]{0:T(128)S(1)}, u32[]{:S(2)}, u32[]{:S(2)}) collective-permute-start(s32[24]{0:T(128)S(1)} %collective-permute-done.8), channel_id=1, source_target_pairs={{0,32},{32,64},{64,96},{96,0},{1,33},{33,65},{65,97},{97,1},{2,34}... | collective-permute-start | bytes 296 | tf_op jit(solution)/shard_map/ppermute | solution.py:77
  42.5 135.8 %collective-permute-start.6 = (bf16[192,4096]{1,0:T(8,128)(2,1)S(1)}, bf16[192,4096]{1,0:T(8,128)(2,1)S(1)}, u32[]{:S(2)}, u32[]{:S(2)}) collective-permute-start(bf16[192,4096]{1,0:T(8,128)(2,1)S(1)} %bitcast.34), channel_id=1, source_target_pairs={{0,1},{1,0},{2,3},{3,2},{4,5},{5,4},{6,7},{7,6},{8,9},{9,8},{10,11... | collective-permute-start | bytes 4718600 | tf_op jit(solution)/shard_map/ppermute | solution.py:118
  215.6 4.7 %collective-permute-start.13 = (f32[48,3072]{1,0:T(8,128)}, f32[48,3072]{1,0:T(8,128)S(1)}, u32[]{:S(2)}, u32[]{:S(2)}) collective-permute-start(f32[48,3072]{1,0:T(8,128)} %get-tuple-element.10), channel_id=1, source_target_pairs={{0,1},{1,0},{2,3},{3,2},{4,5},{5,4},{6,7},{7,6},{8,9},{9,8},{10,11... | collective-permute-start | bytes 1769480 | tf_op jit(solution)/shard_map/ppermute | solution.py:131
  216.0 5.2 %collective-permute-start.14 = (f32[48,3072]{1,0:T(8,128)}, f32[48,3072]{1,0:T(8,128)S(1)}, u32[]{:S(2)}, u32[]{:S(2)}) collective-permute-start(f32[48,3072]{1,0:T(8,128)} %get-tuple-element.11), channel_id=1, source_target_pairs={{0,1},{1,0},{2,3},{3,2},{4,5},{5,4},{6,7},{7,6},{8,9},{9,8},{10,11... | collective-permute-start | bytes 1769480 | tf_op jit(solution)/shard_map/ppermute | solution.py:131
  216.2 2.6 %collective-permute-start.17 = (f32[4,4096]{1,0:T(4,128)}, f32[4,4096]{1,0:T(4,128)S(1)}, u32[]{:S(2)}, u32[]{:S(2)}) collective-permute-start(f32[4,4096]{1,0:T(4,128)} %get-tuple-element.15), channel_id=1, source_target_pairs={{0,1},{1,0},{2,3},{3,2},{4,5},{5,4},{6,7},{7,6},{8,9},{9,8},{10,11... | collective-permute-start | bytes 196616 | tf_op jit(solution)/shard_map/ppermute | solution.py:133
  216.5 5.6 %collective-permute-start.15 = (f32[48,3072]{1,0:T(8,128)}, f32[48,3072]{1,0:T(8,128)S(1)}, u32[]{:S(2)}, u32[]{:S(2)}) collective-permute-start(f32[48,3072]{1,0:T(8,128)} %get-tuple-element.12), channel_id=1, source_target_pairs={{0,1},{1,0},{2,3},{3,2},{4,5},{5,4},{6,7},{7,6},{8,9},{9,8},{10,11... | collective-permute-start | bytes 1769480 | tf_op jit(solution)/shard_map/ppermute | solution.py:131
  216.7 6.2 %collective-permute-start.16 = (f32[48,3072]{1,0:T(8,128)}, f32[48,3072]{1,0:T(8,128)S(1)}, u32[]{:S(2)}, u32[]{:S(2)}) collective-permute-start(f32[48,3072]{1,0:T(8,128)} %get-tuple-element.13), channel_id=1, source_target_pairs={{0,1},{1,0},{2,3},{3,2},{4,5},{5,4},{6,7},{7,6},{8,9},{9,8},{10,11... | collective-permute-start | bytes 1769480 | tf_op jit(solution)/shard_map/ppermute | solution.py:131
Sparse Core Ops, SparseCore 0:
  34.2 162.3 all-gather.1

commit v11 on v10

--- a/solution.py
+++ b/solution.py
@@ -70,14 +70,18 @@
     me = lax.axis_index("mass")
     ahead = [(i, (i + 1) % mass_count) for i in range(mass_count)]
     behind = [(i, (i - 1) % mass_count) for i in range(mass_count)]
-    from_behind = lax.ppermute(pieces[(me + 1) % mass_count], "mass", ahead)
-    from_ahead = lax.ppermute(pieces[(me - 1) % mass_count], "mass", behind)
     far = pieces[(me + 2) % mass_count]
-    half = far.shape[0] // 2
-    first = lax.ppermute(lax.ppermute(far[:half], "mass", ahead), "mass", ahead)
-    second = lax.ppermute(lax.ppermute(far[half:], "mass", behind), "mass", behind)
+    size, half = far.shape[0], far.shape[0] // 2
+    went_ahead = lax.ppermute(
+        jnp.concatenate([pieces[(me + 1) % mass_count], far[:half]]), "mass", ahead
+    )
+    went_behind = lax.ppermute(
+        jnp.concatenate([pieces[(me - 1) % mass_count], far[half:]]), "mass", behind
+    )
+    first = lax.ppermute(went_ahead[size:], "mass", ahead)
+    second = lax.ppermute(went_behind[size:], "mass", behind)
     opposite = jnp.concatenate([first, second], axis=0)
-    stacked = jnp.stack([pieces[me], from_behind, opposite, from_ahead])
+    stacked = jnp.stack([pieces[me], went_ahead[:size], opposite, went_behind[:size]])
     return stacked[(me - jnp.arange(mass_count)) % mass_count]
 
 

time: 231 us -> 234 us (1.013)
  waiting for transfers between devices: 30 us -> 36.1 us
  starting transfers between devices: 20.3 us -> 16.8 us
    ppermute x12 -> x8, waiting for transfers between devices: 11.6 us -> 15.8 us  [the longest x2 12.5 us: exchange_over_mass(): lax.ppermute(jnp.concatenate([pieces[(me + 1) % mass_count], far[:half]])...]
    ppermute x12 -> x8, starting transfers between devices: 15.7 us -> 11.6 us  [the longest x2 5.14 us: exchange_over_mass(): second = lax.ppermute(went_behind[size:], 'mass', behind)]
  transfers between devices with their start and end apart: 19 -> 15, of which waited for: 5 -> 4; matrix products, arithmetic and copies ran while one was open for 4% -> 4% of each run, Pallas kernels for 0% -> 0%
where the time goes in v11:
time: 234 us
  blocking collectives  131 us (56%)
  waiting for transfers between devices  36.1 us (15%)
  Pallas kernels  18.9 us (8%)
  starting transfers between devices  16.8 us (7%)
  between operations  14.9 us (6%)
  other arithmetic  8.66 us (4%)
  local copies, waits for them, and re-layouts  7.19 us (3%)
    unnamed x1, blocking collectives  131 us
    pallas_call x1, Pallas kernels, gram_consensus(): pl.pallas_call(functools.partial(_gram_consensus_kernel, 1.0 / bins, rows...  18.9 us
    all_gather x1, waiting for transfers between devices, shards(): gathered = lax.all_gather(arrived, 'tile', axis=0, tiled=True)  18.5 us
    ppermute x2, waiting for transfers between devices, exchange_over_mass(): lax.ppermute(jnp.concatenate([pieces[(me + 1) % mass_count], far[:half]])...  12.5 us
    ppermute x2, starting transfers between devices, exchange_over_mass(): second = lax.ppermute(went_behind[size:], 'mass', behind)  5.14 us
  transfers between devices with their start and end apart: 15, of which 4 were waited for; matrix products, arithmetic and copies ran while one was open for 4% of the time, Pallas kernels for 0%

profile of v11, /device:TPU:1, one launch (start us, length us, event | category | flops | bytes accessed | tf_op | source)
XLA Modules:
  0.0 233.9 jit_solution(14398163742985852984)
XLA Ops:
  7.3 0.8 fusion.5
  8.2 0.8 select_reduce_fusion.1
  9.0 1.4 fusion
  10.5 0.7 multiply_add_fusion
  11.1 0.6 convolution_convert_fusion
  12.0 2.1 collective-permute-start
  14.1 1.4 collective-permute-start.2
  15.5 12.5 %collective-permute-done = bf16[72,4096]{1,0:T(8,128)(2,1)S(1)} collective-permute-done((bf16[72,4096]{1,0:T(8,128)(2,1)S(1)}, bf16[72,4096]{1,0:T(8,128)(2,1)S(1)}, u32[]{:S(2)}, u32[]{:S(2)}) %collective-permute-start) | collective-permute-done | bytes 589856 | tf_op jit(solution)/shard_map/ppermute | solution.py:75
  28.0 0.3 collective-permute-start.1
  28.4 2.5 %collective-permute-start.3 = (bf16[24,4096]{1,0:T(8,128)(2,1)S(1)}, bf16[24,4096]{1,0:T(8,128)(2,1)S(1)}, u32[]{:S(2)}, u32[]{:S(2)}) collective-permute-start(bf16[24,4096]{1,0:T(8,128)(2,1)S(1)} %slice.70), channel_id=1, source_target_pairs={{0,96},{32,0},{64,32},{96,64},{1,97},{33,1},{65,33},{97,65},{2,98}... | collective-permute-start | bytes 589832 | tf_op jit(solution)/shard_map/ppermute | solution.py:82
  30.9 3.2 %collective-permute-done.1 = bf16[24,4096]{1,0:T(8,128)(2,1)S(1)} collective-permute-done((bf16[24,4096]{1,0:T(8,128)(2,1)S(1)}, bf16[24,4096]{1,0:T(8,128)(2,1)S(1)}, u32[]{:S(2)}, u32[]{:S(2)}) %collective-permute-start.1) | collective-permute-done | bytes 196640 | tf_op jit(solution)/shard_map/ppermute | solution.py:81
  34.4 1.8 gather_fusion
  36.6 0.3 collective-permute-start.5
  37.0 2.3 %collective-permute-start.7 = (s32[72]{0:T(128)S(1)}, s32[72]{0:T(128)S(1)}, u32[]{:S(2)}, u32[]{:S(2)}) collective-permute-start(s32[72]{0:T(128)S(1)} %pad_add_fusion.2), channel_id=1, source_target_pairs={{0,96},{32,0},{64,32},{96,64},{1,97},{33,1},{65,33},{97,65},{2,98}... | collective-permute-start | bytes 872 | tf_op jit(solution)/shard_map/ppermute | solution.py:78
  39.3 0.6 dynamic-slice
  40.8 2.7 %collective-permute-start.8 = (s32[24]{0:T(128)S(1)}, s32[24]{0:T(128)S(1)}, u32[]{:S(2)}, u32[]{:S(2)}) collective-permute-start(s32[24]{0:T(128)S(1)} %slice.62), channel_id=1, source_target_pairs={{0,96},{32,0},{64,32},{96,64},{1,97},{33,1},{65,33},{97,65},{2,98}... | collective-permute-start | bytes 296 | tf_op jit(solution)/shard_map/ppermute | solution.py:82
  43.4 3.8 %collective-permute-start.4 = (bf16[192,4096]{1,0:T(8,128)(2,1)S(1)}, bf16[192,4096]{1,0:T(8,128)(2,1)S(1)}, u32[]{:S(2)}, u32[]{:S(2)}) collective-permute-start(bf16[192,4096]{1,0:T(8,128)(2,1)S(1)} %bitcast.38), channel_id=1, source_target_pairs={{0,1},{1,0},{2,3},{3,2},{4,5},{5,4},{6,7},{7,6},{8,9},{9,8},{10,11... | collective-permute-start | bytes 4718600 | tf_op jit(solution)/shard_map/ppermute | solution.py:122
  47.4 0.6 gather_fusion.1
  48.3 130.5 %all-reduce = s32[6144]{0:T(1024)S(1)} all-reduce(s32[6144]{0:T(1024)S(1)} %dynamic-update-slice), channel_id=1, replica_groups=mesh['mass'=4,'tile'=32] {'tile'}, use_global_device_ids=true, to_apply=%add | all-reduce | flops 6144 | bytes 49152
  178.8 0.7 compare_convert_fusion.oh_ref
  179.5 1.9 pad_maximum_fusion.a_ref
  181.5 18.5 %all-gather.2.cloned.1.call-done.p_ref = bf16[6144,4096]{1,0:T(8,128)(2,1)} async-done(((bf16[192,4096]{1,0:T(8,128)(2,1)}), bf16[6144,4096]{1,0:T(8,128)(2,1)}) %all-gather.2.cloned.1.call-update) | async-done | bytes 50331664 | tf_op jit(solution)/shard_map/all_gather | solution.py:117
  199.9 18.9 %shard_map.50 = (f32[192,6144]{1,0:T(8,128)}, f32[48,3072]{1,0:T(8,128)}, f32[48,3072]{1,0:T(8,128)}, f32[48,3072]{1,0:T(8,128)}, f32[48,3072]{1,0:T(8,128)}, /*index=5*/f32[4,4096]{1,0:T(4,128)}, f32[4,4096]{1,0:T(4,128)}) custom-call(s32[1]{0:T(128)} %bitcast.half_ref, bf16[384,4096]{1,0:T(8,128)(2,1)} %pad_maximum_fusion.a_ref, ...), custom_call_target="tpu_custom_call" | custom-call | flops 9865003008 | bytes 33210368 | tf_op jit(solution)/shard_map/pallas_call | solution.py:58
  218.9 0.3 collective-permute-start.9
  219.2 0.3 collective-permute-start.10
  219.7 0.3 collective-permute-start.11
  220.2 1.9 collective-permute-done.13
  222.1 1.5 add.145
  223.6 0.9 constant_dynamic-update-slice_fusion
  224.4 0.9 constant_dynamic-update-slice_fusion.3
  225.3 0.9 constant_dynamic-update-slice_fusion.2
  226.2 0.9 constant_dynamic-update-slice_fusion.1
  (52 shorter events, 2.3 us)
Async XLA Ops:
  7.2 4.0 %copy-start.1 = (bf16[96,4096]{1,0:T(8,128)(2,1)S(1)}, bf16[96,4096]{1,0:T(8,128)(2,1)}, u32[]{:S(2)}) copy-start(bf16[96,4096]{1,0:T(8,128)(2,1)} %param.3) | copy-start | bytes 2359300
  7.2 192.7 %all-gather.2.cloned.1.call-start = ((), (), s32[]{:S(2)}) async-start(), calls=%async_computation | async-start | bytes 51904512 | tf_op jit(solution)/shard_map/all_gather | solution.py:117
  12.0 16.0 %collective-permute-start = (bf16[72,4096]{1,0:T(8,128)(2,1)S(1)}, bf16[72,4096]{1,0:T(8,128)(2,1)S(1)}, u32[]{:S(2)}, u32[]{:S(2)}) collective-permute-start(bf16[72,4096]{1,0:T(8,128)(2,1)S(1)} %pad_maximum_fusion.2), channel_id=1, source_target_pairs={{0,32},{32,64},{64,96},{96,0},{1,33},{33,65},{65,97},{97,1},{2,34}... | collective-permute-start | bytes 1769480 | tf_op jit(solution)/shard_map/ppermute | solution.py:75
  14.1 14.2 %collective-permute-start.2 = (bf16[72,4096]{1,0:T(8,128)(2,1)S(1)}, bf16[72,4096]{1,0:T(8,128)(2,1)S(1)}, u32[]{:S(2)}, u32[]{:S(2)}) collective-permute-start(bf16[72,4096]{1,0:T(8,128)(2,1)S(1)} %pad_maximum_fusion.3), channel_id=1, source_target_pairs={{0,96},{32,0},{64,32},{96,64},{1,97},{33,1},{65,33},{97,65},{2,98}... | collective-permute-start | bytes 1769480 | tf_op jit(solution)/shard_map/ppermute | solution.py:78
  28.0 6.1 %collective-permute-start.1 = (bf16[24,4096]{1,0:T(8,128)(2,1)S(1)}, bf16[24,4096]{1,0:T(8,128)(2,1)S(1)}, u32[]{:S(2)}, u32[]{:S(2)}) collective-permute-start(bf16[24,4096]{1,0:T(8,128)(2,1)S(1)} %slice.69), channel_id=1, source_target_pairs={{0,32},{32,64},{64,96},{96,0},{1,33},{33,65},{65,97},{97,1},{2,34}... | collective-permute-start | bytes 589832 | tf_op jit(solution)/shard_map/ppermute | solution.py:81
  28.4 5.8 %collective-permute-start.3 = (bf16[24,4096]{1,0:T(8,128)(2,1)S(1)}, bf16[24,4096]{1,0:T(8,128)(2,1)S(1)}, u32[]{:S(2)}, u32[]{:S(2)}) collective-permute-start(bf16[24,4096]{1,0:T(8,128)(2,1)S(1)} %slice.70), channel_id=1, source_target_pairs={{0,96},{32,0},{64,32},{96,64},{1,97},{33,1},{65,33},{97,65},{2,98}... | collective-permute-start | bytes 589832 | tf_op jit(solution)/shard_map/ppermute | solution.py:82
  36.2 3.2 %copy-start.2 = (u32[128]{0:T(128)S(1)}, u32[128]{0:T(128)}, u32[]{:S(2)}) copy-start(u32[128]{0:T(128)} %constant.106) | copy-start | bytes 1540
  36.2 7.3 %copy-start = (bf16[4,48,4096]{2,1,0:T(8,128)(2,1)S(1)}, bf16[4,48,4096]{2,1,0:T(8,128)(2,1)}, u32[]{:S(2)}) copy-start(bf16[4,48,4096]{2,1,0:T(8,128)(2,1)} %gather_fusion) | copy-start | bytes 4718596
  36.6 4.0 %collective-permute-start.5 = (s32[72]{0:T(128)S(1)}, s32[72]{0:T(128)S(1)}, u32[]{:S(2)}, u32[]{:S(2)}) collective-permute-start(s32[72]{0:T(128)S(1)} %pad_add_fusion.1), channel_id=1, source_target_pairs={{0,32},{32,64},{64,96},{96,0},{1,33},{33,65},{65,97},{97,1},{2,34}... | collective-permute-start | bytes 872 | tf_op jit(solution)/shard_map/ppermute | solution.py:75
  37.0 3.7 %collective-permute-start.7 = (s32[72]{0:T(128)S(1)}, s32[72]{0:T(128)S(1)}, u32[]{:S(2)}, u32[]{:S(2)}) collective-permute-start(s32[72]{0:T(128)S(1)} %pad_add_fusion.2), channel_id=1, source_target_pairs={{0,96},{32,0},{64,32},{96,64},{1,97},{33,1},{65,33},{97,65},{2,98}... | collective-permute-start | bytes 872 | tf_op jit(solution)/shard_map/ppermute | solution.py:78
  40.7 6.6 %collective-permute-start.6 = (s32[24]{0:T(128)S(1)}, s32[24]{0:T(128)S(1)}, u32[]{:S(2)}, u32[]{:S(2)}) collective-permute-start(s32[24]{0:T(128)S(1)} %slice.59), channel_id=1, source_target_pairs={{0,32},{32,64},{64,96},{96,0},{1,33},{33,65},{65,97},{97,1},{2,34}... | collective-permute-start | bytes 296 | tf_op jit(solution)/shard_map/ppermute | solution.py:81
  40.8 6.5 %collective-permute-start.8 = (s32[24]{0:T(128)S(1)}, s32[24]{0:T(128)S(1)}, u32[]{:S(2)}, u32[]{:S(2)}) collective-permute-start(s32[24]{0:T(128)S(1)} %slice.62), channel_id=1, source_target_pairs={{0,96},{32,0},{64,32},{96,64},{1,97},{33,1},{65,33},{97,65},{2,98}... | collective-permute-start | bytes 296 | tf_op jit(solution)/shard_map/ppermute | solution.py:82
  43.4 136.1 %collective-permute-start.4 = (bf16[192,4096]{1,0:T(8,128)(2,1)S(1)}, bf16[192,4096]{1,0:T(8,128)(2,1)S(1)}, u32[]{:S(2)}, u32[]{:S(2)}) collective-permute-start(bf16[192,4096]{1,0:T(8,128)(2,1)S(1)} %bitcast.38), channel_id=1, source_target_pairs={{0,1},{1,0},{2,3},{3,2},{4,5},{5,4},{6,7},{7,6},{8,9},{9,8},{10,11... | collective-permute-start | bytes 4718600 | tf_op jit(solution)/shard_map/ppermute | solution.py:122
  218.9 4.7 %collective-permute-start.9 = (f32[48,3072]{1,0:T(8,128)}, f32[48,3072]{1,0:T(8,128)S(1)}, u32[]{:S(2)}, u32[]{:S(2)}) collective-permute-start(f32[48,3072]{1,0:T(8,128)} %get-tuple-element.10), channel_id=1, source_target_pairs={{0,1},{1,0},{2,3},{3,2},{4,5},{5,4},{6,7},{7,6},{8,9},{9,8},{10,11... | collective-permute-start | bytes 1769480 | tf_op jit(solution)/shard_map/ppermute | solution.py:135
  219.2 5.2 %collective-permute-start.10 = (f32[48,3072]{1,0:T(8,128)}, f32[48,3072]{1,0:T(8,128)S(1)}, u32[]{:S(2)}, u32[]{:S(2)}) collective-permute-start(f32[48,3072]{1,0:T(8,128)} %get-tuple-element.11), channel_id=1, source_target_pairs={{0,1},{1,0},{2,3},{3,2},{4,5},{5,4},{6,7},{7,6},{8,9},{9,8},{10,11... | collective-permute-start | bytes 1769480 | tf_op jit(solution)/shard_map/ppermute | solution.py:135
  219.5 2.6 %collective-permute-start.13 = (f32[4,4096]{1,0:T(4,128)}, f32[4,4096]{1,0:T(4,128)S(1)}, u32[]{:S(2)}, u32[]{:S(2)}) collective-permute-start(f32[4,4096]{1,0:T(4,128)} %get-tuple-element.15), channel_id=1, source_target_pairs={{0,1},{1,0},{2,3},{3,2},{4,5},{5,4},{6,7},{7,6},{8,9},{9,8},{10,11... | collective-permute-start | bytes 196616 | tf_op jit(solution)/shard_map/ppermute | solution.py:137
  219.7 5.6 %collective-permute-start.11 = (f32[48,3072]{1,0:T(8,128)}, f32[48,3072]{1,0:T(8,128)S(1)}, u32[]{:S(2)}, u32[]{:S(2)}) collective-permute-start(f32[48,3072]{1,0:T(8,128)} %get-tuple-element.12), channel_id=1, source_target_pairs={{0,1},{1,0},{2,3},{3,2},{4,5},{5,4},{6,7},{7,6},{8,9},{9,8},{10,11... | collective-permute-start | bytes 1769480 | tf_op jit(solution)/shard_map/ppermute | solution.py:135
  220.0 6.2 %collective-permute-start.12 = (f32[48,3072]{1,0:T(8,128)}, f32[48,3072]{1,0:T(8,128)S(1)}, u32[]{:S(2)}, u32[]{:S(2)}) collective-permute-start(f32[48,3072]{1,0:T(8,128)} %get-tuple-element.13), channel_id=1, source_target_pairs={{0,1},{1,0},{2,3},{3,2},{4,5},{5,4},{6,7},{7,6},{8,9},{9,8},{10,11... | collective-permute-start | bytes 1769480 | tf_op jit(solution)/shard_map/ppermute | solution.py:135
Sparse Core Ops, SparseCore 0:
  36.3 163.5 all-gather.1

commit v12 on v10

--- a/solution.py
+++ b/solution.py
@@ -32,7 +32,7 @@
     c_theirs_ref[...] += sums[heads:]
 
 
-def gram_consensus(half, pair_rows, one_hot, gathered, pieces=4, block_rows=1024):
+def gram_consensus(half, pair_rows, one_hot, gathered, pieces=2, block_rows=1024):
     rows = pair_rows.shape[0] // 2
     bins = pair_rows.shape[1]
     total = gathered.shape[0]

time: 231 us -> 231 us (level)
  transfers between devices with their start and end apart: 19 -> 17, of which waited for: 5 -> 5; matrix products, arithmetic and copies ran while one was open for 4% -> 3% of each run, Pallas kernels for 0% -> 0%
where the time goes in v12:
time: 231 us
  blocking collectives  131 us (57%)
  waiting for transfers between devices  32.2 us (14%)
  starting transfers between devices  19.8 us (9%)
  Pallas kernels  18.9 us (8%)
  between operations  14.9 us (6%)
  other arithmetic  8.38 us (4%)
  local copies, waits for them, and re-layouts  5.73 us (2%)
    unnamed x1, blocking collectives  131 us
    pallas_call x1, Pallas kernels, gram_consensus(): pl.pallas_call(functools.partial(_gram_consensus_kernel, 1.0 / bins, rows...  18.9 us
    all_gather x1, waiting for transfers between devices, shards(): gathered = lax.all_gather(arrived, 'tile', axis=0, tiled=True)  16.4 us
    ppermute x4, waiting for transfers between devices, exchange_over_mass(): first = lax.ppermute(lax.ppermute(far[:half], 'mass', ahead), 'mass', ahead)  11.6 us
    ppermute x2, starting transfers between devices, exchange_over_mass(): from_ahead = lax.ppermute(pieces[(me - 1) % mass_count], 'mass', behind)  5.17 us
  transfers between devices with their start and end apart: 17, of which 5 were waited for; matrix products, arithmetic and copies ran while one was open for 3% of the time, Pallas kernels for 0%

profile of v12, /device:TPU:1, one launch (start us, length us, event | category | flops | bytes accessed | tf_op | source)
XLA Modules:
  0.0 231.0 jit_solution(7258086179661096294)
XLA Ops:
  7.2 0.8 fusion.5
  8.2 0.8 select_reduce_fusion.1
  9.0 1.4 fusion
  10.4 0.7 multiply_add_fusion
  11.1 0.6 convolution_convert_fusion
  11.8 2.1 collective-permute-start.1
  13.9 1.3 collective-permute-start.3
  15.5 2.6 %collective-permute-start.5 = (bf16[48,4096]{1,0:T(8,128)(2,1)S(1)}, bf16[48,4096]{1,0:T(8,128)(2,1)S(1)}, u32[]{:S(2)}, u32[]{:S(2)}) collective-permute-start(bf16[48,4096]{1,0:T(8,128)(2,1)S(1)} %get-tuple-element.13), channel_id=1, source_target_pairs={{0,96},{32,0},{64,32},{96,64},{1,97},{33,1},{65,33},{97,65},{2,98}... | collective-permute-start | bytes 1179656 | tf_op jit(solution)/shard_map/ppermute | solution.py:74
  18.1 1.3 collective-permute-done.1
  19.4 0.3 collective-permute-start.2
  19.7 2.4 %collective-permute-start.4 = (bf16[24,4096]{1,0:T(8,128)(2,1)S(1)}, bf16[24,4096]{1,0:T(8,128)(2,1)S(1)}, u32[]{:S(2)}, u32[]{:S(2)}) collective-permute-start(bf16[24,4096]{1,0:T(8,128)(2,1)S(1)} %collective-permute-done.3), channel_id=1, source_target_pairs={{0,96},{32,0},{64,32},{96,64},{1,97},{33,1},{65,33},{97,65},{2,98}... | collective-permute-start | bytes 589832 | tf_op jit(solution)/shard_map/ppermute | solution.py:78
  22.1 9.9 %collective-permute-done.2 = bf16[24,4096]{1,0:T(8,128)(2,1)S(1)} collective-permute-done((bf16[24,4096]{1,0:T(8,128)(2,1)S(1)}, bf16[24,4096]{1,0:T(8,128)(2,1)S(1)}, u32[]{:S(2)}, u32[]{:S(2)}) %collective-permute-start.2) | collective-permute-done | bytes 196640 | tf_op jit(solution)/shard_map/ppermute | solution.py:77
  32.3 1.8 gather_fusion
  34.4 2.6 %collective-permute-start.10 = (s32[24]{0:T(128)S(1)}, s32[24]{0:T(128)S(1)}, u32[]{:S(2)}, u32[]{:S(2)}) collective-permute-start(s32[24]{0:T(128)S(1)} %get-tuple-element.22), channel_id=1, source_target_pairs={{0,96},{32,0},{64,32},{96,64},{1,97},{33,1},{65,33},{97,65},{2,98}... | collective-permute-start | bytes 296 | tf_op jit(solution)/shard_map/ppermute | solution.py:78
  37.1 2.6 %collective-permute-start.12 = (s32[48]{0:T(128)S(1)}, s32[48]{0:T(128)S(1)}, u32[]{:S(2)}, u32[]{:S(2)}) collective-permute-start(s32[48]{0:T(128)S(1)} %get-tuple-element.18), channel_id=1, source_target_pairs={{0,96},{32,0},{64,32},{96,64},{1,97},{33,1},{65,33},{97,65},{2,98}... | collective-permute-start | bytes 584 | tf_op jit(solution)/shard_map/ppermute | solution.py:74
  39.7 0.6 dynamic-slice
  41.0 1.5 collective-permute-start.11
  42.5 3.2 %collective-permute-start.6 = (bf16[192,4096]{1,0:T(8,128)(2,1)S(1)}, bf16[192,4096]{1,0:T(8,128)(2,1)S(1)}, u32[]{:S(2)}, u32[]{:S(2)}) collective-permute-start(bf16[192,4096]{1,0:T(8,128)(2,1)S(1)} %bitcast.34), channel_id=1, source_target_pairs={{0,1},{1,0},{2,3},{3,2},{4,5},{5,4},{6,7},{7,6},{8,9},{9,8},{10,11... | collective-permute-start | bytes 4718600 | tf_op jit(solution)/shard_map/ppermute | solution.py:118
  45.8 0.4 collective-permute-done.9
  46.2 0.6 gather_fusion.1
  47.1 130.5 %all-reduce = s32[6144]{0:T(1024)S(1)} all-reduce(s32[6144]{0:T(1024)S(1)} %dynamic-update-slice), channel_id=1, replica_groups=mesh['mass'=4,'tile'=32] {'tile'}, use_global_device_ids=true, to_apply=%add | all-reduce | flops 6144 | bytes 49152
  177.7 0.7 compare_convert_fusion.oh_ref
  178.4 1.9 pad_maximum_fusion.a_ref
  180.2 16.4 %all-gather.2.cloned.1.call-done.p_ref = bf16[6144,4096]{1,0:T(8,128)(2,1)} async-done(((bf16[192,4096]{1,0:T(8,128)(2,1)}), bf16[6144,4096]{1,0:T(8,128)(2,1)}) %all-gather.2.cloned.1.call-update) | async-done | bytes 50331664 | tf_op jit(solution)/shard_map/all_gather | solution.py:113
  196.7 18.9 %shard_map.50 = (f32[192,6144]{1,0:T(8,128)}, f32[96,3072]{1,0:T(8,128)}, f32[96,3072]{1,0:T(8,128)}, f32[4,4096]{1,0:T(4,128)}, f32[4,4096]{1,0:T(4,128)}) custom-call(s32[1]{0:T(128)} %bitcast.half_ref, bf16[384,4096]{1,0:T(8,128)(2,1)} %pad_maximum_fusion.a_ref, bf16[8,6144]{1,0:T(8,128)(2,1)} %compare_convert_fusion.oh_ref, ...), custom_call_target="tpu_custom_call" | custom-call | flops 9865003008 | bytes 33210368 | tf_op jit(solution)/shard_map/pallas_call | solution.py:58
  215.6 0.3 collective-permute-start.13
  216.0 0.2 collective-permute-start.14
  216.2 0.3 collective-permute-start.15
  216.5 4.1 %collective-permute-done.15 = f32[4,4096]{1,0:T(4,128)S(1)} collective-permute-done((f32[4,4096]{1,0:T(4,128)}, f32[4,4096]{1,0:T(4,128)S(1)}, u32[]{:S(2)}, u32[]{:S(2)}) %collective-permute-start.15) | collective-permute-done | bytes 65568 | tf_op jit(solution)/shard_map/ppermute | solution.py:133
  220.5 1.5 add.143
  222.0 1.1 constant_dynamic-update-slice_fusion
  223.1 1.1 constant_dynamic-update-slice_fusion.1
  (42 shorter events, 1.6 us)
Async XLA Ops:
  7.2 4.0 %copy-start.1 = (bf16[96,4096]{1,0:T(8,128)(2,1)S(1)}, bf16[96,4096]{1,0:T(8,128)(2,1)}, u32[]{:S(2)}) copy-start(bf16[96,4096]{1,0:T(8,128)(2,1)} %param.3) | copy-start | bytes 2359300
  7.2 189.5 %all-gather.2.cloned.1.call-start = ((), (), s32[]{:S(2)}) async-start(), calls=%async_computation | async-start | bytes 51904512 | tf_op jit(solution)/shard_map/all_gather | solution.py:113
  11.8 7.6 %collective-permute-start.1 = (bf16[24,4096]{1,0:T(8,128)(2,1)S(1)}, bf16[24,4096]{1,0:T(8,128)(2,1)S(1)}, u32[]{:S(2)}, u32[]{:S(2)}) collective-permute-start(bf16[24,4096]{1,0:T(8,128)(2,1)S(1)} %get-tuple-element.15), channel_id=1, source_target_pairs={{0,32},{32,64},{64,96},{96,0},{1,33},{33,65},{65,97},{97,1},{2,34}... | collective-permute-start | bytes 589832 | tf_op jit(solution)/shard_map/ppermute | solution.py:77
  13.9 5.8 %collective-permute-start.3 = (bf16[24,4096]{1,0:T(8,128)(2,1)S(1)}, bf16[24,4096]{1,0:T(8,128)(2,1)S(1)}, u32[]{:S(2)}, u32[]{:S(2)}) collective-permute-start(bf16[24,4096]{1,0:T(8,128)(2,1)S(1)} %get-tuple-element.16), channel_id=1, source_target_pairs={{0,96},{32,0},{64,32},{96,64},{1,97},{33,1},{65,33},{97,65},{2,98}... | collective-permute-start | bytes 589832 | tf_op jit(solution)/shard_map/ppermute | solution.py:78
  15.3 16.8 %collective-permute-start = (bf16[48,4096]{1,0:T(8,128)(2,1)S(1)}, bf16[48,4096]{1,0:T(8,128)(2,1)S(1)}, u32[]{:S(2)}, u32[]{:S(2)}) collective-permute-start(bf16[48,4096]{1,0:T(8,128)(2,1)S(1)} %get-tuple-element.14), channel_id=1, source_target_pairs={{0,32},{32,64},{64,96},{96,0},{1,33},{33,65},{65,97},{97,1},{2,34}... | collective-permute-start | bytes 1179656 | tf_op jit(solution)/shard_map/ppermute | solution.py:73
  15.5 16.6 %collective-permute-start.5 = (bf16[48,4096]{1,0:T(8,128)(2,1)S(1)}, bf16[48,4096]{1,0:T(8,128)(2,1)S(1)}, u32[]{:S(2)}, u32[]{:S(2)}) collective-permute-start(bf16[48,4096]{1,0:T(8,128)(2,1)S(1)} %get-tuple-element.13), channel_id=1, source_target_pairs={{0,96},{32,0},{64,32},{96,64},{1,97},{33,1},{65,33},{97,65},{2,98}... | collective-permute-start | bytes 1179656 | tf_op jit(solution)/shard_map/ppermute | solution.py:74
  19.4 12.6 %collective-permute-start.2 = (bf16[24,4096]{1,0:T(8,128)(2,1)S(1)}, bf16[24,4096]{1,0:T(8,128)(2,1)S(1)}, u32[]{:S(2)}, u32[]{:S(2)}) collective-permute-start(bf16[24,4096]{1,0:T(8,128)(2,1)S(1)} %collective-permute-done.1), channel_id=1, source_target_pairs={{0,32},{32,64},{64,96},{96,0},{1,33},{33,65},{65,97},{97,1},{2,34}... | collective-permute-start | bytes 589832 | tf_op jit(solution)/shard_map/ppermute | solution.py:77
  19.7 12.4 %collective-permute-start.4 = (bf16[24,4096]{1,0:T(8,128)(2,1)S(1)}, bf16[24,4096]{1,0:T(8,128)(2,1)S(1)}, u32[]{:S(2)}, u32[]{:S(2)}) collective-permute-start(bf16[24,4096]{1,0:T(8,128)(2,1)S(1)} %collective-permute-done.3), channel_id=1, source_target_pairs={{0,96},{32,0},{64,32},{96,64},{1,97},{33,1},{65,33},{97,65},{2,98}... | collective-permute-start | bytes 589832 | tf_op jit(solution)/shard_map/ppermute | solution.py:78
  34.1 5.6 %copy-start.2 = (u32[128]{0:T(128)S(1)}, u32[128]{0:T(128)}, u32[]{:S(2)}) copy-start(u32[128]{0:T(128)} %constant.103) | copy-start | bytes 1540
  34.1 8.4 %copy-start = (bf16[4,48,4096]{2,1,0:T(8,128)(2,1)S(1)}, bf16[4,48,4096]{2,1,0:T(8,128)(2,1)}, u32[]{:S(2)}) copy-start(bf16[4,48,4096]{2,1,0:T(8,128)(2,1)} %gather_fusion) | copy-start | bytes 4718596
  34.4 6.6 %collective-permute-start.10 = (s32[24]{0:T(128)S(1)}, s32[24]{0:T(128)S(1)}, u32[]{:S(2)}, u32[]{:S(2)}) collective-permute-start(s32[24]{0:T(128)S(1)} %get-tuple-element.22), channel_id=1, source_target_pairs={{0,96},{32,0},{64,32},{96,64},{1,97},{33,1},{65,33},{97,65},{2,98}... | collective-permute-start | bytes 296 | tf_op jit(solution)/shard_map/ppermute | solution.py:78
  37.0 5.5 %collective-permute-start.8 = (s32[24]{0:T(128)S(1)}, s32[24]{0:T(128)S(1)}, u32[]{:S(2)}, u32[]{:S(2)}) collective-permute-start(s32[24]{0:T(128)S(1)} %get-tuple-element.21), channel_id=1, source_target_pairs={{0,32},{32,64},{64,96},{96,0},{1,33},{33,65},{65,97},{97,1},{2,34}... | collective-permute-start | bytes 296 | tf_op jit(solution)/shard_map/ppermute | solution.py:77
  37.0 9.2 %collective-permute-start.7 = (s32[48]{0:T(128)S(1)}, s32[48]{0:T(128)S(1)}, u32[]{:S(2)}, u32[]{:S(2)}) collective-permute-start(s32[48]{0:T(128)S(1)} %get-tuple-element.20), channel_id=1, source_target_pairs={{0,32},{32,64},{64,96},{96,0},{1,33},{33,65},{65,97},{97,1},{2,34}... | collective-permute-start | bytes 584 | tf_op jit(solution)/shard_map/ppermute | solution.py:73
  37.1 9.1 %collective-permute-start.12 = (s32[48]{0:T(128)S(1)}, s32[48]{0:T(128)S(1)}, u32[]{:S(2)}, u32[]{:S(2)}) collective-permute-start(s32[48]{0:T(128)S(1)} %get-tuple-element.18), channel_id=1, source_target_pairs={{0,96},{32,0},{64,32},{96,64},{1,97},{33,1},{65,33},{97,65},{2,98}... | collective-permute-start | bytes 584 | tf_op jit(solution)/shard_map/ppermute | solution.py:74
  41.0 4.8 %collective-permute-start.11 = (s32[24]{0:T(128)S(1)}, s32[24]{0:T(128)S(1)}, u32[]{:S(2)}, u32[]{:S(2)}) collective-permute-start(s32[24]{0:T(128)S(1)} %collective-permute-done.10), channel_id=1, source_target_pairs={{0,96},{32,0},{64,32},{96,64},{1,97},{33,1},{65,33},{97,65},{2,98}... | collective-permute-start | bytes 296 | tf_op jit(solution)/shard_map/ppermute | solution.py:78
  42.5 3.6 %collective-permute-start.9 = (s32[24]{0:T(128)S(1)}, s32[24]{0:T(128)S(1)}, u32[]{:S(2)}, u32[]{:S(2)}) collective-permute-start(s32[24]{0:T(128)S(1)} %collective-permute-done.8), channel_id=1, source_target_pairs={{0,32},{32,64},{64,96},{96,0},{1,33},{33,65},{65,97},{97,1},{2,34}... | collective-permute-start | bytes 296 | tf_op jit(solution)/shard_map/ppermute | solution.py:77
  42.5 135.8 %collective-permute-start.6 = (bf16[192,4096]{1,0:T(8,128)(2,1)S(1)}, bf16[192,4096]{1,0:T(8,128)(2,1)S(1)}, u32[]{:S(2)}, u32[]{:S(2)}) collective-permute-start(bf16[192,4096]{1,0:T(8,128)(2,1)S(1)} %bitcast.34), channel_id=1, source_target_pairs={{0,1},{1,0},{2,3},{3,2},{4,5},{5,4},{6,7},{7,6},{8,9},{9,8},{10,11... | collective-permute-start | bytes 4718600 | tf_op jit(solution)/shard_map/ppermute | solution.py:118
  215.6 6.4 %collective-permute-start.13 = (f32[96,3072]{1,0:T(8,128)}, f32[96,3072]{1,0:T(8,128)S(1)}, u32[]{:S(2)}, u32[]{:S(2)}) collective-permute-start(f32[96,3072]{1,0:T(8,128)} %get-tuple-element.8), channel_id=1, source_target_pairs={{0,1},{1,0},{2,3},{3,2},{4,5},{5,4},{6,7},{7,6},{8,9},{9,8},{10,11... | collective-permute-start | bytes 3538952 | tf_op jit(solution)/shard_map/ppermute | solution.py:131
  216.0 7.2 %collective-permute-start.14 = (f32[96,3072]{1,0:T(8,128)}, f32[96,3072]{1,0:T(8,128)S(1)}, u32[]{:S(2)}, u32[]{:S(2)}) collective-permute-start(f32[96,3072]{1,0:T(8,128)} %get-tuple-element.9), channel_id=1, source_target_pairs={{0,1},{1,0},{2,3},{3,2},{4,5},{5,4},{6,7},{7,6},{8,9},{9,8},{10,11... | collective-permute-start | bytes 3538952 | tf_op jit(solution)/shard_map/ppermute | solution.py:131
  216.2 4.3 %collective-permute-start.15 = (f32[4,4096]{1,0:T(4,128)}, f32[4,4096]{1,0:T(4,128)S(1)}, u32[]{:S(2)}, u32[]{:S(2)}) collective-permute-start(f32[4,4096]{1,0:T(4,128)} %get-tuple-element.11), channel_id=1, source_target_pairs={{0,1},{1,0},{2,3},{3,2},{4,5},{5,4},{6,7},{7,6},{8,9},{9,8},{10,11... | collective-permute-start | bytes 196616 | tf_op jit(solution)/shard_map/ppermute | solution.py:133
Sparse Core Ops, SparseCore 0:
  34.2 162.3 all-gather.1

commit v13 on v10

--- a/solution.py
+++ b/solution.py
@@ -130,7 +130,10 @@
     for p, piece in enumerate(theirs):
         returned = lax.ppermute(piece, "tile", swap)
         gram_tiles = lax.dynamic_update_slice(gram_tiles, returned, (p * piece.shape[0], other))
-    consensus = sums_mine + lax.ppermute(sums_theirs, "tile", swap)
+    gram_tiles, from_partner = lax.optimization_barrier(
+        (gram_tiles, lax.ppermute(sums_theirs, "tile", swap))
+    )
+    consensus = sums_mine + from_partner
     return (gram_tiles, consensus)
 
 

time: 231 us -> 229 us (level)
  transfers between devices with their start and end apart: 19 -> 19, of which waited for: 5 -> 5; matrix products, arithmetic and copies ran while one was open for 4% -> 3% of each run, Pallas kernels for 0% -> 0%
where the time goes in v13:
time: 229 us
  blocking collectives  131 us (57%)
  waiting for transfers between devices  29.1 us (13%)
  starting transfers between devices  20.3 us (9%)
  Pallas kernels  18.9 us (8%)
  between operations  14.9 us (7%)
  other arithmetic  7.54 us (3%)
  local copies, waits for them, and re-layouts  6.96 us (3%)
    unnamed x1, blocking collectives  131 us
    pallas_call x1, Pallas kernels, gram_consensus(): pl.pallas_call(functools.partial(_gram_consensus_kernel, 1.0 / bins, rows...  18.9 us
    all_gather x1, waiting for transfers between devices, shards(): gathered = lax.all_gather(arrived, 'tile', axis=0, tiled=True)  16.4 us
    ppermute x4, waiting for transfers between devices, exchange_over_mass(): first = lax.ppermute(lax.ppermute(far[:half], 'mass', ahead), 'mass', ahead)  11.6 us
    ppermute x2, starting transfers between devices, exchange_over_mass(): from_ahead = lax.ppermute(pieces[(me - 1) % mass_count], 'mass', behind)  5.17 us
  transfers between devices with their start and end apart: 19, of which 5 were waited for; matrix products, arithmetic and copies ran while one was open for 3% of the time, Pallas kernels for 0%

profile of v13, /device:TPU:1, one launch (start us, length us, event | category | flops | bytes accessed | tf_op | source)
XLA Modules:
  0.0 228.8 jit_solution(4483482480486510305)
XLA Ops:
  7.2 0.8 fusion.5
  8.2 0.8 select_reduce_fusion.1
  9.0 1.4 fusion
  10.4 0.7 multiply_add_fusion
  11.1 0.6 convolution_convert_fusion
  11.8 2.1 collective-permute-start.1
  13.9 1.3 collective-permute-start.3
  15.5 2.6 %collective-permute-start.5 = (bf16[48,4096]{1,0:T(8,128)(2,1)S(1)}, bf16[48,4096]{1,0:T(8,128)(2,1)S(1)}, u32[]{:S(2)}, u32[]{:S(2)}) collective-permute-start(bf16[48,4096]{1,0:T(8,128)(2,1)S(1)} %get-tuple-element.21), channel_id=1, source_target_pairs={{0,96},{32,0},{64,32},{96,64},{1,97},{33,1},{65,33},{97,65},{2,98}... | collective-permute-start | bytes 1179656 | tf_op jit(solution)/shard_map/ppermute | solution.py:74
  18.1 1.3 collective-permute-done.1
  19.4 0.3 collective-permute-start.2
  19.7 2.4 %collective-permute-start.4 = (bf16[24,4096]{1,0:T(8,128)(2,1)S(1)}, bf16[24,4096]{1,0:T(8,128)(2,1)S(1)}, u32[]{:S(2)}, u32[]{:S(2)}) collective-permute-start(bf16[24,4096]{1,0:T(8,128)(2,1)S(1)} %collective-permute-done.3), channel_id=1, source_target_pairs={{0,96},{32,0},{64,32},{96,64},{1,97},{33,1},{65,33},{97,65},{2,98}... | collective-permute-start | bytes 589832 | tf_op jit(solution)/shard_map/ppermute | solution.py:78
  22.1 9.9 %collective-permute-done.2 = bf16[24,4096]{1,0:T(8,128)(2,1)S(1)} collective-permute-done((bf16[24,4096]{1,0:T(8,128)(2,1)S(1)}, bf16[24,4096]{1,0:T(8,128)(2,1)S(1)}, u32[]{:S(2)}, u32[]{:S(2)}) %collective-permute-start.2) | collective-permute-done | bytes 196640 | tf_op jit(solution)/shard_map/ppermute | solution.py:77
  32.3 1.8 gather_fusion
  34.4 2.6 %collective-permute-start.10 = (s32[24]{0:T(128)S(1)}, s32[24]{0:T(128)S(1)}, u32[]{:S(2)}, u32[]{:S(2)}) collective-permute-start(s32[24]{0:T(128)S(1)} %get-tuple-element.30), channel_id=1, source_target_pairs={{0,96},{32,0},{64,32},{96,64},{1,97},{33,1},{65,33},{97,65},{2,98}... | collective-permute-start | bytes 296 | tf_op jit(solution)/shard_map/ppermute | solution.py:78
  37.1 2.6 %collective-permute-start.12 = (s32[48]{0:T(128)S(1)}, s32[48]{0:T(128)S(1)}, u32[]{:S(2)}, u32[]{:S(2)}) collective-permute-start(s32[48]{0:T(128)S(1)} %get-tuple-element.26), channel_id=1, source_target_pairs={{0,96},{32,0},{64,32},{96,64},{1,97},{33,1},{65,33},{97,65},{2,98}... | collective-permute-start | bytes 584 | tf_op jit(solution)/shard_map/ppermute | solution.py:74
  39.7 0.6 dynamic-slice
  41.0 1.5 collective-permute-start.11
  42.5 3.2 %collective-permute-start.6 = (bf16[192,4096]{1,0:T(8,128)(2,1)S(1)}, bf16[192,4096]{1,0:T(8,128)(2,1)S(1)}, u32[]{:S(2)}, u32[]{:S(2)}) collective-permute-start(bf16[192,4096]{1,0:T(8,128)(2,1)S(1)} %bitcast.34), channel_id=1, source_target_pairs={{0,1},{1,0},{2,3},{3,2},{4,5},{5,4},{6,7},{7,6},{8,9},{9,8},{10,11... | collective-permute-start | bytes 4718600 | tf_op jit(solution)/shard_map/ppermute | solution.py:118
  45.8 0.4 collective-permute-done.9
  46.2 0.6 gather_fusion.1
  47.1 130.5 %all-reduce = s32[6144]{0:T(1024)S(1)} all-reduce(s32[6144]{0:T(1024)S(1)} %dynamic-update-slice), channel_id=1, replica_groups=mesh['mass'=4,'tile'=32] {'tile'}, use_global_device_ids=true, to_apply=%add | all-reduce | flops 6144 | bytes 49152
  177.7 0.7 compare_convert_fusion.oh_ref
  178.4 1.9 pad_maximum_fusion.a_ref
  180.2 16.4 %all-gather.2.cloned.1.call-done.p_ref = bf16[6144,4096]{1,0:T(8,128)(2,1)} async-done(((bf16[192,4096]{1,0:T(8,128)(2,1)}), bf16[6144,4096]{1,0:T(8,128)(2,1)}) %all-gather.2.cloned.1.call-update) | async-done | bytes 50331664 | tf_op jit(solution)/shard_map/all_gather | solution.py:113
  196.7 18.9 %shard_map.50 = (f32[192,6144]{1,0:T(8,128)}, f32[48,3072]{1,0:T(8,128)}, f32[48,3072]{1,0:T(8,128)}, f32[48,3072]{1,0:T(8,128)}, f32[48,3072]{1,0:T(8,128)}, /*index=5*/f32[4,4096]{1,0:T(4,128)}, f32[4,4096]{1,0:T(4,128)}) custom-call(s32[1]{0:T(128)} %bitcast.half_ref, bf16[384,4096]{1,0:T(8,128)(2,1)} %pad_maximum_fusion.a_ref, ...), custom_call_target="tpu_custom_call" | custom-call | flops 9865003008 | bytes 33210368 | tf_op jit(solution)/shard_map/pallas_call | solution.py:58
  215.6 0.3 collective-permute-start.13
  217.0 0.9 collective-permute-done.13
  217.9 0.9 constant_dynamic-update-slice_fusion
  218.8 0.9 constant_dynamic-update-slice_fusion.3
  219.6 0.9 constant_dynamic-update-slice_fusion.2
  220.5 0.9 constant_dynamic-update-slice_fusion.1
  221.4 0.6 add.145
  (50 shorter events, 2.6 us)
Async XLA Ops:
  7.2 4.0 %copy-start.1 = (bf16[96,4096]{1,0:T(8,128)(2,1)S(1)}, bf16[96,4096]{1,0:T(8,128)(2,1)}, u32[]{:S(2)}) copy-start(bf16[96,4096]{1,0:T(8,128)(2,1)} %param.3) | copy-start | bytes 2359300
  7.2 189.5 %all-gather.2.cloned.1.call-start = ((), (), s32[]{:S(2)}) async-start(), calls=%async_computation | async-start | bytes 51904512 | tf_op jit(solution)/shard_map/all_gather | solution.py:113
  11.8 7.6 %collective-permute-start.1 = (bf16[24,4096]{1,0:T(8,128)(2,1)S(1)}, bf16[24,4096]{1,0:T(8,128)(2,1)S(1)}, u32[]{:S(2)}, u32[]{:S(2)}) collective-permute-start(bf16[24,4096]{1,0:T(8,128)(2,1)S(1)} %get-tuple-element.23), channel_id=1, source_target_pairs={{0,32},{32,64},{64,96},{96,0},{1,33},{33,65},{65,97},{97,1},{2,34}... | collective-permute-start | bytes 589832 | tf_op jit(solution)/shard_map/ppermute | solution.py:77
  13.9 5.8 %collective-permute-start.3 = (bf16[24,4096]{1,0:T(8,128)(2,1)S(1)}, bf16[24,4096]{1,0:T(8,128)(2,1)S(1)}, u32[]{:S(2)}, u32[]{:S(2)}) collective-permute-start(bf16[24,4096]{1,0:T(8,128)(2,1)S(1)} %get-tuple-element.24), channel_id=1, source_target_pairs={{0,96},{32,0},{64,32},{96,64},{1,97},{33,1},{65,33},{97,65},{2,98}... | collective-permute-start | bytes 589832 | tf_op jit(solution)/shard_map/ppermute | solution.py:78
  15.3 16.8 %collective-permute-start = (bf16[48,4096]{1,0:T(8,128)(2,1)S(1)}, bf16[48,4096]{1,0:T(8,128)(2,1)S(1)}, u32[]{:S(2)}, u32[]{:S(2)}) collective-permute-start(bf16[48,4096]{1,0:T(8,128)(2,1)S(1)} %get-tuple-element.22), channel_id=1, source_target_pairs={{0,32},{32,64},{64,96},{96,0},{1,33},{33,65},{65,97},{97,1},{2,34}... | collective-permute-start | bytes 1179656 | tf_op jit(solution)/shard_map/ppermute | solution.py:73
  15.5 16.6 %collective-permute-start.5 = (bf16[48,4096]{1,0:T(8,128)(2,1)S(1)}, bf16[48,4096]{1,0:T(8,128)(2,1)S(1)}, u32[]{:S(2)}, u32[]{:S(2)}) collective-permute-start(bf16[48,4096]{1,0:T(8,128)(2,1)S(1)} %get-tuple-element.21), channel_id=1, source_target_pairs={{0,96},{32,0},{64,32},{96,64},{1,97},{33,1},{65,33},{97,65},{2,98}... | collective-permute-start | bytes 1179656 | tf_op jit(solution)/shard_map/ppermute | solution.py:74
  19.4 12.6 %collective-permute-start.2 = (bf16[24,4096]{1,0:T(8,128)(2,1)S(1)}, bf16[24,4096]{1,0:T(8,128)(2,1)S(1)}, u32[]{:S(2)}, u32[]{:S(2)}) collective-permute-start(bf16[24,4096]{1,0:T(8,128)(2,1)S(1)} %collective-permute-done.1), channel_id=1, source_target_pairs={{0,32},{32,64},{64,96},{96,0},{1,33},{33,65},{65,97},{97,1},{2,34}... | collective-permute-start | bytes 589832 | tf_op jit(solution)/shard_map/ppermute | solution.py:77
  19.7 12.4 %collective-permute-start.4 = (bf16[24,4096]{1,0:T(8,128)(2,1)S(1)}, bf16[24,4096]{1,0:T(8,128)(2,1)S(1)}, u32[]{:S(2)}, u32[]{:S(2)}) collective-permute-start(bf16[24,4096]{1,0:T(8,128)(2,1)S(1)} %collective-permute-done.3), channel_id=1, source_target_pairs={{0,96},{32,0},{64,32},{96,64},{1,97},{33,1},{65,33},{97,65},{2,98}... | collective-permute-start | bytes 589832 | tf_op jit(solution)/shard_map/ppermute | solution.py:78
  34.1 5.6 %copy-start.3 = (u32[128]{0:T(128)S(1)}, u32[128]{0:T(128)}, u32[]{:S(2)}) copy-start(u32[128]{0:T(128)} %constant.106) | copy-start | bytes 1540
  34.1 8.4 %copy-start = (bf16[4,48,4096]{2,1,0:T(8,128)(2,1)S(1)}, bf16[4,48,4096]{2,1,0:T(8,128)(2,1)}, u32[]{:S(2)}) copy-start(bf16[4,48,4096]{2,1,0:T(8,128)(2,1)} %gather_fusion) | copy-start | bytes 4718596
  34.4 6.6 %collective-permute-start.10 = (s32[24]{0:T(128)S(1)}, s32[24]{0:T(128)S(1)}, u32[]{:S(2)}, u32[]{:S(2)}) collective-permute-start(s32[24]{0:T(128)S(1)} %get-tuple-element.30), channel_id=1, source_target_pairs={{0,96},{32,0},{64,32},{96,64},{1,97},{33,1},{65,33},{97,65},{2,98}... | collective-permute-start | bytes 296 | tf_op jit(solution)/shard_map/ppermute | solution.py:78
  37.0 5.5 %collective-permute-start.8 = (s32[24]{0:T(128)S(1)}, s32[24]{0:T(128)S(1)}, u32[]{:S(2)}, u32[]{:S(2)}) collective-permute-start(s32[24]{0:T(128)S(1)} %get-tuple-element.29), channel_id=1, source_target_pairs={{0,32},{32,64},{64,96},{96,0},{1,33},{33,65},{65,97},{97,1},{2,34}... | collective-permute-start | bytes 296 | tf_op jit(solution)/shard_map/ppermute | solution.py:77
  37.0 9.2 %collective-permute-start.7 = (s32[48]{0:T(128)S(1)}, s32[48]{0:T(128)S(1)}, u32[]{:S(2)}, u32[]{:S(2)}) collective-permute-start(s32[48]{0:T(128)S(1)} %get-tuple-element.28), channel_id=1, source_target_pairs={{0,32},{32,64},{64,96},{96,0},{1,33},{33,65},{65,97},{97,1},{2,34}... | collective-permute-start | bytes 584 | tf_op jit(solution)/shard_map/ppermute | solution.py:73
  37.1 9.1 %collective-permute-start.12 = (s32[48]{0:T(128)S(1)}, s32[48]{0:T(128)S(1)}, u32[]{:S(2)}, u32[]{:S(2)}) collective-permute-start(s32[48]{0:T(128)S(1)} %get-tuple-element.26), channel_id=1, source_target_pairs={{0,96},{32,0},{64,32},{96,64},{1,97},{33,1},{65,33},{97,65},{2,98}... | collective-permute-start | bytes 584 | tf_op jit(solution)/shard_map/ppermute | solution.py:74
  41.0 4.8 %collective-permute-start.11 = (s32[24]{0:T(128)S(1)}, s32[24]{0:T(128)S(1)}, u32[]{:S(2)}, u32[]{:S(2)}) collective-permute-start(s32[24]{0:T(128)S(1)} %collective-permute-done.10), channel_id=1, source_target_pairs={{0,96},{32,0},{64,32},{96,64},{1,97},{33,1},{65,33},{97,65},{2,98}... | collective-permute-start | bytes 296 | tf_op jit(solution)/shard_map/ppermute | solution.py:78
  42.5 3.6 %collective-permute-start.9 = (s32[24]{0:T(128)S(1)}, s32[24]{0:T(128)S(1)}, u32[]{:S(2)}, u32[]{:S(2)}) collective-permute-start(s32[24]{0:T(128)S(1)} %collective-permute-done.8), channel_id=1, source_target_pairs={{0,32},{32,64},{64,96},{96,0},{1,33},{33,65},{65,97},{97,1},{2,34}... | collective-permute-start | bytes 296 | tf_op jit(solution)/shard_map/ppermute | solution.py:77
  42.5 135.8 %collective-permute-start.6 = (bf16[192,4096]{1,0:T(8,128)(2,1)S(1)}, bf16[192,4096]{1,0:T(8,128)(2,1)S(1)}, u32[]{:S(2)}, u32[]{:S(2)}) collective-permute-start(bf16[192,4096]{1,0:T(8,128)(2,1)S(1)} %bitcast.34), channel_id=1, source_target_pairs={{0,1},{1,0},{2,3},{3,2},{4,5},{5,4},{6,7},{7,6},{8,9},{9,8},{10,11... | collective-permute-start | bytes 4718600 | tf_op jit(solution)/shard_map/ppermute | solution.py:118
  215.6 2.3 %collective-permute-start.13 = (f32[48,3072]{1,0:T(8,128)}, f32[48,3072]{1,0:T(8,128)S(1)}, u32[]{:S(2)}, u32[]{:S(2)}) collective-permute-start(f32[48,3072]{1,0:T(8,128)} %get-tuple-element.12), channel_id=1, source_target_pairs={{0,1},{1,0},{2,3},{3,2},{4,5},{5,4},{6,7},{7,6},{8,9},{9,8},{10,11... | collective-permute-start | bytes 1769480 | tf_op jit(solution)/shard_map/ppermute | solution.py:131
  216.0 2.8 %collective-permute-start.14 = (f32[48,3072]{1,0:T(8,128)}, f32[48,3072]{1,0:T(8,128)S(1)}, u32[]{:S(2)}, u32[]{:S(2)}) collective-permute-start(f32[48,3072]{1,0:T(8,128)} %get-tuple-element.13), channel_id=1, source_target_pairs={{0,1},{1,0},{2,3},{3,2},{4,5},{5,4},{6,7},{7,6},{8,9},{9,8},{10,11... | collective-permute-start | bytes 1769480 | tf_op jit(solution)/shard_map/ppermute | solution.py:131
  216.2 3.4 %collective-permute-start.15 = (f32[48,3072]{1,0:T(8,128)}, f32[48,3072]{1,0:T(8,128)S(1)}, u32[]{:S(2)}, u32[]{:S(2)}) collective-permute-start(f32[48,3072]{1,0:T(8,128)} %get-tuple-element.14), channel_id=1, source_target_pairs={{0,1},{1,0},{2,3},{3,2},{4,5},{5,4},{6,7},{7,6},{8,9},{9,8},{10,11... | collective-permute-start | bytes 1769480 | tf_op jit(solution)/shard_map/ppermute | solution.py:131
  216.5 4.0 %collective-permute-start.16 = (f32[48,3072]{1,0:T(8,128)}, f32[48,3072]{1,0:T(8,128)S(1)}, u32[]{:S(2)}, u32[]{:S(2)}) collective-permute-start(f32[48,3072]{1,0:T(8,128)} %get-tuple-element.15), channel_id=1, source_target_pairs={{0,1},{1,0},{2,3},{3,2},{4,5},{5,4},{6,7},{7,6},{8,9},{9,8},{10,11... | collective-permute-start | bytes 1769480 | tf_op jit(solution)/shard_map/ppermute | solution.py:131
  216.7 4.6 %collective-permute-start.17 = (f32[4,4096]{1,0:T(4,128)}, f32[4,4096]{1,0:T(4,128)S(1)}, u32[]{:S(2)}, u32[]{:S(2)}) collective-permute-start(f32[4,4096]{1,0:T(4,128)} %get-tuple-element.16), channel_id=1, source_target_pairs={{0,1},{1,0},{2,3},{3,2},{4,5},{5,4},{6,7},{7,6},{8,9},{9,8},{10,11... | collective-permute-start | bytes 196616 | tf_op jit(solution)/shard_map/ppermute | solution.py:134
  218.8 2.6 %copy-start.2 = (f32[4,4096]{1,0:T(4,128)S(1)}, f32[4,4096]{1,0:T(4,128)}, u32[]{:S(2)}) copy-start(f32[4,4096]{1,0:T(4,128)} %get-tuple-element.18) | copy-start | bytes 196612
Sparse Core Ops, SparseCore 0:
  34.2 162.3 all-gather.1

commit v14 on v13

--- a/solution.py
+++ b/solution.py
@@ -32,7 +32,7 @@
     c_theirs_ref[...] += sums[heads:]
 
 
-def gram_consensus(half, pair_rows, one_hot, gathered, pieces=4, block_rows=1024):
+def gram_consensus(half, pair_rows, one_hot, gathered, pieces=2, block_rows=1024):
     rows = pair_rows.shape[0] // 2
     bins = pair_rows.shape[1]
     total = gathered.shape[0]

time: 229 us -> 229 us (level)
  transfers between devices with their start and end apart: 19 -> 17, of which waited for: 5 -> 6; matrix products, arithmetic and copies ran while one was open for 3% -> 3% of each run, Pallas kernels for 0% -> 0%
where the time goes in v14:
time: 229 us
  blocking collectives  131 us (57%)
  waiting for transfers between devices  31 us (14%)
  starting transfers between devices  19.8 us (9%)
  Pallas kernels  18.9 us (8%)
  between operations  14.9 us (7%)
  other arithmetic  7.54 us (3%)
  local copies, waits for them, and re-layouts  5.73 us (3%)
    unnamed x1, blocking collectives  131 us
    pallas_call x1, Pallas kernels, gram_consensus(): pl.pallas_call(functools.partial(_gram_consensus_kernel, 1.0 / bins, rows...  18.9 us
    all_gather x1, waiting for transfers between devices, shards(): gathered = lax.all_gather(arrived, 'tile', axis=0, tiled=True)  16.4 us
    ppermute x4, waiting for transfers between devices, exchange_over_mass(): first = lax.ppermute(lax.ppermute(far[:half], 'mass', ahead), 'mass', ahead)  11.6 us
    ppermute x2, starting transfers between devices, exchange_over_mass(): from_ahead = lax.ppermute(pieces[(me - 1) % mass_count], 'mass', behind)  5.17 us
  transfers between devices with their start and end apart: 17, of which 6 were waited for; matrix products, arithmetic and copies ran while one was open for 3% of the time, Pallas kernels for 0%

profile of v14, /device:TPU:1, one launch (start us, length us, event | category | flops | bytes accessed | tf_op | source)
XLA Modules:
  0.0 229.0 jit_solution(9284145036606065128)
XLA Ops:
  7.2 0.8 fusion.5
  8.2 0.8 select_reduce_fusion.1
  9.0 1.4 fusion
  10.4 0.7 multiply_add_fusion
  11.1 0.6 convolution_convert_fusion
  11.8 2.1 collective-permute-start.1
  13.9 1.3 collective-permute-start.3
  15.5 2.6 %collective-permute-start.5 = (bf16[48,4096]{1,0:T(8,128)(2,1)S(1)}, bf16[48,4096]{1,0:T(8,128)(2,1)S(1)}, u32[]{:S(2)}, u32[]{:S(2)}) collective-permute-start(bf16[48,4096]{1,0:T(8,128)(2,1)S(1)} %get-tuple-element.17), channel_id=1, source_target_pairs={{0,96},{32,0},{64,32},{96,64},{1,97},{33,1},{65,33},{97,65},{2,98}... | collective-permute-start | bytes 1179656 | tf_op jit(solution)/shard_map/ppermute | solution.py:74
  18.1 1.3 collective-permute-done.1
  19.4 0.3 collective-permute-start.2
  19.7 2.4 %collective-permute-start.4 = (bf16[24,4096]{1,0:T(8,128)(2,1)S(1)}, bf16[24,4096]{1,0:T(8,128)(2,1)S(1)}, u32[]{:S(2)}, u32[]{:S(2)}) collective-permute-start(bf16[24,4096]{1,0:T(8,128)(2,1)S(1)} %collective-permute-done.3), channel_id=1, source_target_pairs={{0,96},{32,0},{64,32},{96,64},{1,97},{33,1},{65,33},{97,65},{2,98}... | collective-permute-start | bytes 589832 | tf_op jit(solution)/shard_map/ppermute | solution.py:78
  22.1 9.9 %collective-permute-done.2 = bf16[24,4096]{1,0:T(8,128)(2,1)S(1)} collective-permute-done((bf16[24,4096]{1,0:T(8,128)(2,1)S(1)}, bf16[24,4096]{1,0:T(8,128)(2,1)S(1)}, u32[]{:S(2)}, u32[]{:S(2)}) %collective-permute-start.2) | collective-permute-done | bytes 196640 | tf_op jit(solution)/shard_map/ppermute | solution.py:77
  32.3 1.8 gather_fusion
  34.4 2.6 %collective-permute-start.10 = (s32[24]{0:T(128)S(1)}, s32[24]{0:T(128)S(1)}, u32[]{:S(2)}, u32[]{:S(2)}) collective-permute-start(s32[24]{0:T(128)S(1)} %get-tuple-element.26), channel_id=1, source_target_pairs={{0,96},{32,0},{64,32},{96,64},{1,97},{33,1},{65,33},{97,65},{2,98}... | collective-permute-start | bytes 296 | tf_op jit(solution)/shard_map/ppermute | solution.py:78
  37.1 2.6 %collective-permute-start.12 = (s32[48]{0:T(128)S(1)}, s32[48]{0:T(128)S(1)}, u32[]{:S(2)}, u32[]{:S(2)}) collective-permute-start(s32[48]{0:T(128)S(1)} %get-tuple-element.22), channel_id=1, source_target_pairs={{0,96},{32,0},{64,32},{96,64},{1,97},{33,1},{65,33},{97,65},{2,98}... | collective-permute-start | bytes 584 | tf_op jit(solution)/shard_map/ppermute | solution.py:74
  39.7 0.6 dynamic-slice
  41.0 1.5 collective-permute-start.11
  42.5 3.2 %collective-permute-start.6 = (bf16[192,4096]{1,0:T(8,128)(2,1)S(1)}, bf16[192,4096]{1,0:T(8,128)(2,1)S(1)}, u32[]{:S(2)}, u32[]{:S(2)}) collective-permute-start(bf16[192,4096]{1,0:T(8,128)(2,1)S(1)} %bitcast.34), channel_id=1, source_target_pairs={{0,1},{1,0},{2,3},{3,2},{4,5},{5,4},{6,7},{7,6},{8,9},{9,8},{10,11... | collective-permute-start | bytes 4718600 | tf_op jit(solution)/shard_map/ppermute | solution.py:118
  45.8 0.4 collective-permute-done.9
  46.2 0.6 gather_fusion.1
  47.1 130.5 %all-reduce = s32[6144]{0:T(1024)S(1)} all-reduce(s32[6144]{0:T(1024)S(1)} %dynamic-update-slice), channel_id=1, replica_groups=mesh['mass'=4,'tile'=32] {'tile'}, use_global_device_ids=true, to_apply=%add | all-reduce | flops 6144 | bytes 49152
  177.7 0.7 compare_convert_fusion.oh_ref
  178.4 1.9 pad_maximum_fusion.a_ref
  180.2 16.4 %all-gather.2.cloned.1.call-done.p_ref = bf16[6144,4096]{1,0:T(8,128)(2,1)} async-done(((bf16[192,4096]{1,0:T(8,128)(2,1)}), bf16[6144,4096]{1,0:T(8,128)(2,1)}) %all-gather.2.cloned.1.call-update) | async-done | bytes 50331664 | tf_op jit(solution)/shard_map/all_gather | solution.py:113
  196.7 18.9 %shard_map.50 = (f32[192,6144]{1,0:T(8,128)}, f32[96,3072]{1,0:T(8,128)}, f32[96,3072]{1,0:T(8,128)}, f32[4,4096]{1,0:T(4,128)}, f32[4,4096]{1,0:T(4,128)}) custom-call(s32[1]{0:T(128)} %bitcast.half_ref, bf16[384,4096]{1,0:T(8,128)(2,1)} %pad_maximum_fusion.a_ref, bf16[8,6144]{1,0:T(8,128)(2,1)} %compare_convert_fusion.oh_ref, ...), custom_call_target="tpu_custom_call" | custom-call | flops 9865003008 | bytes 33210368 | tf_op jit(solution)/shard_map/pallas_call | solution.py:58
  215.6 0.3 collective-permute-start.13
  216.2 0.3 collective-permute-start.15
  216.5 2.3 collective-permute-done.13
  218.7 1.1 constant_dynamic-update-slice_fusion
  219.8 0.6 collective-permute-done.14
  220.4 1.1 constant_dynamic-update-slice_fusion.1
  221.5 0.6 add.143
  (44 shorter events, 1.8 us)
Async XLA Ops:
  7.2 4.0 %copy-start.1 = (bf16[96,4096]{1,0:T(8,128)(2,1)S(1)}, bf16[96,4096]{1,0:T(8,128)(2,1)}, u32[]{:S(2)}) copy-start(bf16[96,4096]{1,0:T(8,128)(2,1)} %param.3) | copy-start | bytes 2359300
  7.2 189.5 %all-gather.2.cloned.1.call-start = ((), (), s32[]{:S(2)}) async-start(), calls=%async_computation | async-start | bytes 51904512 | tf_op jit(solution)/shard_map/all_gather | solution.py:113
  11.8 7.6 %collective-permute-start.1 = (bf16[24,4096]{1,0:T(8,128)(2,1)S(1)}, bf16[24,4096]{1,0:T(8,128)(2,1)S(1)}, u32[]{:S(2)}, u32[]{:S(2)}) collective-permute-start(bf16[24,4096]{1,0:T(8,128)(2,1)S(1)} %get-tuple-element.19), channel_id=1, source_target_pairs={{0,32},{32,64},{64,96},{96,0},{1,33},{33,65},{65,97},{97,1},{2,34}... | collective-permute-start | bytes 589832 | tf_op jit(solution)/shard_map/ppermute | solution.py:77
  13.9 5.8 %collective-permute-start.3 = (bf16[24,4096]{1,0:T(8,128)(2,1)S(1)}, bf16[24,4096]{1,0:T(8,128)(2,1)S(1)}, u32[]{:S(2)}, u32[]{:S(2)}) collective-permute-start(bf16[24,4096]{1,0:T(8,128)(2,1)S(1)} %get-tuple-element.20), channel_id=1, source_target_pairs={{0,96},{32,0},{64,32},{96,64},{1,97},{33,1},{65,33},{97,65},{2,98}... | collective-permute-start | bytes 589832 | tf_op jit(solution)/shard_map/ppermute | solution.py:78
  15.3 16.8 %collective-permute-start = (bf16[48,4096]{1,0:T(8,128)(2,1)S(1)}, bf16[48,4096]{1,0:T(8,128)(2,1)S(1)}, u32[]{:S(2)}, u32[]{:S(2)}) collective-permute-start(bf16[48,4096]{1,0:T(8,128)(2,1)S(1)} %get-tuple-element.18), channel_id=1, source_target_pairs={{0,32},{32,64},{64,96},{96,0},{1,33},{33,65},{65,97},{97,1},{2,34}... | collective-permute-start | bytes 1179656 | tf_op jit(solution)/shard_map/ppermute | solution.py:73
  15.5 16.6 %collective-permute-start.5 = (bf16[48,4096]{1,0:T(8,128)(2,1)S(1)}, bf16[48,4096]{1,0:T(8,128)(2,1)S(1)}, u32[]{:S(2)}, u32[]{:S(2)}) collective-permute-start(bf16[48,4096]{1,0:T(8,128)(2,1)S(1)} %get-tuple-element.17), channel_id=1, source_target_pairs={{0,96},{32,0},{64,32},{96,64},{1,97},{33,1},{65,33},{97,65},{2,98}... | collective-permute-start | bytes 1179656 | tf_op jit(solution)/shard_map/ppermute | solution.py:74
  19.4 12.6 %collective-permute-start.2 = (bf16[24,4096]{1,0:T(8,128)(2,1)S(1)}, bf16[24,4096]{1,0:T(8,128)(2,1)S(1)}, u32[]{:S(2)}, u32[]{:S(2)}) collective-permute-start(bf16[24,4096]{1,0:T(8,128)(2,1)S(1)} %collective-permute-done.1), channel_id=1, source_target_pairs={{0,32},{32,64},{64,96},{96,0},{1,33},{33,65},{65,97},{97,1},{2,34}... | collective-permute-start | bytes 589832 | tf_op jit(solution)/shard_map/ppermute | solution.py:77
  19.7 12.4 %collective-permute-start.4 = (bf16[24,4096]{1,0:T(8,128)(2,1)S(1)}, bf16[24,4096]{1,0:T(8,128)(2,1)S(1)}, u32[]{:S(2)}, u32[]{:S(2)}) collective-permute-start(bf16[24,4096]{1,0:T(8,128)(2,1)S(1)} %collective-permute-done.3), channel_id=1, source_target_pairs={{0,96},{32,0},{64,32},{96,64},{1,97},{33,1},{65,33},{97,65},{2,98}... | collective-permute-start | bytes 589832 | tf_op jit(solution)/shard_map/ppermute | solution.py:78
  34.1 5.6 %copy-start.3 = (u32[128]{0:T(128)S(1)}, u32[128]{0:T(128)}, u32[]{:S(2)}) copy-start(u32[128]{0:T(128)} %constant.103) | copy-start | bytes 1540
  34.1 8.4 %copy-start = (bf16[4,48,4096]{2,1,0:T(8,128)(2,1)S(1)}, bf16[4,48,4096]{2,1,0:T(8,128)(2,1)}, u32[]{:S(2)}) copy-start(bf16[4,48,4096]{2,1,0:T(8,128)(2,1)} %gather_fusion) | copy-start | bytes 4718596
  34.4 6.6 %collective-permute-start.10 = (s32[24]{0:T(128)S(1)}, s32[24]{0:T(128)S(1)}, u32[]{:S(2)}, u32[]{:S(2)}) collective-permute-start(s32[24]{0:T(128)S(1)} %get-tuple-element.26), channel_id=1, source_target_pairs={{0,96},{32,0},{64,32},{96,64},{1,97},{33,1},{65,33},{97,65},{2,98}... | collective-permute-start | bytes 296 | tf_op jit(solution)/shard_map/ppermute | solution.py:78
  37.0 5.5 %collective-permute-start.8 = (s32[24]{0:T(128)S(1)}, s32[24]{0:T(128)S(1)}, u32[]{:S(2)}, u32[]{:S(2)}) collective-permute-start(s32[24]{0:T(128)S(1)} %get-tuple-element.25), channel_id=1, source_target_pairs={{0,32},{32,64},{64,96},{96,0},{1,33},{33,65},{65,97},{97,1},{2,34}... | collective-permute-start | bytes 296 | tf_op jit(solution)/shard_map/ppermute | solution.py:77
  37.0 9.2 %collective-permute-start.7 = (s32[48]{0:T(128)S(1)}, s32[48]{0:T(128)S(1)}, u32[]{:S(2)}, u32[]{:S(2)}) collective-permute-start(s32[48]{0:T(128)S(1)} %get-tuple-element.24), channel_id=1, source_target_pairs={{0,32},{32,64},{64,96},{96,0},{1,33},{33,65},{65,97},{97,1},{2,34}... | collective-permute-start | bytes 584 | tf_op jit(solution)/shard_map/ppermute | solution.py:73
  37.1 9.1 %collective-permute-start.12 = (s32[48]{0:T(128)S(1)}, s32[48]{0:T(128)S(1)}, u32[]{:S(2)}, u32[]{:S(2)}) collective-permute-start(s32[48]{0:T(128)S(1)} %get-tuple-element.22), channel_id=1, source_target_pairs={{0,96},{32,0},{64,32},{96,64},{1,97},{33,1},{65,33},{97,65},{2,98}... | collective-permute-start | bytes 584 | tf_op jit(solution)/shard_map/ppermute | solution.py:74
  41.0 4.8 %collective-permute-start.11 = (s32[24]{0:T(128)S(1)}, s32[24]{0:T(128)S(1)}, u32[]{:S(2)}, u32[]{:S(2)}) collective-permute-start(s32[24]{0:T(128)S(1)} %collective-permute-done.10), channel_id=1, source_target_pairs={{0,96},{32,0},{64,32},{96,64},{1,97},{33,1},{65,33},{97,65},{2,98}... | collective-permute-start | bytes 296 | tf_op jit(solution)/shard_map/ppermute | solution.py:78
  42.5 3.6 %collective-permute-start.9 = (s32[24]{0:T(128)S(1)}, s32[24]{0:T(128)S(1)}, u32[]{:S(2)}, u32[]{:S(2)}) collective-permute-start(s32[24]{0:T(128)S(1)} %collective-permute-done.8), channel_id=1, source_target_pairs={{0,32},{32,64},{64,96},{96,0},{1,33},{33,65},{65,97},{97,1},{2,34}... | collective-permute-start | bytes 296 | tf_op jit(solution)/shard_map/ppermute | solution.py:77
  42.5 135.8 %collective-permute-start.6 = (bf16[192,4096]{1,0:T(8,128)(2,1)S(1)}, bf16[192,4096]{1,0:T(8,128)(2,1)S(1)}, u32[]{:S(2)}, u32[]{:S(2)}) collective-permute-start(bf16[192,4096]{1,0:T(8,128)(2,1)S(1)} %bitcast.34), channel_id=1, source_target_pairs={{0,1},{1,0},{2,3},{3,2},{4,5},{5,4},{6,7},{7,6},{8,9},{9,8},{10,11... | collective-permute-start | bytes 4718600 | tf_op jit(solution)/shard_map/ppermute | solution.py:118
  215.6 3.1 %collective-permute-start.13 = (f32[96,3072]{1,0:T(8,128)}, f32[96,3072]{1,0:T(8,128)S(1)}, u32[]{:S(2)}, u32[]{:S(2)}) collective-permute-start(f32[96,3072]{1,0:T(8,128)} %get-tuple-element.10), channel_id=1, source_target_pairs={{0,1},{1,0},{2,3},{3,2},{4,5},{5,4},{6,7},{7,6},{8,9},{9,8},{10,11... | collective-permute-start | bytes 3538952 | tf_op jit(solution)/shard_map/ppermute | solution.py:131
  216.0 4.5 %collective-permute-start.14 = (f32[96,3072]{1,0:T(8,128)}, f32[96,3072]{1,0:T(8,128)S(1)}, u32[]{:S(2)}, u32[]{:S(2)}) collective-permute-start(f32[96,3072]{1,0:T(8,128)} %get-tuple-element.11), channel_id=1, source_target_pairs={{0,1},{1,0},{2,3},{3,2},{4,5},{5,4},{6,7},{7,6},{8,9},{9,8},{10,11... | collective-permute-start | bytes 3538952 | tf_op jit(solution)/shard_map/ppermute | solution.py:131
  216.2 5.3 %collective-permute-start.15 = (f32[4,4096]{1,0:T(4,128)}, f32[4,4096]{1,0:T(4,128)S(1)}, u32[]{:S(2)}, u32[]{:S(2)}) collective-permute-start(f32[4,4096]{1,0:T(4,128)} %get-tuple-element.12), channel_id=1, source_target_pairs={{0,1},{1,0},{2,3},{3,2},{4,5},{5,4},{6,7},{7,6},{8,9},{9,8},{10,11... | collective-permute-start | bytes 196616 | tf_op jit(solution)/shard_map/ppermute | solution.py:134
  219.8 1.7 copy-start.2
Sparse Core Ops, SparseCore 0:
  34.2 162.3 all-gather.1

commit v15 on v14

--- a/solution.py
+++ b/solution.py
@@ -32,7 +32,7 @@
     c_theirs_ref[...] += sums[heads:]
 
 
-def gram_consensus(half, pair_rows, one_hot, gathered, pieces=2, block_rows=1024):
+def gram_consensus(half, pair_rows, one_hot, gathered, pieces=2, block_rows=512):
     rows = pair_rows.shape[0] // 2
     bins = pair_rows.shape[1]
     total = gathered.shape[0]

time: 229 us -> 229 us (level)
  no operation moved by 1% of the time
where the time goes in v15:
time: 229 us
  blocking collectives  131 us (57%)
  waiting for transfers between devices  31 us (14%)
  starting transfers between devices  19.8 us (9%)
  Pallas kernels  18.8 us (8%)
  between operations  14.9 us (7%)
  other arithmetic  7.54 us (3%)
  local copies, waits for them, and re-layouts  5.73 us (3%)
    unnamed x1, blocking collectives  131 us
    pallas_call x1, Pallas kernels, gram_consensus(): pl.pallas_call(functools.partial(_gram_consensus_kernel, 1.0 / bins, rows...  18.8 us
    all_gather x1, waiting for transfers between devices, shards(): gathered = lax.all_gather(arrived, 'tile', axis=0, tiled=True)  16.4 us
    ppermute x4, waiting for transfers between devices, exchange_over_mass(): first = lax.ppermute(lax.ppermute(far[:half], 'mass', ahead), 'mass', ahead)  11.6 us
    ppermute x2, starting transfers between devices, exchange_over_mass(): from_ahead = lax.ppermute(pieces[(me - 1) % mass_count], 'mass', behind)  5.17 us
  transfers between devices with their start and end apart: 17, of which 6 were waited for; matrix products, arithmetic and copies ran while one was open for 3% of the time, Pallas kernels for 0%

profile of v15, /device:TPU:1, one launch (start us, length us, event | category | flops | bytes accessed | tf_op | source)
XLA Modules:
  0.0 228.9 jit_solution(17806201062275912231)
XLA Ops:
  7.2 0.8 fusion.5
  8.2 0.8 select_reduce_fusion.1
  9.0 1.4 fusion
  10.4 0.7 multiply_add_fusion
  11.1 0.6 convolution_convert_fusion
  11.8 2.1 collective-permute-start.1
  13.9 1.3 collective-permute-start.3
  15.5 2.6 %collective-permute-start.5 = (bf16[48,4096]{1,0:T(8,128)(2,1)S(1)}, bf16[48,4096]{1,0:T(8,128)(2,1)S(1)}, u32[]{:S(2)}, u32[]{:S(2)}) collective-permute-start(bf16[48,4096]{1,0:T(8,128)(2,1)S(1)} %get-tuple-element.17), channel_id=1, source_target_pairs={{0,96},{32,0},{64,32},{96,64},{1,97},{33,1},{65,33},{97,65},{2,98}... | collective-permute-start | bytes 1179656 | tf_op jit(solution)/shard_map/ppermute | solution.py:74
  18.1 1.3 collective-permute-done.1
  19.4 0.3 collective-permute-start.2
  19.7 2.4 %collective-permute-start.4 = (bf16[24,4096]{1,0:T(8,128)(2,1)S(1)}, bf16[24,4096]{1,0:T(8,128)(2,1)S(1)}, u32[]{:S(2)}, u32[]{:S(2)}) collective-permute-start(bf16[24,4096]{1,0:T(8,128)(2,1)S(1)} %collective-permute-done.3), channel_id=1, source_target_pairs={{0,96},{32,0},{64,32},{96,64},{1,97},{33,1},{65,33},{97,65},{2,98}... | collective-permute-start | bytes 589832 | tf_op jit(solution)/shard_map/ppermute | solution.py:78
  22.1 9.9 %collective-permute-done.2 = bf16[24,4096]{1,0:T(8,128)(2,1)S(1)} collective-permute-done((bf16[24,4096]{1,0:T(8,128)(2,1)S(1)}, bf16[24,4096]{1,0:T(8,128)(2,1)S(1)}, u32[]{:S(2)}, u32[]{:S(2)}) %collective-permute-start.2) | collective-permute-done | bytes 196640 | tf_op jit(solution)/shard_map/ppermute | solution.py:77
  32.3 1.8 gather_fusion
  34.4 2.6 %collective-permute-start.10 = (s32[24]{0:T(128)S(1)}, s32[24]{0:T(128)S(1)}, u32[]{:S(2)}, u32[]{:S(2)}) collective-permute-start(s32[24]{0:T(128)S(1)} %get-tuple-element.26), channel_id=1, source_target_pairs={{0,96},{32,0},{64,32},{96,64},{1,97},{33,1},{65,33},{97,65},{2,98}... | collective-permute-start | bytes 296 | tf_op jit(solution)/shard_map/ppermute | solution.py:78
  37.1 2.6 %collective-permute-start.12 = (s32[48]{0:T(128)S(1)}, s32[48]{0:T(128)S(1)}, u32[]{:S(2)}, u32[]{:S(2)}) collective-permute-start(s32[48]{0:T(128)S(1)} %get-tuple-element.22), channel_id=1, source_target_pairs={{0,96},{32,0},{64,32},{96,64},{1,97},{33,1},{65,33},{97,65},{2,98}... | collective-permute-start | bytes 584 | tf_op jit(solution)/shard_map/ppermute | solution.py:74
  39.7 0.6 dynamic-slice
  41.0 1.5 collective-permute-start.11
  42.5 3.2 %collective-permute-start.6 = (bf16[192,4096]{1,0:T(8,128)(2,1)S(1)}, bf16[192,4096]{1,0:T(8,128)(2,1)S(1)}, u32[]{:S(2)}, u32[]{:S(2)}) collective-permute-start(bf16[192,4096]{1,0:T(8,128)(2,1)S(1)} %bitcast.34), channel_id=1, source_target_pairs={{0,1},{1,0},{2,3},{3,2},{4,5},{5,4},{6,7},{7,6},{8,9},{9,8},{10,11... | collective-permute-start | bytes 4718600 | tf_op jit(solution)/shard_map/ppermute | solution.py:118
  45.8 0.4 collective-permute-done.9
  46.2 0.6 gather_fusion.1
  47.1 130.5 %all-reduce = s32[6144]{0:T(1024)S(1)} all-reduce(s32[6144]{0:T(1024)S(1)} %dynamic-update-slice), channel_id=1, replica_groups=mesh['mass'=4,'tile'=32] {'tile'}, use_global_device_ids=true, to_apply=%add | all-reduce | flops 6144 | bytes 49152
  177.7 0.7 compare_convert_fusion.oh_ref
  178.4 1.9 pad_maximum_fusion.a_ref
  180.2 16.4 %all-gather.2.cloned.1.call-done.p_ref = bf16[6144,4096]{1,0:T(8,128)(2,1)} async-done(((bf16[192,4096]{1,0:T(8,128)(2,1)}), bf16[6144,4096]{1,0:T(8,128)(2,1)}) %all-gather.2.cloned.1.call-update) | async-done | bytes 50331664 | tf_op jit(solution)/shard_map/all_gather | solution.py:113
  196.7 18.8 %shard_map.50 = (f32[192,6144]{1,0:T(8,128)}, f32[96,3072]{1,0:T(8,128)}, f32[96,3072]{1,0:T(8,128)}, f32[4,4096]{1,0:T(4,128)}, f32[4,4096]{1,0:T(4,128)}) custom-call(s32[1]{0:T(128)} %bitcast.half_ref, bf16[384,4096]{1,0:T(8,128)(2,1)} %pad_maximum_fusion.a_ref, bf16[8,6144]{1,0:T(8,128)(2,1)} %compare_convert_fusion.oh_ref, ...), custom_call_target="tpu_custom_call" | custom-call | flops 9865003008 | bytes 33210368 | tf_op jit(solution)/shard_map/pallas_call | solution.py:58
  215.4 0.3 collective-permute-start.13
  216.0 0.3 collective-permute-start.15
  216.3 2.3 collective-permute-done.13
  218.6 1.1 constant_dynamic-update-slice_fusion
  219.7 0.6 collective-permute-done.14
  220.3 1.1 constant_dynamic-update-slice_fusion.1
  221.4 0.6 add.143
  (44 shorter events, 1.8 us)
Async XLA Ops:
  7.2 4.0 %copy-start.1 = (bf16[96,4096]{1,0:T(8,128)(2,1)S(1)}, bf16[96,4096]{1,0:T(8,128)(2,1)}, u32[]{:S(2)}) copy-start(bf16[96,4096]{1,0:T(8,128)(2,1)} %param.3) | copy-start | bytes 2359300
  7.2 189.5 %all-gather.2.cloned.1.call-start = ((), (), s32[]{:S(2)}) async-start(), calls=%async_computation | async-start | bytes 51904512 | tf_op jit(solution)/shard_map/all_gather | solution.py:113
  11.8 7.6 %collective-permute-start.1 = (bf16[24,4096]{1,0:T(8,128)(2,1)S(1)}, bf16[24,4096]{1,0:T(8,128)(2,1)S(1)}, u32[]{:S(2)}, u32[]{:S(2)}) collective-permute-start(bf16[24,4096]{1,0:T(8,128)(2,1)S(1)} %get-tuple-element.19), channel_id=1, source_target_pairs={{0,32},{32,64},{64,96},{96,0},{1,33},{33,65},{65,97},{97,1},{2,34}... | collective-permute-start | bytes 589832 | tf_op jit(solution)/shard_map/ppermute | solution.py:77
  13.9 5.8 %collective-permute-start.3 = (bf16[24,4096]{1,0:T(8,128)(2,1)S(1)}, bf16[24,4096]{1,0:T(8,128)(2,1)S(1)}, u32[]{:S(2)}, u32[]{:S(2)}) collective-permute-start(bf16[24,4096]{1,0:T(8,128)(2,1)S(1)} %get-tuple-element.20), channel_id=1, source_target_pairs={{0,96},{32,0},{64,32},{96,64},{1,97},{33,1},{65,33},{97,65},{2,98}... | collective-permute-start | bytes 589832 | tf_op jit(solution)/shard_map/ppermute | solution.py:78
  15.3 16.8 %collective-permute-start = (bf16[48,4096]{1,0:T(8,128)(2,1)S(1)}, bf16[48,4096]{1,0:T(8,128)(2,1)S(1)}, u32[]{:S(2)}, u32[]{:S(2)}) collective-permute-start(bf16[48,4096]{1,0:T(8,128)(2,1)S(1)} %get-tuple-element.18), channel_id=1, source_target_pairs={{0,32},{32,64},{64,96},{96,0},{1,33},{33,65},{65,97},{97,1},{2,34}... | collective-permute-start | bytes 1179656 | tf_op jit(solution)/shard_map/ppermute | solution.py:73
  15.5 16.6 %collective-permute-start.5 = (bf16[48,4096]{1,0:T(8,128)(2,1)S(1)}, bf16[48,4096]{1,0:T(8,128)(2,1)S(1)}, u32[]{:S(2)}, u32[]{:S(2)}) collective-permute-start(bf16[48,4096]{1,0:T(8,128)(2,1)S(1)} %get-tuple-element.17), channel_id=1, source_target_pairs={{0,96},{32,0},{64,32},{96,64},{1,97},{33,1},{65,33},{97,65},{2,98}... | collective-permute-start | bytes 1179656 | tf_op jit(solution)/shard_map/ppermute | solution.py:74
  19.4 12.6 %collective-permute-start.2 = (bf16[24,4096]{1,0:T(8,128)(2,1)S(1)}, bf16[24,4096]{1,0:T(8,128)(2,1)S(1)}, u32[]{:S(2)}, u32[]{:S(2)}) collective-permute-start(bf16[24,4096]{1,0:T(8,128)(2,1)S(1)} %collective-permute-done.1), channel_id=1, source_target_pairs={{0,32},{32,64},{64,96},{96,0},{1,33},{33,65},{65,97},{97,1},{2,34}... | collective-permute-start | bytes 589832 | tf_op jit(solution)/shard_map/ppermute | solution.py:77
  19.7 12.4 %collective-permute-start.4 = (bf16[24,4096]{1,0:T(8,128)(2,1)S(1)}, bf16[24,4096]{1,0:T(8,128)(2,1)S(1)}, u32[]{:S(2)}, u32[]{:S(2)}) collective-permute-start(bf16[24,4096]{1,0:T(8,128)(2,1)S(1)} %collective-permute-done.3), channel_id=1, source_target_pairs={{0,96},{32,0},{64,32},{96,64},{1,97},{33,1},{65,33},{97,65},{2,98}... | collective-permute-start | bytes 589832 | tf_op jit(solution)/shard_map/ppermute | solution.py:78
  34.1 5.6 %copy-start.3 = (u32[128]{0:T(128)S(1)}, u32[128]{0:T(128)}, u32[]{:S(2)}) copy-start(u32[128]{0:T(128)} %constant.103) | copy-start | bytes 1540
  34.1 8.4 %copy-start = (bf16[4,48,4096]{2,1,0:T(8,128)(2,1)S(1)}, bf16[4,48,4096]{2,1,0:T(8,128)(2,1)}, u32[]{:S(2)}) copy-start(bf16[4,48,4096]{2,1,0:T(8,128)(2,1)} %gather_fusion) | copy-start | bytes 4718596
  34.4 6.6 %collective-permute-start.10 = (s32[24]{0:T(128)S(1)}, s32[24]{0:T(128)S(1)}, u32[]{:S(2)}, u32[]{:S(2)}) collective-permute-start(s32[24]{0:T(128)S(1)} %get-tuple-element.26), channel_id=1, source_target_pairs={{0,96},{32,0},{64,32},{96,64},{1,97},{33,1},{65,33},{97,65},{2,98}... | collective-permute-start | bytes 296 | tf_op jit(solution)/shard_map/ppermute | solution.py:78
  37.0 5.5 %collective-permute-start.8 = (s32[24]{0:T(128)S(1)}, s32[24]{0:T(128)S(1)}, u32[]{:S(2)}, u32[]{:S(2)}) collective-permute-start(s32[24]{0:T(128)S(1)} %get-tuple-element.25), channel_id=1, source_target_pairs={{0,32},{32,64},{64,96},{96,0},{1,33},{33,65},{65,97},{97,1},{2,34}... | collective-permute-start | bytes 296 | tf_op jit(solution)/shard_map/ppermute | solution.py:77
  37.0 9.2 %collective-permute-start.7 = (s32[48]{0:T(128)S(1)}, s32[48]{0:T(128)S(1)}, u32[]{:S(2)}, u32[]{:S(2)}) collective-permute-start(s32[48]{0:T(128)S(1)} %get-tuple-element.24), channel_id=1, source_target_pairs={{0,32},{32,64},{64,96},{96,0},{1,33},{33,65},{65,97},{97,1},{2,34}... | collective-permute-start | bytes 584 | tf_op jit(solution)/shard_map/ppermute | solution.py:73
  37.1 9.1 %collective-permute-start.12 = (s32[48]{0:T(128)S(1)}, s32[48]{0:T(128)S(1)}, u32[]{:S(2)}, u32[]{:S(2)}) collective-permute-start(s32[48]{0:T(128)S(1)} %get-tuple-element.22), channel_id=1, source_target_pairs={{0,96},{32,0},{64,32},{96,64},{1,97},{33,1},{65,33},{97,65},{2,98}... | collective-permute-start | bytes 584 | tf_op jit(solution)/shard_map/ppermute | solution.py:74
  41.0 4.8 %collective-permute-start.11 = (s32[24]{0:T(128)S(1)}, s32[24]{0:T(128)S(1)}, u32[]{:S(2)}, u32[]{:S(2)}) collective-permute-start(s32[24]{0:T(128)S(1)} %collective-permute-done.10), channel_id=1, source_target_pairs={{0,96},{32,0},{64,32},{96,64},{1,97},{33,1},{65,33},{97,65},{2,98}... | collective-permute-start | bytes 296 | tf_op jit(solution)/shard_map/ppermute | solution.py:78
  42.5 3.6 %collective-permute-start.9 = (s32[24]{0:T(128)S(1)}, s32[24]{0:T(128)S(1)}, u32[]{:S(2)}, u32[]{:S(2)}) collective-permute-start(s32[24]{0:T(128)S(1)} %collective-permute-done.8), channel_id=1, source_target_pairs={{0,32},{32,64},{64,96},{96,0},{1,33},{33,65},{65,97},{97,1},{2,34}... | collective-permute-start | bytes 296 | tf_op jit(solution)/shard_map/ppermute | solution.py:77
  42.5 135.8 %collective-permute-start.6 = (bf16[192,4096]{1,0:T(8,128)(2,1)S(1)}, bf16[192,4096]{1,0:T(8,128)(2,1)S(1)}, u32[]{:S(2)}, u32[]{:S(2)}) collective-permute-start(bf16[192,4096]{1,0:T(8,128)(2,1)S(1)} %bitcast.34), channel_id=1, source_target_pairs={{0,1},{1,0},{2,3},{3,2},{4,5},{5,4},{6,7},{7,6},{8,9},{9,8},{10,11... | collective-permute-start | bytes 4718600 | tf_op jit(solution)/shard_map/ppermute | solution.py:118
  215.4 3.1 %collective-permute-start.13 = (f32[96,3072]{1,0:T(8,128)}, f32[96,3072]{1,0:T(8,128)S(1)}, u32[]{:S(2)}, u32[]{:S(2)}) collective-permute-start(f32[96,3072]{1,0:T(8,128)} %get-tuple-element.10), channel_id=1, source_target_pairs={{0,1},{1,0},{2,3},{3,2},{4,5},{5,4},{6,7},{7,6},{8,9},{9,8},{10,11... | collective-permute-start | bytes 3538952 | tf_op jit(solution)/shard_map/ppermute | solution.py:131
  215.8 4.5 %collective-permute-start.14 = (f32[96,3072]{1,0:T(8,128)}, f32[96,3072]{1,0:T(8,128)S(1)}, u32[]{:S(2)}, u32[]{:S(2)}) collective-permute-start(f32[96,3072]{1,0:T(8,128)} %get-tuple-element.11), channel_id=1, source_target_pairs={{0,1},{1,0},{2,3},{3,2},{4,5},{5,4},{6,7},{7,6},{8,9},{9,8},{10,11... | collective-permute-start | bytes 3538952 | tf_op jit(solution)/shard_map/ppermute | solution.py:131
  216.0 5.3 %collective-permute-start.15 = (f32[4,4096]{1,0:T(4,128)}, f32[4,4096]{1,0:T(4,128)S(1)}, u32[]{:S(2)}, u32[]{:S(2)}) collective-permute-start(f32[4,4096]{1,0:T(4,128)} %get-tuple-element.12), channel_id=1, source_target_pairs={{0,1},{1,0},{2,3},{3,2},{4,5},{5,4},{6,7},{7,6},{8,9},{9,8},{10,11... | collective-permute-start | bytes 196616 | tf_op jit(solution)/shard_map/ppermute | solution.py:134
  219.7 1.7 copy-start.2
Sparse Core Ops, SparseCore 0:
  34.2 162.3 all-gather.1

commit v16 on v15

--- a/solution.py
+++ b/solution.py
@@ -32,7 +32,7 @@
     c_theirs_ref[...] += sums[heads:]
 
 
-def gram_consensus(half, pair_rows, one_hot, gathered, pieces=2, block_rows=512):
+def gram_consensus(half, pair_rows, one_hot, gathered, pieces=3, block_rows=1024):
     rows = pair_rows.shape[0] // 2
     bins = pair_rows.shape[1]
     total = gathered.shape[0]

time: 229 us -> 229 us (level)
  transfers between devices with their start and end apart: 17 -> 18, of which waited for: 6 -> 7; matrix products, arithmetic and copies ran while one was open for 3% -> 3% of each run, Pallas kernels for 0% -> 0%
where the time goes in v16:
time: 229 us
  blocking collectives  131 us (57%)
  waiting for transfers between devices  30 us (13%)
  starting transfers between devices  20.1 us (9%)
  Pallas kernels  18.9 us (8%)
  between operations  14.9 us (7%)
  other arithmetic  7.53 us (3%)
  local copies, waits for them, and re-layouts  6.36 us (3%)
    unnamed x1, blocking collectives  131 us
    pallas_call x1, Pallas kernels, gram_consensus(): pl.pallas_call(functools.partial(_gram_consensus_kernel, 1.0 / bins, rows...  18.9 us
    all_gather x1, waiting for transfers between devices, shards(): gathered = lax.all_gather(arrived, 'tile', axis=0, tiled=True)  16.4 us
    ppermute x4, waiting for transfers between devices, exchange_over_mass(): first = lax.ppermute(lax.ppermute(far[:half], 'mass', ahead), 'mass', ahead)  11.6 us
    ppermute x2, starting transfers between devices, exchange_over_mass(): from_ahead = lax.ppermute(pieces[(me - 1) % mass_count], 'mass', behind)  5.17 us
  transfers between devices with their start and end apart: 18, of which 7 were waited for; matrix products, arithmetic and copies ran while one was open for 3% of the time, Pallas kernels for 0%

profile of v16, /device:TPU:1, one launch (start us, length us, event | category | flops | bytes accessed | tf_op | source)
XLA Modules:
  0.0 228.9 jit_solution(17808624650956419379)
XLA Ops:
  7.2 0.8 fusion.5
  8.2 0.8 select_reduce_fusion.1
  9.0 1.4 fusion
  10.4 0.7 multiply_add_fusion
  11.1 0.6 convolution_convert_fusion
  11.8 2.1 collective-permute-start.1
  13.9 1.3 collective-permute-start.3
  15.5 2.6 %collective-permute-start.5 = (bf16[48,4096]{1,0:T(8,128)(2,1)S(1)}, bf16[48,4096]{1,0:T(8,128)(2,1)S(1)}, u32[]{:S(2)}, u32[]{:S(2)}) collective-permute-start(bf16[48,4096]{1,0:T(8,128)(2,1)S(1)} %get-tuple-element.19), channel_id=1, source_target_pairs={{0,96},{32,0},{64,32},{96,64},{1,97},{33,1},{65,33},{97,65},{2,98}... | collective-permute-start | bytes 1179656 | tf_op jit(solution)/shard_map/ppermute | solution.py:74
  18.1 1.3 collective-permute-done.1
  19.4 0.3 collective-permute-start.2
  19.7 2.4 %collective-permute-start.4 = (bf16[24,4096]{1,0:T(8,128)(2,1)S(1)}, bf16[24,4096]{1,0:T(8,128)(2,1)S(1)}, u32[]{:S(2)}, u32[]{:S(2)}) collective-permute-start(bf16[24,4096]{1,0:T(8,128)(2,1)S(1)} %collective-permute-done.3), channel_id=1, source_target_pairs={{0,96},{32,0},{64,32},{96,64},{1,97},{33,1},{65,33},{97,65},{2,98}... | collective-permute-start | bytes 589832 | tf_op jit(solution)/shard_map/ppermute | solution.py:78
  22.1 9.9 %collective-permute-done.2 = bf16[24,4096]{1,0:T(8,128)(2,1)S(1)} collective-permute-done((bf16[24,4096]{1,0:T(8,128)(2,1)S(1)}, bf16[24,4096]{1,0:T(8,128)(2,1)S(1)}, u32[]{:S(2)}, u32[]{:S(2)}) %collective-permute-start.2) | collective-permute-done | bytes 196640 | tf_op jit(solution)/shard_map/ppermute | solution.py:77
  32.3 1.8 gather_fusion
  34.4 2.6 %collective-permute-start.10 = (s32[24]{0:T(128)S(1)}, s32[24]{0:T(128)S(1)}, u32[]{:S(2)}, u32[]{:S(2)}) collective-permute-start(s32[24]{0:T(128)S(1)} %get-tuple-element.28), channel_id=1, source_target_pairs={{0,96},{32,0},{64,32},{96,64},{1,97},{33,1},{65,33},{97,65},{2,98}... | collective-permute-start | bytes 296 | tf_op jit(solution)/shard_map/ppermute | solution.py:78
  37.1 2.6 %collective-permute-start.12 = (s32[48]{0:T(128)S(1)}, s32[48]{0:T(128)S(1)}, u32[]{:S(2)}, u32[]{:S(2)}) collective-permute-start(s32[48]{0:T(128)S(1)} %get-tuple-element.24), channel_id=1, source_target_pairs={{0,96},{32,0},{64,32},{96,64},{1,97},{33,1},{65,33},{97,65},{2,98}... | collective-permute-start | bytes 584 | tf_op jit(solution)/shard_map/ppermute | solution.py:74
  39.7 0.6 dynamic-slice
  41.0 1.5 collective-permute-start.11
  42.5 3.2 %collective-permute-start.6 = (bf16[192,4096]{1,0:T(8,128)(2,1)S(1)}, bf16[192,4096]{1,0:T(8,128)(2,1)S(1)}, u32[]{:S(2)}, u32[]{:S(2)}) collective-permute-start(bf16[192,4096]{1,0:T(8,128)(2,1)S(1)} %bitcast.34), channel_id=1, source_target_pairs={{0,1},{1,0},{2,3},{3,2},{4,5},{5,4},{6,7},{7,6},{8,9},{9,8},{10,11... | collective-permute-start | bytes 4718600 | tf_op jit(solution)/shard_map/ppermute | solution.py:118
  45.8 0.4 collective-permute-done.9
  46.2 0.6 gather_fusion.1
  47.1 130.5 %all-reduce = s32[6144]{0:T(1024)S(1)} all-reduce(s32[6144]{0:T(1024)S(1)} %dynamic-update-slice), channel_id=1, replica_groups=mesh['mass'=4,'tile'=32] {'tile'}, use_global_device_ids=true, to_apply=%add | all-reduce | flops 6144 | bytes 49152
  177.7 0.7 compare_convert_fusion.oh_ref
  178.4 1.9 pad_maximum_fusion.a_ref
  180.2 16.4 %all-gather.2.cloned.1.call-done.p_ref = bf16[6144,4096]{1,0:T(8,128)(2,1)} async-done(((bf16[192,4096]{1,0:T(8,128)(2,1)}), bf16[6144,4096]{1,0:T(8,128)(2,1)}) %all-gather.2.cloned.1.call-update) | async-done | bytes 50331664 | tf_op jit(solution)/shard_map/all_gather | solution.py:113
  196.7 18.9 %shard_map.50 = (f32[192,6144]{1,0:T(8,128)}, f32[64,3072]{1,0:T(8,128)}, f32[64,3072]{1,0:T(8,128)}, f32[64,3072]{1,0:T(8,128)}, f32[4,4096]{1,0:T(4,128)}, /*index=5*/f32[4,4096]{1,0:T(4,128)}) custom-call(s32[1]{0:T(128)} %bitcast.half_ref, bf16[384,4096]{1,0:T(8,128)(2,1)} %pad_maximum_fusion.a_ref, bf16[8,6144]{1,0:T(8,128)(2,1)} %compare_convert_fusion.oh_ref, ...), custom_call_target="tpu_custom_call" | custom-call | flops 9865003008 | bytes 33210368 | tf_op jit(solution)/shard_map/pallas_call | solution.py:58
  215.6 0.3 collective-permute-start.13
  216.2 0.3 collective-permute-start.15
  216.7 1.5 collective-permute-done.13
  218.2 0.9 constant_dynamic-update-slice_fusion
  219.3 0.9 constant_dynamic-update-slice_fusion.1
  220.4 0.9 constant_dynamic-update-slice_fusion.2
  221.4 0.6 add.144
  (47 shorter events, 2.5 us)
Async XLA Ops:
  7.2 4.0 %copy-start.1 = (bf16[96,4096]{1,0:T(8,128)(2,1)S(1)}, bf16[96,4096]{1,0:T(8,128)(2,1)}, u32[]{:S(2)}) copy-start(bf16[96,4096]{1,0:T(8,128)(2,1)} %param.3) | copy-start | bytes 2359300
  7.2 189.5 %all-gather.2.cloned.1.call-start = ((), (), s32[]{:S(2)}) async-start(), calls=%async_computation | async-start | bytes 51904512 | tf_op jit(solution)/shard_map/all_gather | solution.py:113
  11.8 7.6 %collective-permute-start.1 = (bf16[24,4096]{1,0:T(8,128)(2,1)S(1)}, bf16[24,4096]{1,0:T(8,128)(2,1)S(1)}, u32[]{:S(2)}, u32[]{:S(2)}) collective-permute-start(bf16[24,4096]{1,0:T(8,128)(2,1)S(1)} %get-tuple-element.21), channel_id=1, source_target_pairs={{0,32},{32,64},{64,96},{96,0},{1,33},{33,65},{65,97},{97,1},{2,34}... | collective-permute-start | bytes 589832 | tf_op jit(solution)/shard_map/ppermute | solution.py:77
  13.9 5.8 %collective-permute-start.3 = (bf16[24,4096]{1,0:T(8,128)(2,1)S(1)}, bf16[24,4096]{1,0:T(8,128)(2,1)S(1)}, u32[]{:S(2)}, u32[]{:S(2)}) collective-permute-start(bf16[24,4096]{1,0:T(8,128)(2,1)S(1)} %get-tuple-element.22), channel_id=1, source_target_pairs={{0,96},{32,0},{64,32},{96,64},{1,97},{33,1},{65,33},{97,65},{2,98}... | collective-permute-start | bytes 589832 | tf_op jit(solution)/shard_map/ppermute | solution.py:78
  15.3 16.8 %collective-permute-start = (bf16[48,4096]{1,0:T(8,128)(2,1)S(1)}, bf16[48,4096]{1,0:T(8,128)(2,1)S(1)}, u32[]{:S(2)}, u32[]{:S(2)}) collective-permute-start(bf16[48,4096]{1,0:T(8,128)(2,1)S(1)} %get-tuple-element.20), channel_id=1, source_target_pairs={{0,32},{32,64},{64,96},{96,0},{1,33},{33,65},{65,97},{97,1},{2,34}... | collective-permute-start | bytes 1179656 | tf_op jit(solution)/shard_map/ppermute | solution.py:73
  15.5 16.6 %collective-permute-start.5 = (bf16[48,4096]{1,0:T(8,128)(2,1)S(1)}, bf16[48,4096]{1,0:T(8,128)(2,1)S(1)}, u32[]{:S(2)}, u32[]{:S(2)}) collective-permute-start(bf16[48,4096]{1,0:T(8,128)(2,1)S(1)} %get-tuple-element.19), channel_id=1, source_target_pairs={{0,96},{32,0},{64,32},{96,64},{1,97},{33,1},{65,33},{97,65},{2,98}... | collective-permute-start | bytes 1179656 | tf_op jit(solution)/shard_map/ppermute | solution.py:74
  19.4 12.6 %collective-permute-start.2 = (bf16[24,4096]{1,0:T(8,128)(2,1)S(1)}, bf16[24,4096]{1,0:T(8,128)(2,1)S(1)}, u32[]{:S(2)}, u32[]{:S(2)}) collective-permute-start(bf16[24,4096]{1,0:T(8,128)(2,1)S(1)} %collective-permute-done.1), channel_id=1, source_target_pairs={{0,32},{32,64},{64,96},{96,0},{1,33},{33,65},{65,97},{97,1},{2,34}... | collective-permute-start | bytes 589832 | tf_op jit(solution)/shard_map/ppermute | solution.py:77
  19.7 12.4 %collective-permute-start.4 = (bf16[24,4096]{1,0:T(8,128)(2,1)S(1)}, bf16[24,4096]{1,0:T(8,128)(2,1)S(1)}, u32[]{:S(2)}, u32[]{:S(2)}) collective-permute-start(bf16[24,4096]{1,0:T(8,128)(2,1)S(1)} %collective-permute-done.3), channel_id=1, source_target_pairs={{0,96},{32,0},{64,32},{96,64},{1,97},{33,1},{65,33},{97,65},{2,98}... | collective-permute-start | bytes 589832 | tf_op jit(solution)/shard_map/ppermute | solution.py:78
  34.1 5.6 %copy-start.3 = (u32[128]{0:T(128)S(1)}, u32[128]{0:T(128)}, u32[]{:S(2)}) copy-start(u32[128]{0:T(128)} %constant.103) | copy-start | bytes 1540
  34.1 8.4 %copy-start = (bf16[4,48,4096]{2,1,0:T(8,128)(2,1)S(1)}, bf16[4,48,4096]{2,1,0:T(8,128)(2,1)}, u32[]{:S(2)}) copy-start(bf16[4,48,4096]{2,1,0:T(8,128)(2,1)} %gather_fusion) | copy-start | bytes 4718596
  34.4 6.6 %collective-permute-start.10 = (s32[24]{0:T(128)S(1)}, s32[24]{0:T(128)S(1)}, u32[]{:S(2)}, u32[]{:S(2)}) collective-permute-start(s32[24]{0:T(128)S(1)} %get-tuple-element.28), channel_id=1, source_target_pairs={{0,96},{32,0},{64,32},{96,64},{1,97},{33,1},{65,33},{97,65},{2,98}... | collective-permute-start | bytes 296 | tf_op jit(solution)/shard_map/ppermute | solution.py:78
  37.0 5.5 %collective-permute-start.8 = (s32[24]{0:T(128)S(1)}, s32[24]{0:T(128)S(1)}, u32[]{:S(2)}, u32[]{:S(2)}) collective-permute-start(s32[24]{0:T(128)S(1)} %get-tuple-element.27), channel_id=1, source_target_pairs={{0,32},{32,64},{64,96},{96,0},{1,33},{33,65},{65,97},{97,1},{2,34}... | collective-permute-start | bytes 296 | tf_op jit(solution)/shard_map/ppermute | solution.py:77
  37.0 9.2 %collective-permute-start.7 = (s32[48]{0:T(128)S(1)}, s32[48]{0:T(128)S(1)}, u32[]{:S(2)}, u32[]{:S(2)}) collective-permute-start(s32[48]{0:T(128)S(1)} %get-tuple-element.26), channel_id=1, source_target_pairs={{0,32},{32,64},{64,96},{96,0},{1,33},{33,65},{65,97},{97,1},{2,34}... | collective-permute-start | bytes 584 | tf_op jit(solution)/shard_map/ppermute | solution.py:73
  37.1 9.1 %collective-permute-start.12 = (s32[48]{0:T(128)S(1)}, s32[48]{0:T(128)S(1)}, u32[]{:S(2)}, u32[]{:S(2)}) collective-permute-start(s32[48]{0:T(128)S(1)} %get-tuple-element.24), channel_id=1, source_target_pairs={{0,96},{32,0},{64,32},{96,64},{1,97},{33,1},{65,33},{97,65},{2,98}... | collective-permute-start | bytes 584 | tf_op jit(solution)/shard_map/ppermute | solution.py:74
  41.0 4.8 %collective-permute-start.11 = (s32[24]{0:T(128)S(1)}, s32[24]{0:T(128)S(1)}, u32[]{:S(2)}, u32[]{:S(2)}) collective-permute-start(s32[24]{0:T(128)S(1)} %collective-permute-done.10), channel_id=1, source_target_pairs={{0,96},{32,0},{64,32},{96,64},{1,97},{33,1},{65,33},{97,65},{2,98}... | collective-permute-start | bytes 296 | tf_op jit(solution)/shard_map/ppermute | solution.py:78
  42.5 3.6 %collective-permute-start.9 = (s32[24]{0:T(128)S(1)}, s32[24]{0:T(128)S(1)}, u32[]{:S(2)}, u32[]{:S(2)}) collective-permute-start(s32[24]{0:T(128)S(1)} %collective-permute-done.8), channel_id=1, source_target_pairs={{0,32},{32,64},{64,96},{96,0},{1,33},{33,65},{65,97},{97,1},{2,34}... | collective-permute-start | bytes 296 | tf_op jit(solution)/shard_map/ppermute | solution.py:77
  42.5 135.8 %collective-permute-start.6 = (bf16[192,4096]{1,0:T(8,128)(2,1)S(1)}, bf16[192,4096]{1,0:T(8,128)(2,1)S(1)}, u32[]{:S(2)}, u32[]{:S(2)}) collective-permute-start(bf16[192,4096]{1,0:T(8,128)(2,1)S(1)} %bitcast.34), channel_id=1, source_target_pairs={{0,1},{1,0},{2,3},{3,2},{4,5},{5,4},{6,7},{7,6},{8,9},{9,8},{10,11... | collective-permute-start | bytes 4718600 | tf_op jit(solution)/shard_map/ppermute | solution.py:118
  215.6 2.6 %collective-permute-start.13 = (f32[64,3072]{1,0:T(8,128)}, f32[64,3072]{1,0:T(8,128)S(1)}, u32[]{:S(2)}, u32[]{:S(2)}) collective-permute-start(f32[64,3072]{1,0:T(8,128)} %get-tuple-element.11), channel_id=1, source_target_pairs={{0,1},{1,0},{2,3},{3,2},{4,5},{5,4},{6,7},{7,6},{8,9},{9,8},{10,11... | collective-permute-start | bytes 2359304 | tf_op jit(solution)/shard_map/ppermute | solution.py:131
  216.0 3.4 %collective-permute-start.14 = (f32[64,3072]{1,0:T(8,128)}, f32[64,3072]{1,0:T(8,128)S(1)}, u32[]{:S(2)}, u32[]{:S(2)}) collective-permute-start(f32[64,3072]{1,0:T(8,128)} %get-tuple-element.12), channel_id=1, source_target_pairs={{0,1},{1,0},{2,3},{3,2},{4,5},{5,4},{6,7},{7,6},{8,9},{9,8},{10,11... | collective-permute-start | bytes 2359304 | tf_op jit(solution)/shard_map/ppermute | solution.py:131
  216.2 4.2 %collective-permute-start.15 = (f32[64,3072]{1,0:T(8,128)}, f32[64,3072]{1,0:T(8,128)S(1)}, u32[]{:S(2)}, u32[]{:S(2)}) collective-permute-start(f32[64,3072]{1,0:T(8,128)} %get-tuple-element.13), channel_id=1, source_target_pairs={{0,1},{1,0},{2,3},{3,2},{4,5},{5,4},{6,7},{7,6},{8,9},{9,8},{10,11... | collective-permute-start | bytes 2359304 | tf_op jit(solution)/shard_map/ppermute | solution.py:131
  216.5 4.9 %collective-permute-start.16 = (f32[4,4096]{1,0:T(4,128)}, f32[4,4096]{1,0:T(4,128)S(1)}, u32[]{:S(2)}, u32[]{:S(2)}) collective-permute-start(f32[4,4096]{1,0:T(4,128)} %get-tuple-element.14), channel_id=1, source_target_pairs={{0,1},{1,0},{2,3},{3,2},{4,5},{5,4},{6,7},{7,6},{8,9},{9,8},{10,11... | collective-permute-start | bytes 196616 | tf_op jit(solution)/shard_map/ppermute | solution.py:134
  219.1 2.3 copy-start.2
Sparse Core Ops, SparseCore 0:
  34.2 162.3 all-gather.1
